TPU v7x, 32 devices: a whole 2x2x4 slice. The times are simulated.
32 devices in a mesh: groups: 2 (over x), cell: 16 (over z, y, core).
Axes of the slice: x: 2, y: 2, z: 4, core: 2. Of those that a mesh axis runs over, the one named last changes fastest.
Arguments:
- cells: bfloat16 [256, 64, 768], P(('groups', 'cell')), parts along dimension 0, may hold values from -6 to 6
- cotangent: bfloat16 [256, 64, 768], P('groups', 'cell'), parts along dimension 0, may hold values from -6 to 6
- row_weight: bfloat16 [768, 3072], replicated, may hold values from -0.21875 to 0.21875
- col_weight: bfloat16 [768, 3072], replicated, may hold values from -0.21875 to 0.21875
Outputs:
- grad_cells: bfloat16 [256, 64, 768], P(('groups', 'cell')), parts along dimension 0
- row_grad: float32 [1536, 3072], P(('groups', 'cell')), parts along dimension 0
- col_grad: float32 [1536, 3072], P(('groups', 'cell')), parts along dimension 0
There are 2 independent parts, one for each index of `groups`. A program takes and returns all parts, laid end to end along the dimension named above; an argument that names none is the same for every part. Nothing has to cross between parts.
All inputs are finite; a program needn't handle non-finite values.
Results may differ from a plain program's by a relative error of at most 0.012.
Values may be sent and summed in bfloat16 or wider, within the bound.
No kernel may reach another device: no remote copies, remote signals or barrier semaphores. Data moves between devices by JAX's collectives and lax.ppermute only.
A program may use at most 128 MiB of HBM per device.

v0:
```python
import jax
import jax.numpy as jnp
from jax import lax
from jax.sharding import PartitionSpec as P

HEADS = 12


EPS = 1e-06


def normalize(values):
    return values * lax.rsqrt(jnp.mean(values * values, axis=-1, keepdims=True) + EPS)


def attend_heads(queries, keys_part, values_part):
    head_size = queries.shape[-1]
    scores = jnp.einsum(
        "bhle,bhme->bhlm", queries, keys_part, preferred_element_type=jnp.float32
    ) * head_size ** (-0.5)
    weights = jax.nn.softmax(scores, axis=-1).astype(jnp.bfloat16)
    mixture = jnp.einsum("bhlm,bhme->bhle", weights, values_part, preferred_element_type=jnp.float32)
    return mixture.astype(jnp.bfloat16)


def forms_of(attn_dim):
    return "bld" if attn_dim == 1 else "lbd", "blf" if attn_dim == 1 else "lbf"


def split_weight(weight):
    model_width = weight.shape[0]
    head_size = model_width // HEADS
    projection = weight[:, : 3 * model_width].reshape(model_width, 3, HEADS, head_size)
    output = weight[:, 3 * model_width :].reshape(HEADS, head_size, model_width)
    return projection, output


def forward(cells_in, weight, attn_dim, with_result):
    cell_form, out_form = forms_of(attn_dim)
    projection, output = split_weight(weight)
    inputs_f = cells_in.astype(jnp.float32)
    normed = normalize(inputs_f).astype(jnp.bfloat16)
    projected = jnp.einsum(
        cell_form + ",dthe->tbhle", normed, projection, preferred_element_type=jnp.float32
    ).astype(jnp.bfloat16)
    attended = attend_heads(projected[0], projected[1], projected[2])
    result = None
    if with_result:
        result = (
            inputs_f
            + jnp.einsum("bhle,hef->" + out_form, attended, output, preferred_element_type=jnp.float32)
        ).astype(jnp.bfloat16)
    return (inputs_f, normed, projected, attended, result)


def backward(saved, weight, upstream, attn_dim):
    inputs_f, normed, projected, attended, result = saved
    cell_form, out_form = forms_of(attn_dim)
    projection, output = split_weight(weight)
    grad_attended = jnp.einsum(
        out_form + ",hef->bhle", upstream, output, preferred_element_type=jnp.float32
    ).astype(jnp.bfloat16)
    unused, pull = jax.vjp(attend_heads, projected[0], projected[1], projected[2])
    grad_projected = jnp.stack(pull(grad_attended)).astype(jnp.bfloat16)
    grad_normed = jnp.einsum(
        "tbhle,dthe->" + cell_form, grad_projected, projection, preferred_element_type=jnp.float32
    )
    unused_norm, pull_norm = jax.vjp(normalize, inputs_f)
    grad_input = (upstream.astype(jnp.float32) + pull_norm(grad_normed)[0]).astype(jnp.bfloat16)
    return (grad_input, grad_projected)


def weight_term(normed, grad_projected, attended, upstream, attn_dim):
    cell_form, out_form = forms_of(attn_dim)
    model_width = normed.shape[-1]
    first = jnp.einsum(
        cell_form + ",tbhle->dthe", normed, grad_projected, preferred_element_type=jnp.float32
    ).reshape(model_width, 3 * model_width)
    second = jnp.einsum(
        "bhle," + out_form + "->hef", attended, upstream, preferred_element_type=jnp.float32
    ).reshape(model_width, model_width)
    return jnp.concatenate([first, second], axis=1)


def body(cells, cotangent, row_weight, col_weight):
    row_saved = forward(cells, row_weight, 1, True)
    mid_columns = lax.all_to_all(row_saved[4], "cell", split_axis=1, concat_axis=0, tiled=True)
    col_saved = forward(mid_columns, col_weight, 0, False)
    grad_mid_columns, grad_col_proj = backward(col_saved, col_weight, cotangent, 0)
    col_term = weight_term(col_saved[1], grad_col_proj, col_saved[3], cotangent, 0)
    col_grad = lax.psum_scatter(
        col_term.astype(jnp.bfloat16), "cell", scatter_dimension=0, tiled=True
    ).astype(jnp.float32)
    grad_mid = lax.all_to_all(grad_mid_columns, "cell", split_axis=0, concat_axis=1, tiled=True)
    grad_cells, grad_row_proj = backward(row_saved, row_weight, grad_mid, 1)
    row_term = weight_term(row_saved[1], grad_row_proj, row_saved[3], grad_mid, 1)
    row_grad = lax.psum_scatter(
        row_term.astype(jnp.bfloat16), "cell", scatter_dimension=0, tiled=True
    ).astype(jnp.float32)
    return (grad_cells, row_grad, col_grad)


def solution(mesh):
    placed = (P(("groups", "cell"), None, None), P("groups", "cell", None), P(), P())
    return jax.shard_map(
        body,
        mesh=mesh,
        in_specs=placed,
        out_specs=(
            P(("groups", "cell"), None, None),
            P(("groups", "cell"), None),
            P(("groups", "cell"), None),
        ),
        check_vma=False,
    )
```

profile of v0, /device:TPU:0, one launch (start us, length us, event | category | flops | bytes accessed | tf_op | source)
XLA Modules:
  0.0 270.4 jit_solution(11330183502335654397)
XLA Ops:
  7.2 2.4 slice.44
  11.8 3.6 %copy.139 = bf16[768,2304]{0,1:T(8,128)(2,1)} copy(bf16[768,2304]{1,0:T(8,128)(2,1)S(1)} %slice-done) | data formatting | bytes 7077888 | tf_op jit(solution)/shard_map/slice | solution.py:33
  15.4 5.8 %convert_bitcast_fusion = bf16[3,8,12,64,64]{4,3,2,0,1:T(8,128)(2,1)S(1)} fusion(bf16[768,3,12,64,1]{0,3,2,1,4:T(8,128)(2,1)} %bitcast.196, bf16[8,64,768]{2,1,0:T(8,128)(2,1)} %param.4, f32[8,64]{1,0:T(8,128)S(1)} %fusion.70), kind=kOutput, calls=%fused_computation.7 | convolution fusion | flops 1814298624 | bytes 6686720 | tf_op jit(solution)/shard_map/bld,dthe->tbhle/dot_general | solution.py:43
  22.2 4.7 %fusion.82 = (f32[8,12,64]{2,1,0:T(8,128)S(1)}, f32[8,12,64,64]{2,3,1,0:T(8,128)S(1)}) fusion(f32[8,12,64,64]{2,3,1,0:T(8,128)S(1)} %fusion.43), kind=kOutput, calls=%fused_computation.123 | output fusion | flops 1572927 | bytes 3170304 | tf_op jit(solution)/shard_map/sub | solution.py:21
  28.6 1.2 copy-done.18
  30.7 1.3 copy.141
  32.0 7.4 %all-to-all-start = ((bf16[8,64,768]{2,0,1:T(8,128)(2,1)}), bf16[8,64,768]{2,0,1:T(8,128)(2,1)}, u32[]{:S(2)}, u32[]{:S(2)}) async-start(bf16[8,64,768]{2,0,1:T(8,128)(2,1)} %copy.141), calls=%async_computation | async-start | bytes 1572864 | tf_op jit(solution)/shard_map/all_to_all | solution.py:87
  39.5 2.5 slice.39
  41.9 2.0 slice-done.1
  43.9 3.6 %copy.146 = bf16[768,2304]{0,1:T(8,128)(2,1)} copy(bf16[768,2304]{1,0:T(8,128)(2,1)S(1)} %slice-done.1) | data formatting | bytes 7077888 | tf_op jit(solution)/shard_map/slice | solution.py:33
  47.5 3.3 %fusion.47 = bf16[4,12,128,64]{2,3,0,1:T(8,128)(2,1)} fusion(bf16[12,64,768,1]{2,1,3,0:T(8,128)(2,1)} %bitcast.207, bf16[128,4,768]{2,1,0:T(4,128)(2,1)} %param.5), kind=kOutput, calls=%fused_computation.86 | convolution fusion | flops 604372992 | bytes 2752512 | tf_op jit(solution)/shard_map/lbf,hef->bhle/dot_general | solution.py:60
  50.9 7.3 %all-to-all-done = bf16[8,64,768]{2,0,1:T(8,128)(2,1)} async-done(((bf16[8,64,768]{2,0,1:T(8,128)(2,1)}), bf16[8,64,768]{2,0,1:T(8,128)(2,1)}, u32[]{:S(2)}, u32[]{:S(2)}) %all-to-all-start) | async-done | bytes 786464 | tf_op jit(solution)/shard_map/all_to_all | solution.py:87
  58.2 2.0 multiply_reduce_fusion.2
  60.2 1.4 copy.143
  61.6 1.3 multiply_add_fusion
  62.9 1.4 copy.144
  64.3 3.6 %convert_bitcast_fusion.1 = bf16[3,4,12,128,64]{3,4,2,0,1:T(8,128)(2,1)S(1)} fusion(bf16[768,3,12,64,1]{0,3,2,1,4:T(8,128)(2,1)S(1)} %bitcast.198, f32[16,8,4]{1,2,0:T(4,128)} %copy.144, bf16[8,64,768]{2,0,1:T(8,128)(2,1)} %all-to-all-done), kind=kOutput, calls=%fused_computation.40 | convolution fusion | flops 1814298624 | bytes 6686720 | tf_op jit(solution)/shard_map/lbd,dthe->tbhle/dot_general | solution.py:43
  68.6 3.2 %fusion.83 = (f32[4,12,128]{2,1,0:T(8,128)S(1)}, f32[4,12,128,128]{2,3,1,0:T(8,128)S(1)}) fusion(f32[4,12,128,128]{2,3,1,0:T(8,128)S(1)} %fusion.63), kind=kOutput, calls=%fused_computation.124 | output fusion | flops 3145855 | bytes 6316032 | tf_op jit(solution)/shard_map/jvp()/sub | solution.py:21
  71.9 2.9 %fusion.6 = (f32[4,12,128]{2,1,0:T(8,128)}, bf16[4,12,128,128]{2,3,1,0:T(8,128)(2,1)S(1)}, bf16[4,12,128,128]{2,3,1,0:T(8,128)(2,1)}) fusion(f32[4,12,128,128]{2,3,1,0:T(8,128)S(1)} %get-tuple-element.12, f32[4,12,128]{2,1,0:T(8,128)S(1)} %multiply_divide_fusion.1, f32[4,12,128]{2,1,0:T(8,128)S(1)} %get-tuple-element.11, ...), kind=kOutput, calls=%fused_computation.16 | convolution fusion | flops 106162176 | bytes 7954432 | tf_op jit(solution)/shard_map/transpose(jvp(bhlm,bhme->bhle))/dot_general | solution.py:22
  76.0 2.1 fusion.46
  78.1 4.1 %bitcast_convert_fusion.2 = bf16[12,64,768]{2,1,0:T(8,128)(2,1)} fusion(bf16[4,12,128,128]{2,3,1,0:T(8,128)(2,1)} %copy-done.16, bf16[128,4,768]{2,1,0:T(4,128)(2,1)} %param.5, bf16[3,4,12,128,64]{3,4,2,0,1:T(8,128)(2,1)} %copy-done.20), kind=kOutput, calls=%fused_computation.38 | convolution fusion | flops 705626112 | bytes 4325376 | tf_op jit(solution)/shard_map/bhle,lbf->hef/dot_general | solution.py:79
  82.9 4.8 %fusion.49 = bf16[1,4,12,128,64]{3,4,2,1,0:T(8,128)(2,1)} fusion(bf16[3,4,12,128,64]{3,4,2,0,1:T(8,128)(2,1)} %copy-done.20, f32[4,12,128,128]{2,3,1,0:T(8,128)} %copy-done.5, bf16[4,12,128,128]{2,3,1,0:T(8,128)(2,1)} %get-tuple-element.13, f32[4,12,128]{2,1,0:T(8,128)S(1)} %neg.12, f32[4,12,128]{2,1,0:T(8,128)} %copy-done.29), kind=kOutput, calls=%fused_computation.88 | convolution fusion | flops 104988672 | bytes 6348800 | tf_op jit(solution)/shard_map/transpose(jvp(bhle,bhme->bhlm))/dot_general | solution.py:18
  87.7 2.8 %fusion.48 = bf16[1,4,12,128,64]{3,4,2,1,0:T(8,128)(2,1)} fusion(bf16[3,4,12,128,64]{3,4,2,0,1:T(8,128)(2,1)} %copy-done.20, f32[4,12,128,128]{2,3,1,0:T(8,128)S(1)} %copy-done.6, bf16[4,12,128,128]{2,3,1,0:T(8,128)(2,1)S(1)} %copy-done.36, f32[4,12,128]{2,1,0:T(8,128)S(1)} %neg.12, f32[4,12,128]{2,1,0:T(8,128)S(1)} %copy-done.30), kind=kOutput, calls=%fused_computation.87 | convolution fusion | flops 104988672 | bytes 6340608 | tf_op jit(solution)/shard_map/transpose(jvp(bhle,bhme->bhlm))/dot_general | solution.py:18
  92.0 1.9 fusion.50
  95.5 4.4 %fusion.31 = (f32[128,4]{0,1:T(4,128)S(1)}, f32[4,128,768,1,1]{2,1,3,0,4:T(8,128)}) fusion(bf16[768,3,12,64,1]{0,3,2,4,1:T(8,128)(2,1)S(1)} %bitcast.199, bf16[1,4,12,128,64]{3,4,2,1,0:T(8,128)(2,1)S(1)} %copy-done.7, bf16[1,4,12,128,64]{3,4,2,1,0:T(8,128)(2,1)S(1)} %copy-done.21, bf16[1,4,12,128,64]{3,4,2,1,0:T(8,128)(2,1)S(1)} %copy-done.22, ...), kind=kOutput, calls=%fused_computation.67 | convolution fusion | flops 1815477760 | bytes 8259584 | tf_op jit(solution)/shard_map/tbhle,dthe->lbd/dot_general | solution.py:65
  99.9 3.5 %bitcast_convert_fusion.1 = bf16[768,2304]{1,0:T(8,128)(2,1)S(1)} fusion(bf16[2304,4,128]{2,0,1:T(8,128)(2,1)S(1)} %bitcast.202, f32[128,4]{0,1:T(4,128)S(1)} %get-tuple-element.7, bf16[8,64,768]{2,0,1:T(8,128)(2,1)} %all-to-all-done), kind=kOutput, calls=%fused_computation.3 | convolution fusion | flops 1814888448 | bytes 6686720 | tf_op jit(solution)/shard_map/lbd,tbhle->dthe/dot_general | solution.py:76
  103.4 2.8 %pad_maximum_fusion.2 = bf16[768,3072]{1,0:T(8,128)(2,1)} fusion(bf16[768,768]{1,0:T(8,128)(2,1)S(1)} %bitcast.204, bf16[768,2304]{1,0:T(8,128)(2,1)S(1)} %bitcast_convert_fusion.1), kind=kLoop, calls=%fused_computation.6 | loop fusion | flops 9437184 | bytes 9437184 | tf_op jit(solution)/shard_map/concatenate | solution.py:82
  106.3 1.4 copy-done.15
  107.8 1.5 fusion.20
  109.4 1.5 copy.154
  110.9 5.5 %all-to-all-start.1 = ((bf16[128,4,768]{2,1,0:T(4,128)(2,1)}), bf16[128,4,768]{2,1,0:T(4,128)(2,1)S(1)}, u32[]{:S(2)}, u32[]{:S(2)}) async-start(bf16[128,4,768]{2,1,0:T(4,128)(2,1)} %copy.154), calls=%async_computation.1 | async-start | bytes 1572864 | tf_op jit(solution)/shard_map/all_to_all | solution.py:94
  116.6 2.6 copy.158
  119.3 2.0 dot_general.96
  122.0 13.1 %all-to-all-done.1 = bf16[128,4,768]{2,1,0:T(4,128)(2,1)S(1)} async-done(((bf16[128,4,768]{2,1,0:T(4,128)(2,1)}), bf16[128,4,768]{2,1,0:T(4,128)(2,1)S(1)}, u32[]{:S(2)}, u32[]{:S(2)}) %all-to-all-start.1) | async-done | bytes 786464 | tf_op jit(solution)/shard_map/all_to_all | solution.py:94
  135.7 3.2 %bitcast_convert_fusion.3 = bf16[768,768]{0,1:T(8,128)(2,1)} fusion(bf16[768,8,64]{0,2,1:T(8,128)(2,1)} %dot_general.96, bf16[8,64,768]{2,1,0:T(8,128)(2,1)S(1)} %all_to_all.24), kind=kOutput, calls=%fused_computation.39 | convolution fusion | flops 604569600 | bytes 2752512 | tf_op jit(solution)/shard_map/bhle,blf->hef/dot_general | solution.py:79
  138.9 2.4 copy.160
  141.3 1.4 convolution_convert_fusion
  143.2 2.5 fusion.11
  149.5 4.0 %bitcast_convert_fusion = bf16[768,3,12,64]{0,3,2,1:T(8,128)(2,1)} fusion(bf16[1,8,12,64,64]{4,3,2,1,0:T(8,128)(2,1)S(1)} %fusion.37, bf16[1,8,12,64,64]{4,3,2,1,0:T(8,128)(2,1)S(1)} %fusion.36, bf16[1,8,12,64,64]{4,3,2,1,0:T(8,128)(2,1)S(1)} %fusion.35, bf16[8,64,768]{2,1,0:T(8,128)(2,1)S(1)} %copy-done.10, f32[8,64]{1,0:T(8,128)S(1)} %copy-done.34), kind=kOutput, calls=%fused_computation.2 | convolution fusion | flops 1821966336 | bytes 6686720 | tf_op jit(solution)/shard_map/bld,tbhle->dthe/dot_general | solution.py:76
  153.5 4.6 %copy.159 = bf16[768,2304]{1,0:T(8,128)(2,1)S(1)} copy(bf16[768,2304]{0,1:T(8,128)(2,1)} %bitcast.200) | data formatting | bytes 7077888 | tf_op jit(solution)/shard_map/reshape | solution.py:78
  158.1 4.0 %pad_maximum_fusion.1 = bf16[768,3072]{1,0:T(8,128)(2,1)} fusion(bf16[768,768]{1,0:T(8,128)(2,1)} %copy.160, bf16[768,2304]{1,0:T(8,128)(2,1)S(1)} %copy.159), kind=kLoop, calls=%fused_computation.5 | loop fusion | flops 9437184 | bytes 9437184 | tf_op jit(solution)/shard_map/concatenate | solution.py:82
  162.1 2.0 copy-done.3
  164.2 5.9 %fusion.26 = (f32[8,64]{1,0:T(8,128)S(1)}, f32[8,64,768,1,1]{2,1,3,0,4:T(8,128)S(1)}) fusion(bf16[8,64,768]{2,1,0:T(8,128)(2,1)} %param.4, bf16[768,3,12,64,1]{0,3,2,4,1:T(8,128)(2,1)S(1)} %bitcast.197, bf16[1,8,12,64,64]{4,3,2,1,0:T(8,128)(2,1)} %copy-done.35, bf16[1,8,12,64,64]{4,3,2,1,0:T(8,128)(2,1)} %copy-done.38, ...), kind=kOutput, calls=%fused_computation.56 | convolution fusion | flops 1815477760 | bytes 8259584 | tf_op jit(solution)/shard_map/tbhle,dthe->bld/dot_general | solution.py:65
  170.2 1.3 fusion.22
  171.5 11.3 %reduce-scatter.5.cloned.1.call-done = bf16[48,3072]{1,0:T(8,128)(2,1)} async-done(((bf16[768,3072]{1,0:T(8,128)(2,1)}), bf16[48,3072]{1,0:T(8,128)(2,1)}) %reduce-scatter.5.cloned.1.call-update) | async-done | bytes 294928 | tf_op jit(solution)/shard_map/reduce_scatter | solution.py:91
  182.8 1.8 convert_element_type.168
  184.6 77.2 %reduce-scatter.3.cloned.1.call-done = bf16[48,3072]{1,0:T(8,128)(2,1)} async-done(((bf16[768,3072]{1,0:T(8,128)(2,1)}), bf16[48,3072]{1,0:T(8,128)(2,1)}) %reduce-scatter.3.cloned.1.call-update) | async-done | bytes 294928 | tf_op jit(solution)/shard_map/reduce_scatter | solution.py:97
  261.7 1.8 convert_element_type.165
  (108 shorter events, 17.5 us)
Async XLA Ops:
  9.6 1.1 copy-start.8
  9.6 2.2 slice-start
  10.9 0.6 copy-start.31
  11.8 3.6 %copy-start.33 = (f32[8,64]{1,0:T(8,128)}, f32[8,64]{1,0:T(8,128)S(1)}, u32[]{:S(2)}) copy-start(f32[8,64]{1,0:T(8,128)S(1)} %fusion.70) | copy-start | bytes 6148
  21.3 5.6 %copy-start.2 = (bf16[3,8,12,64,64]{4,3,2,0,1:T(8,128)(2,1)}, bf16[3,8,12,64,64]{4,3,2,0,1:T(8,128)(2,1)S(1)}, u32[]{:S(2)}) copy-start(bf16[3,8,12,64,64]{4,3,2,0,1:T(8,128)(2,1)S(1)} %convert_bitcast_fusion) | copy-start | bytes 7077892
  26.9 1.6 copy-start
  26.9 1.7 copy-start.25
  26.9 1.7 copy-start.9
  26.9 2.9 %copy-start.18 = (bf16[768,768]{1,0:T(8,128)(2,1)S(1)}, bf16[768,768]{1,0:T(8,128)(2,1)}, u32[]{:S(2)}) copy-start(bf16[768,768]{1,0:T(8,128)(2,1)} %slice.44) | copy-start | bytes 3538948
  28.5 2.1 copy-start.14
  32.0 26.2 %all-to-all-start = ((bf16[8,64,768]{2,0,1:T(8,128)(2,1)}), bf16[8,64,768]{2,0,1:T(8,128)(2,1)}, u32[]{:S(2)}, u32[]{:S(2)}) async-start(bf16[8,64,768]{2,0,1:T(8,128)(2,1)} %copy.141), calls=%async_computation | async-start | bytes 1572864 | tf_op jit(solution)/shard_map/all_to_all | solution.py:87
  39.4 143.4 %reduce-scatter.5.cloned.1.call-start = ((), (), s32[]{:S(2)}) async-start(), calls=%async_computation.5 | async-start | bytes 5013504 | tf_op jit(solution)/shard_map/reduce_scatter | solution.py:91
  41.9 2.0 slice-start.1
  47.5 16.8 %copy-start.4 = (bf16[768,2304]{0,1:T(8,128)(2,1)S(1)}, bf16[768,2304]{0,1:T(8,128)(2,1)}, u32[]{:S(2)}) copy-start(bf16[768,2304]{0,1:T(8,128)(2,1)} %copy.146) | copy-start | bytes 10616836
  68.0 3.9 %copy-start.20 = (bf16[3,4,12,128,64]{3,4,2,0,1:T(8,128)(2,1)}, bf16[3,4,12,128,64]{3,4,2,0,1:T(8,128)(2,1)S(1)}, u32[]{:S(2)}) copy-start(bf16[3,4,12,128,64]{3,4,2,0,1:T(8,128)(2,1)S(1)} %convert_bitcast_fusion.1) | copy-start | bytes 7077892
  68.6 3.3 %copy-start.24 = (bf16[4,12,128,64]{2,3,0,1:T(8,128)(2,1)S(1)}, bf16[4,12,128,64]{2,3,0,1:T(8,128)(2,1)}, u32[]{:S(2)}) copy-start(bf16[4,12,128,64]{2,3,0,1:T(8,128)(2,1)} %fusion.47) | copy-start | bytes 2359300
  71.8 3.0 %copy-start.5 = (f32[4,12,128,128]{2,3,1,0:T(8,128)}, f32[4,12,128,128]{2,3,1,0:T(8,128)S(1)}, u32[]{:S(2)}) copy-start(f32[4,12,128,128]{2,3,1,0:T(8,128)S(1)} %get-tuple-element.12) | copy-start | bytes 9437188
  71.9 3.0 %copy-start.29 = (f32[4,12,128]{2,1,0:T(8,128)}, f32[4,12,128]{2,1,0:T(8,128)S(1)}, u32[]{:S(2)}) copy-start(f32[4,12,128]{2,1,0:T(8,128)S(1)} %get-tuple-element.11) | copy-start | bytes 73732
  74.8 1.1 copy-start.16
  82.9 4.8 %copy-start.6 = (f32[4,12,128,128]{2,3,1,0:T(8,128)S(1)}, f32[4,12,128,128]{2,3,1,0:T(8,128)}, u32[]{:S(2)}) copy-start(f32[4,12,128,128]{2,3,1,0:T(8,128)} %copy-done.5) | copy-start | bytes 9437188
  82.9 4.8 %copy-start.30 = (f32[4,12,128]{2,1,0:T(8,128)S(1)}, f32[4,12,128]{2,1,0:T(8,128)}, u32[]{:S(2)}) copy-start(f32[4,12,128]{2,1,0:T(8,128)} %copy-done.29) | copy-start | bytes 73732
  82.9 4.8 %copy-start.36 = (bf16[4,12,128,128]{2,3,1,0:T(8,128)(2,1)S(1)}, bf16[4,12,128,128]{2,3,1,0:T(8,128)(2,1)}, u32[]{:S(2)}) copy-start(bf16[4,12,128,128]{2,3,1,0:T(8,128)(2,1)} %get-tuple-element.13) | copy-start | bytes 4718596
  93.9 1.1 copy-start.7
  93.9 1.4 copy-start.21
  93.9 1.6 copy-start.22
  99.9 3.5 %copy-start.17 = (bf16[12,64,768]{2,1,0:T(8,128)(2,1)S(1)}, bf16[12,64,768]{2,1,0:T(8,128)(2,1)}, u32[]{:S(2)}) copy-start(bf16[12,64,768]{2,1,0:T(8,128)(2,1)} %bitcast_convert_fusion.2) | copy-start | bytes 3538948
  106.2 1.4 copy-start.15
  106.2 1.6 copy-start.23
  110.9 24.2 %all-to-all-start.1 = ((bf16[128,4,768]{2,1,0:T(4,128)(2,1)}), bf16[128,4,768]{2,1,0:T(4,128)(2,1)S(1)}, u32[]{:S(2)}, u32[]{:S(2)}) async-start(bf16[128,4,768]{2,1,0:T(4,128)(2,1)} %copy.154), calls=%async_computation.1 | async-start | bytes 1572864 | tf_op jit(solution)/shard_map/all_to_all | solution.py:94
  116.3 145.4 %reduce-scatter.3.cloned.1.call-start = ((), (), s32[]{:S(2)}) async-start(), calls=%async_computation.4 | async-start | bytes 5013504 | tf_op jit(solution)/shard_map/reduce_scatter | solution.py:97
  116.6 4.7 %copy-start.26 = (f32[8,12,64]{2,1,0:T(8,128)S(1)}, f32[8,12,64]{2,1,0:T(8,128)}, u32[]{:S(2)}) copy-start(f32[8,12,64]{2,1,0:T(8,128)} %copy-done.25) | copy-start | bytes 73732
  135.5 3.4 %copy-start.12 = (bf16[8,64,768]{2,1,0:T(8,128)(2,1)}, bf16[8,64,768]{2,1,0:T(8,128)(2,1)S(1)}, u32[]{:S(2)}) copy-start(bf16[8,64,768]{2,1,0:T(8,128)(2,1)S(1)} %all_to_all.24) | copy-start | bytes 2359300
  135.7 5.6 %copy-start.19 = (bf16[768,768]{1,0:T(8,128)(2,1)S(1)}, bf16[768,768]{1,0:T(8,128)(2,1)}, u32[]{:S(2)}) copy-start(bf16[768,768]{1,0:T(8,128)(2,1)} %slice.44) | copy-start | bytes 3538948
  141.3 1.9 copy-start.1
  141.3 1.9 copy-start.28
  143.2 2.6 copy-start.27
  143.2 3.2 %slice-start.2 = ((s8[4718592]{0:T(1024)(128)(4,1)}), s8[4194304]{0:T(1024)(128)(4,1)S(1)}, s32[]{:S(2)}) async-start(s8[4718592]{0:T(1024)(128)(4,1)} %bitcast.194), calls=%async_computation.8 | async-start | bytes 8388608
  145.8 1.1 slice-start.3
  146.3 2.3 copy-start.35
  147.8 1.2 copy-start.37
  147.8 1.7 copy-start.10
  147.8 1.7 copy-start.34
  149.5 4.0 %copy-start.38 = (bf16[1,8,12,64,64]{4,3,2,1,0:T(8,128)(2,1)}, bf16[1,8,12,64,64]{4,3,2,1,0:T(8,128)(2,1)S(1)}, u32[]{:S(2)}) copy-start(bf16[1,8,12,64,64]{4,3,2,1,0:T(8,128)(2,1)S(1)} %fusion.36) | copy-start | bytes 2359300
  162.1 2.0 copy-start.3
  164.2 6.0 %copy-start.32 = (f32[8,64]{1,0:T(8,128)S(1)}, f32[8,64]{1,0:T(8,128)}, u32[]{:S(2)}) copy-start(f32[8,64]{1,0:T(8,128)} %copy-done.31) | copy-start | bytes 6148
  164.2 6.0 %copy-start.11 = (bf16[8,64,768]{2,1,0:T(8,128)(2,1)S(1)}, bf16[8,64,768]{2,1,0:T(8,128)(2,1)}, u32[]{:S(2)}) copy-start(bf16[8,64,768]{2,1,0:T(8,128)(2,1)} %param.4) | copy-start | bytes 2359300
  164.2 6.0 %copy-start.13 = (bf16[8,64,768]{2,1,0:T(8,128)(2,1)S(1)}, bf16[8,64,768]{2,1,0:T(8,128)(2,1)}, u32[]{:S(2)}) copy-start(bf16[8,64,768]{2,1,0:T(8,128)(2,1)} %copy-done.12) | copy-start | bytes 2359300
Sparse Core Ops, SparseCore 0:
  106.4 76.3 reduce-scatter.4
  187.1 74.5 reduce-scatter.2
where the time goes:
time: 272 us; the launch traced here: 270 us
  waiting for transfers between devices  109 us (40%)
  matrix products  59.9 us (22%)
  local copies, waits for them, and re-layouts  45.9 us (17%)
  other arithmetic  28.1 us (10%)
  between operations  14.5 us (5%)
  starting transfers between devices  13.2 us (5%)
    reduce_scatter x1, waiting for transfers between devices, body(): lax.psum_scatter(row_term.astype(jnp.bfloat16), 'cell', scatter_dimension...  77.2 us
    all_to_all x1, waiting for transfers between devices, body(): lax.all_to_all(grad_mid_columns, 'cell', split_axis=0, concat_axis=1, til...  13.1 us
    unnamed x82, local copies, waits for them, and re-layouts  11.5 us
    reduce_scatter x1, waiting for transfers between devices, body(): lax.psum_scatter(col_term.astype(jnp.bfloat16), 'cell', scatter_dimension...  11.3 us
    dot_general x6, matrix products, attend_heads(): jnp.einsum('bhle,bhme->bhlm', queries, keys_part, preferred_element_type=...  11 us
    dot_general x2, matrix products, backward(): jnp.einsum('tbhle,dthe->' + cell_form, grad_projected, projection, prefer...  10.3 us
    slice x6, local copies, waits for them, and re-layouts, split_weight(): weight[:, :3 * model_width].reshape(model_width, 3, HEADS, head_size)  9.54 us
    dot_general x2, matrix products, forward(): jnp.einsum(cell_form + ',dthe->tbhle', normed, projection, preferred_elem...  9.46 us
  transfers between devices with their start and end apart: 4, of which 4 were waited for; matrix products, arithmetic and copies ran while one was open for 19% of the time, Pallas kernels for 0%

commit v1 on v0

--- a/solution.py
+++ b/solution.py
@@ -82,21 +82,37 @@
     return jnp.concatenate([first, second], axis=1)
 
 
+def pair_then_scatter(term, axis_name):
+    count = lax.axis_size(axis_name)
+    block = term.shape[0] // count
+    index = lax.axis_index(axis_name)
+    pairs = term.reshape((count // 2, 2, block) + term.shape[1:])
+    mine = index & 1
+    keep = lax.dynamic_index_in_dim(pairs, mine, axis=1, keepdims=False)
+    send = lax.dynamic_index_in_dim(pairs, 1 - mine, axis=1, keepdims=False)
+    received = lax.ppermute(send.astype(jnp.bfloat16), axis_name, perm=[(i, i ^ 1) for i in range(count)])
+    summed = (keep + received.astype(jnp.float32)).astype(jnp.bfloat16)
+    groups = [list(range(low, count, 2)) for low in range(2)]
+    return lax.psum_scatter(
+        summed.reshape((count // 2 * block,) + term.shape[1:]),
+        axis_name,
+        scatter_dimension=0,
+        axis_index_groups=groups,
+        tiled=True,
+    ).astype(jnp.float32)
+
+
 def body(cells, cotangent, row_weight, col_weight):
     row_saved = forward(cells, row_weight, 1, True)
     mid_columns = lax.all_to_all(row_saved[4], "cell", split_axis=1, concat_axis=0, tiled=True)
     col_saved = forward(mid_columns, col_weight, 0, False)
     grad_mid_columns, grad_col_proj = backward(col_saved, col_weight, cotangent, 0)
     col_term = weight_term(col_saved[1], grad_col_proj, col_saved[3], cotangent, 0)
-    col_grad = lax.psum_scatter(
-        col_term.astype(jnp.bfloat16), "cell", scatter_dimension=0, tiled=True
-    ).astype(jnp.float32)
+    col_grad = pair_then_scatter(col_term, "cell")
     grad_mid = lax.all_to_all(grad_mid_columns, "cell", split_axis=0, concat_axis=1, tiled=True)
     grad_cells, grad_row_proj = backward(row_saved, row_weight, grad_mid, 1)
     row_term = weight_term(row_saved[1], grad_row_proj, row_saved[3], grad_mid, 1)
-    row_grad = lax.psum_scatter(
-        row_term.astype(jnp.bfloat16), "cell", scatter_dimension=0, tiled=True
-    ).astype(jnp.float32)
+    row_grad = pair_then_scatter(row_term, "cell")
     return (grad_cells, row_grad, col_grad)
 
 

time: 272 us -> 295 us (1.085)
  local copies, waits for them, and re-layouts: 45.9 us -> 97.4 us
  waiting for transfers between devices: 109 us -> 73.7 us
  matrix products: 59.9 us -> 64.8 us
    concatenate x0 -> x2, local copies, waits for them, and re-layouts: none -> 56.2 us  [weight_term(): return jnp.concatenate([first, second], axis=1)]
    reduce_scatter x2, waiting for transfers between devices: 88.4 us -> 60.1 us  [pair_then_scatter(): lax.psum_scatter(summed.reshape((count // 2 * block,) + term.shape[1:]),...]
    all_to_all x1, waiting for transfers between devices: 13.1 us -> 1.9 us  [body(): lax.all_to_all(grad_mid_columns, 'cell', split_axis=0, concat_axis=1, til...]
    convert_element_type x2 -> x6, other arithmetic: 3.63 us -> 13.6 us  [the longest x2 5.87 us: pair_then_scatter(): summed = (keep + received.astype(jnp.float32)).astype(jnp.bfloat16)]
    concatenate x2 -> x0, other arithmetic: 6.86 us -> none  [weight_term(): return jnp.concatenate([first, second], axis=1)]
    dot_general x1 -> x3, local copies, waits for them, and re-layouts: 0.49 us -> 6.42 us  [weight_term(): jnp.einsum(cell_form + ',tbhle->dthe', normed, grad_projected, preferred_...]
    unnamed x82 -> x60, local copies, waits for them, and re-layouts: 11.5 us -> 6.87 us
    reshape x1 -> x0, local copies, waits for them, and re-layouts: 4.62 us -> none  [weight_term(): first = jnp.einsum(cell_form + ',tbhle->dthe', normed, grad_projected, pr...]
  transfers between devices with their start and end apart: 4 -> 6, of which waited for: 4 -> 4; matrix products, arithmetic and copies ran while one was open for 19% -> 41% of each run, Pallas kernels for 0% -> 0%
where the time goes in v1:
time: 295 us; the launch traced here: 293 us
  local copies, waits for them, and re-layouts  97.4 us (33%)
  waiting for transfers between devices  73.7 us (25%)
  matrix products  64.8 us (22%)
  other arithmetic  28.1 us (10%)
  between operations  14.5 us (5%)
  starting transfers between devices  14.2 us (5%)
    reduce_scatter x2, waiting for transfers between devices, pair_then_scatter(): lax.psum_scatter(summed.reshape((count // 2 * block,) + term.shape[1:]),...  60.1 us
    concatenate x2, local copies, waits for them, and re-layouts, weight_term(): return jnp.concatenate([first, second], axis=1)  56.2 us
    dot_general x5, matrix products, attend_heads(): jnp.einsum('bhlm,bhme->bhle', weights, values_part, preferred_element_typ...  12.5 us
    dot_general x2, matrix products, weight_term(): jnp.einsum(cell_form + ',tbhle->dthe', normed, grad_projected, preferred_...  11 us
    dot_general x2, matrix products, backward(): jnp.einsum('tbhle,dthe->' + cell_form, grad_projected, projection, prefer...  9.89 us
    dot_general x2, matrix products, forward(): jnp.einsum(cell_form + ',dthe->tbhle', normed, projection, preferred_elem...  9.46 us
    dot_general x6, matrix products, attend_heads(): jnp.einsum('bhle,bhme->bhlm', queries, keys_part, preferred_element_type=...  9.45 us
    slice x6, local copies, waits for them, and re-layouts, split_weight(): weight[:, :3 * model_width].reshape(model_width, 3, HEADS, head_size)  9.42 us
  transfers between devices with their start and end apart: 6, of which 4 were waited for; matrix products, arithmetic and copies ran while one was open for 41% of the time, Pallas kernels for 0%

profile of v1, /device:TPU:0, one launch (start us, length us, event | category | flops | bytes accessed | tf_op | source)
XLA Modules:
  0.0 292.7 jit_solution(12648552916811847191)
XLA Ops:
  7.2 2.4 slice.44
  11.8 3.6 %copy.143 = bf16[768,2304]{0,1:T(8,128)(2,1)} copy(bf16[768,2304]{1,0:T(8,128)(2,1)S(1)} %slice-done.3) | data formatting | bytes 7077888 | tf_op jit(solution)/shard_map/slice | solution.py:33
  15.4 5.8 %convert_bitcast_fusion = bf16[3,8,12,64,64]{4,3,2,0,1:T(8,128)(2,1)S(1)} fusion(bf16[768,3,12,64,1]{0,3,2,1,4:T(8,128)(2,1)} %bitcast.232, bf16[8,64,768]{2,1,0:T(8,128)(2,1)} %param.4, f32[8,64]{1,0:T(8,128)S(1)} %fusion.88), kind=kOutput, calls=%fused_computation.24 | convolution fusion | flops 1814298624 | bytes 6686720 | tf_op jit(solution)/shard_map/bld,dthe->tbhle/dot_general | solution.py:43
  22.2 4.7 %fusion.100 = (f32[8,12,64]{2,1,0:T(8,128)S(1)}, f32[8,12,64,64]{2,3,1,0:T(8,128)S(1)}) fusion(f32[8,12,64,64]{2,3,1,0:T(8,128)S(1)} %fusion.58), kind=kOutput, calls=%fused_computation.147 | output fusion | flops 1572927 | bytes 3170304 | tf_op jit(solution)/shard_map/sub | solution.py:21
  31.9 7.4 %all-to-all-start = ((bf16[8,64,768]{2,0,1:T(8,128)(2,1)}), bf16[8,64,768]{2,0,1:T(8,128)(2,1)}, u32[]{:S(2)}, u32[]{:S(2)}) async-start(bf16[8,64,768]{2,0,1:T(8,128)(2,1)} %copy.145), calls=%async_computation | async-start | bytes 1572864 | tf_op jit(solution)/shard_map/all_to_all | solution.py:107
  39.4 2.4 slice.39
  41.8 2.0 slice-done.2
  43.8 3.6 %copy.150 = bf16[768,2304]{0,1:T(8,128)(2,1)} copy(bf16[768,2304]{1,0:T(8,128)(2,1)S(1)} %slice-done.2) | data formatting | bytes 7077888 | tf_op jit(solution)/shard_map/slice | solution.py:33
  47.3 3.3 %fusion.63 = bf16[4,12,128,64]{2,3,0,1:T(8,128)(2,1)} fusion(bf16[12,64,768,1]{2,1,3,0:T(8,128)(2,1)} %bitcast.242, bf16[128,4,768]{2,1,0:T(4,128)(2,1)} %param.5), kind=kOutput, calls=%fused_computation.107 | convolution fusion | flops 604372992 | bytes 2752512 | tf_op jit(solution)/shard_map/lbf,hef->bhle/dot_general | solution.py:60
  50.7 7.5 %all-to-all-done = bf16[8,64,768]{2,0,1:T(8,128)(2,1)} async-done(((bf16[8,64,768]{2,0,1:T(8,128)(2,1)}), bf16[8,64,768]{2,0,1:T(8,128)(2,1)}, u32[]{:S(2)}, u32[]{:S(2)}) %all-to-all-start) | async-done | bytes 786464 | tf_op jit(solution)/shard_map/all_to_all | solution.py:107
  58.1 2.0 multiply_reduce_fusion.2
  60.1 1.4 copy.147
  62.9 1.4 copy.148
  64.3 3.6 %convert_bitcast_fusion.1 = bf16[3,4,12,128,64]{3,4,2,0,1:T(8,128)(2,1)S(1)} fusion(bf16[768,3,12,64,1]{0,3,2,1,4:T(8,128)(2,1)S(1)} %bitcast.234, f32[16,8,4]{1,2,0:T(4,128)} %copy.148, bf16[8,64,768]{2,0,1:T(8,128)(2,1)} %all-to-all-done), kind=kOutput, calls=%fused_computation.58 | convolution fusion | flops 1814298624 | bytes 6686720 | tf_op jit(solution)/shard_map/lbd,dthe->tbhle/dot_general | solution.py:43
  68.6 3.0 %fusion.101 = (f32[4,12,128]{2,1,0:T(8,128)S(1)}, f32[4,12,128,128]{2,3,1,0:T(8,128)S(1)}) fusion(f32[4,12,128,128]{2,3,1,0:T(8,128)S(1)} %fusion.81), kind=kOutput, calls=%fused_computation.148 | output fusion | flops 3145855 | bytes 6316032 | tf_op jit(solution)/shard_map/jvp()/sub | solution.py:21
  71.6 2.2 fusion.18
  73.9 2.1 fusion.65
  76.0 1.7 fusion.64
  79.2 2.9 fusion.62
  82.4 1.9 copy.166
  84.3 3.4 %fusion.45 = (f32[128,4]{0,1:T(4,128)S(1)}, f32[4,128,768,1,1]{2,1,3,0,4:T(8,128)S(1)}) fusion(bf16[768,3,12,64,1]{0,3,2,4,1:T(8,128)(2,1)S(1)} %bitcast.235, bf16[1,4,12,128,64]{3,4,2,1,0:T(8,128)(2,1)S(1)} %fusion.62, bf16[1,4,12,128,64]{3,4,2,1,0:T(8,128)(2,1)S(1)} %copy-done.16, bf16[1,4,12,128,64]{3,4,2,1,0:T(8,128)(2,1)S(1)} %copy-done.17, ...), kind=kOutput, calls=%fused_computation.86 | convolution fusion | flops 1815477760 | bytes 8259584 | tf_op jit(solution)/shard_map/tbhle,dthe->lbd/dot_general | solution.py:65
  87.7 1.6 fusion.68
  90.5 1.5 copy.158
  92.0 5.5 %all-to-all-start.1 = ((bf16[128,4,768]{2,1,0:T(4,128)(2,1)}), bf16[128,4,768]{2,1,0:T(4,128)(2,1)S(1)}, u32[]{:S(2)}, u32[]{:S(2)}) async-start(bf16[128,4,768]{2,1,0:T(4,128)(2,1)} %copy.158), calls=%async_computation.1 | async-start | bytes 1572864 | tf_op jit(solution)/shard_map/all_to_all | solution.py:112
  97.8 3.2 %fusion.76 = f32[8,2,48,2304,1]{3,2,0,1,4:T(8,128)S(1)} fusion(bf16[2304,4,128,1,1]{2,0,3,4,1:T(8,128)(2,1)S(1)} %bitcast.237, bf16[8,2,48,4,128]{4,2,1,0,3:T(8,128)(2,1)} %bitcast.243), kind=kOutput, calls=%fused_computation.123 | convolution fusion | flops 1811939328 | bytes 10223616 | tf_op jit(solution)/shard_map/lbd,tbhle->dthe/dot_general | solution.py:76
  101.0 3.3 %copy.238 = f32[8,2,48,2304,1]{3,2,1,0,4:T(8,128)} copy(f32[8,2,48,2304,1]{3,2,0,1,4:T(8,128)S(1)} %fusion.76) | data formatting | bytes 14155776 | tf_op jit(solution)/shard_map/lbd,tbhle->dthe/dot_general | solution.py:76
  104.3 3.0 %fusion.60 = f32[12,64,768,1]{2,1,3,0:T(8,128)S(1)} fusion(bf16[4,12,128,128]{2,3,1,0:T(8,128)(2,1)} %get-tuple-element.4, bf16[128,4,768]{2,1,0:T(4,128)(2,1)} %param.5, bf16[3,4,12,128,64]{3,4,2,0,1:T(8,128)(2,1)} %copy-done.15), kind=kOutput, calls=%fused_computation.105 | convolution fusion | flops 705036288 | bytes 5505024 | tf_op jit(solution)/shard_map/bhle,lbf->hef/dot_general | solution.py:79
  107.3 3.8 %fusion.31 = bf16[8,48,3072]{2,1,0:T(8,128)(2,1)} fusion(s32[]{:T(128)S(6)} %select_n.10, f32[8,2,48,768]{3,2,1,0:T(8,128)S(1)} %bitcast.228, f32[8,2,48,2304]{3,2,1,0:T(8,128)} %bitcast.219), kind=kLoop, calls=%fused_computation.56 | loop fusion | flops 4718592 | bytes 11796484 | tf_op jit(solution)/shard_map/convert_element_type | solution.py:93
  111.5 2.8 copy.163
  114.3 1.9 all-to-all-done.1
  117.1 1.4 copy.239
  119.6 3.1 %convolution_convert_fusion = bf16[8,64,12,64]{3,1,2,0:T(8,128)(2,1)S(1)} fusion(bf16[12,64,768,1]{2,1,0,3:T(8,128)(2,1)} %bitcast.240, bf16[8,64,768,1]{2,1,0,3:T(8,128)(2,1)} %reshape.137), kind=kOutput, calls=%fused_computation.61 | convolution fusion | flops 604372992 | bytes 2752512 | tf_op jit(solution)/shard_map/blf,hef->bhle/dot_general | solution.py:60
  122.7 3.0 %fusion.23 = (f32[8,12,64]{2,1,0:T(8,128)S(1)}, bf16[8,12,64,64]{2,3,1,0:T(8,128)(2,1)S(1)}) fusion(f32[8,12,64,64]{2,3,1,0:T(8,128)S(1)} %copy-done.2, f32[8,12,64]{2,1,0:T(8,128)S(1)} %multiply_divide_fusion, bf16[3,8,12,64,64]{4,3,2,0,1:T(8,128)(2,1)} %copy-done.3, bf16[8,64,12,64]{3,1,2,0:T(8,128)(2,1)S(1)} %convolution_convert_fusion), kind=kOutput, calls=%fused_computation.38 | convolution fusion | flops 52291584 | bytes 4767744 | tf_op jit(solution)/shard_map/transpose(jvp(bhlm,bhme->bhle))/dot_general | solution.py:22
  125.7 2.1 fusion.50
  127.8 2.0 fusion.51
  129.9 3.8 %fusion.7 = bf16[8,48,3072]{2,1,0:T(8,128)(2,1)} fusion(s32[]{:T(128)S(6)} %select_n.9, f32[8,2,48,2304]{3,2,1,0:T(8,128)S(1)} %bitcast.222, f32[8,2,48,768]{3,2,1,0:T(8,128)S(1)} %bitcast.229, bf16[8,48,3072]{2,1,0:T(8,128)(2,1)} %collective-permute-done.1), kind=kLoop, calls=%fused_computation.16 | loop fusion | flops 4718592 | bytes 14155780 | tf_op jit(solution)/shard_map/convert_element_type | solution.py:94
  135.0 3.6 %fusion.52 = bf16[1,8,12,64,64]{4,3,2,1,0:T(8,128)(2,1)} fusion(bf16[8,64,12,64]{3,1,2,0:T(8,128)(2,1)S(1)} %copy-done.13, f32[8,12,64,64]{2,3,1,0:T(8,128)} %copy-done.1, f32[8,12,64]{2,1,0:T(8,128)S(1)} %copy-done.21), kind=kOutput, calls=%fused_computation.98 | convolution fusion | flops 51511296 | bytes 3170304 | tf_op jit(solution)/shard_map/transpose(jvp(bhlm,bhme->bhle))/dot_general | solution.py:22
  139.7 7.9 %convolution_bitcast_fusion = f32[768,3,12,64]{0,3,2,1:T(8,128)} fusion(bf16[1,8,12,64,64]{4,3,2,1,0:T(8,128)(2,1)} %fusion.52, bf16[1,8,12,64,64]{4,3,2,1,0:T(8,128)(2,1)} %fusion.51, bf16[1,8,12,64,64]{4,3,2,1,0:T(8,128)(2,1)} %fusion.50, bf16[8,64,768]{2,1,0:T(8,128)(2,1)S(1)} %copy-done.8, f32[8,64]{1,0:T(8,128)S(1)} %copy-done.25), kind=kOutput, calls=%fused_computation.48 | convolution fusion | flops 1820196864 | bytes 10225664 | tf_op jit(solution)/shard_map/bld,tbhle->dthe/dot_general | solution.py:76
  147.6 31.9 %reshape.147 = f32[8,2,48,2304]{2,1,0,3:T(2,128)} reshape(f32[768,3,12,64]{0,3,2,1:T(8,128)} %convolution_bitcast_fusion) | data formatting | bytes 14155776 | tf_op jit(solution)/shard_map/concatenate | solution.py:82
  179.5 24.4 %copy.195 = f32[8,2,48,2304]{3,2,1,0:T(8,128)} copy(f32[8,2,48,2304]{2,1,0,3:T(2,128)} %reshape.147) | data formatting | bytes 14155776 | tf_op jit(solution)/shard_map/concatenate | solution.py:82
  203.8 2.2 convolution_bitcast_fusion.1
  207.8 4.3 %collective-permute-done = bf16[8,48,3072]{2,1,0:T(8,128)(2,1)S(1)} collective-permute-done((bf16[8,48,3072]{2,1,0:T(8,128)(2,1)S(1)}, bf16[8,48,3072]{2,1,0:T(8,128)(2,1)S(1)}, u32[]{:S(2)}, u32[]{:S(2)}) %collective-permute-start) | collective-permute-done | bytes 2359328 | tf_op jit(solution)/shard_map/ppermute | solution.py:93
  212.0 2.1 fusion.13
  214.3 6.5 %fusion.40 = (f32[8,64]{1,0:T(8,128)S(1)}, f32[8,64,768,1,1]{2,1,3,0,4:T(8,128)S(1)}) fusion(bf16[8,64,768]{2,1,0:T(8,128)(2,1)S(1)} %copy-done.8, bf16[768,3,12,64,1]{0,3,2,4,1:T(8,128)(2,1)} %bitcast.233, bf16[1,8,12,64,64]{4,3,2,1,0:T(8,128)(2,1)} %fusion.52, bf16[1,8,12,64,64]{4,3,2,1,0:T(8,128)(2,1)} %fusion.51, bf16[1,8,12,64,64]{4,3,2,1,0:T(8,128)(2,1)} %fusion.50), kind=kOutput, calls=%fused_computation.75 | convolution fusion | flops 1815477760 | bytes 8259584 | tf_op jit(solution)/shard_map/tbhle,dthe->bld/dot_general | solution.py:65
  220.9 1.3 fusion.36
  222.2 1.8 convert_element_type.198
  224.0 60.1 %reduce-scatter.3.cloned.1.call-done = bf16[48,3072]{1,0:T(8,128)(2,1)} async-done(((bf16[384,3072]{1,0:T(8,128)(2,1)}), bf16[48,3072]{1,0:T(8,128)(2,1)}) %reduce-scatter.3.cloned.1.call-update) | async-done | bytes 294928 | tf_op jit(solution)/shard_map/reduce_scatter | solution.py:96
  284.1 1.8 convert_element_type.191
  (95 shorter events, 20.2 us)
Async XLA Ops:
  9.6 1.1 copy-start.6
  9.6 2.2 slice-start.3
  10.9 0.6 copy-start.22
  11.8 3.6 %copy-start.24 = (f32[8,64]{1,0:T(8,128)}, f32[8,64]{1,0:T(8,128)S(1)}, u32[]{:S(2)}) copy-start(f32[8,64]{1,0:T(8,128)S(1)} %fusion.88) | copy-start | bytes 6148
  21.3 5.6 %copy-start.3 = (bf16[3,8,12,64,64]{4,3,2,0,1:T(8,128)(2,1)}, bf16[3,8,12,64,64]{4,3,2,0,1:T(8,128)(2,1)S(1)}, u32[]{:S(2)}) copy-start(bf16[3,8,12,64,64]{4,3,2,0,1:T(8,128)(2,1)S(1)} %convert_bitcast_fusion) | copy-start | bytes 7077892
  26.9 1.7 copy-start.1
  26.9 1.7 copy-start.20
  26.9 1.7 copy-start.7
  26.9 2.8 copy-start.14
  28.6 2.0 copy-start.10
  31.9 26.2 %all-to-all-start = ((bf16[8,64,768]{2,0,1:T(8,128)(2,1)}), bf16[8,64,768]{2,0,1:T(8,128)(2,1)}, u32[]{:S(2)}, u32[]{:S(2)}) async-start(bf16[8,64,768]{2,0,1:T(8,128)(2,1)} %copy.145), calls=%async_computation | async-start | bytes 1572864 | tf_op jit(solution)/shard_map/all_to_all | solution.py:107
  41.8 2.0 slice-start.2
  47.3 17.0 %copy-start.4 = (bf16[768,2304]{0,1:T(8,128)(2,1)S(1)}, bf16[768,2304]{0,1:T(8,128)(2,1)}, u32[]{:S(2)}) copy-start(bf16[768,2304]{0,1:T(8,128)(2,1)} %copy.150) | copy-start | bytes 10616836
  67.9 8.0 %copy-start.15 = (bf16[3,4,12,128,64]{3,4,2,0,1:T(8,128)(2,1)}, bf16[3,4,12,128,64]{3,4,2,0,1:T(8,128)(2,1)S(1)}, u32[]{:S(2)}) copy-start(bf16[3,4,12,128,64]{3,4,2,0,1:T(8,128)(2,1)S(1)} %convert_bitcast_fusion.1) | copy-start | bytes 7077892
  68.6 3.1 %copy-start.18 = (bf16[4,12,128,64]{2,3,0,1:T(8,128)(2,1)S(1)}, bf16[4,12,128,64]{2,3,0,1:T(8,128)(2,1)}, u32[]{:S(2)}) copy-start(bf16[4,12,128,64]{2,3,0,1:T(8,128)(2,1)} %fusion.63) | copy-start | bytes 2359300
  79.2 2.9 copy-start.16
  79.2 2.9 copy-start.17
  84.3 3.4 %copy-start.19 = (bf16[128,4,768]{2,1,0:T(4,128)(2,1)S(1)}, bf16[128,4,768]{2,1,0:T(4,128)(2,1)}, u32[]{:S(2)}) copy-start(bf16[128,4,768]{2,1,0:T(4,128)(2,1)} %param.5) | copy-start | bytes 2359300
  90.5 7.2 %copy-start.9 = (bf16[3,12,64,4,128]{4,2,1,0,3:T(8,128)(2,1)S(1)}, bf16[3,12,64,4,128]{4,2,1,0,3:T(8,128)(2,1)}, u32[]{:S(2)}) copy-start(bf16[3,12,64,4,128]{4,2,1,0,3:T(8,128)(2,1)} %copy.166) | copy-start | bytes 7077892
  92.0 24.2 %all-to-all-start.1 = ((bf16[128,4,768]{2,1,0:T(4,128)(2,1)}), bf16[128,4,768]{2,1,0:T(4,128)(2,1)S(1)}, u32[]{:S(2)}, u32[]{:S(2)}) async-start(bf16[128,4,768]{2,1,0:T(4,128)(2,1)} %copy.158), calls=%async_computation.1 | async-start | bytes 1572864 | tf_op jit(solution)/shard_map/all_to_all | solution.py:112
  97.5 124.7 %reduce-scatter.5.cloned.1.call-start = ((), (), s32[]{:S(2)}) async-start(), calls=%async_computation.5 | async-start | bytes 2654208 | tf_op jit(solution)/shard_map/reduce_scatter | solution.py:96
  111.1 3.2 %copy-start.21 = (f32[8,12,64]{2,1,0:T(8,128)S(1)}, f32[8,12,64]{2,1,0:T(8,128)}, u32[]{:S(2)}) copy-start(f32[8,12,64]{2,1,0:T(8,128)} %copy-done.20) | copy-start | bytes 73732
  111.1 18.7 %collective-permute-start.1 = (bf16[8,48,3072]{2,1,0:T(8,128)(2,1)}, bf16[8,48,3072]{2,1,0:T(8,128)(2,1)}, u32[]{:S(2)}, u32[]{:S(2)}) collective-permute-start(bf16[8,48,3072]{2,1,0:T(8,128)(2,1)} %fusion.31), channel_id=1, source_target_pairs={{0,1},{1,0},{2,3},{3,2},{4,5},{5,4},{6,7},{7,6},{8,9},{9,8},{10,11... | collective-permute-start | bytes 7077896 | tf_op jit(solution)/shard_map/ppermute | solution.py:93
  116.2 0.9 copy-start.5
  119.6 3.1 %copy-start.2 = (f32[8,12,64,64]{2,3,1,0:T(8,128)S(1)}, f32[8,12,64,64]{2,3,1,0:T(8,128)}, u32[]{:S(2)}) copy-start(f32[8,12,64,64]{2,3,1,0:T(8,128)} %copy-done.1) | copy-start | bytes 4718596
  119.6 6.1 %slice-start.4 = ((s8[4718592]{0:T(1024)(128)(4,1)}), s8[4194304]{0:T(1024)(128)(4,1)S(1)}, s32[]{:S(2)}) async-start(s8[4718592]{0:T(1024)(128)(4,1)} %bitcast.230), calls=%async_computation.10 | async-start | bytes 8388608
  122.7 3.0 %copy-start.12 = (bf16[8,64,12,64]{3,1,2,0:T(8,128)(2,1)}, bf16[8,64,12,64]{3,1,2,0:T(8,128)(2,1)S(1)}, u32[]{:S(2)}) copy-start(bf16[8,64,12,64]{3,1,2,0:T(8,128)(2,1)S(1)} %convolution_convert_fusion) | copy-start | bytes 2359300
  122.7 3.0 %slice-start.5 = ((s8[4718592]{0:T(1024)(128)(4,1)}), s8[524288]{0:T(1024)(128)(4,1)S(1)}, s32[]{:S(2)}) async-start(s8[4718592]{0:T(1024)(128)(4,1)} %bitcast.230), calls=%async_computation.11 | async-start | bytes 1048576
  125.7 4.1 %slice-start = ((s8[7077888]{0:T(1024)(128)(4,1)}), s8[4194304]{0:T(1024)(128)(4,1)S(1)}, s32[]{:S(2)}) async-start(s8[7077888]{0:T(1024)(128)(4,1)} %bitcast.220), calls=%async_computation.6 | async-start | bytes 8388608
  127.8 2.0 slice-start.1
  133.6 1.4 copy-start.13
  133.6 6.1 %copy-start.8 = (bf16[8,64,768]{2,1,0:T(8,128)(2,1)S(1)}, bf16[8,64,768]{2,1,0:T(8,128)(2,1)}, u32[]{:S(2)}) copy-start(bf16[8,64,768]{2,1,0:T(8,128)(2,1)} %param.4) | copy-start | bytes 2359300
  133.7 6.1 %copy-start.25 = (f32[8,64]{1,0:T(8,128)S(1)}, f32[8,64]{1,0:T(8,128)}, u32[]{:S(2)}) copy-start(f32[8,64]{1,0:T(8,128)} %copy-done.24) | copy-start | bytes 6148
  133.7 150.4 %reduce-scatter.3.cloned.1.call-start = ((), (), s32[]{:S(2)}) async-start(), calls=%async_computation.4 | async-start | bytes 2654208 | tf_op jit(solution)/shard_map/reduce_scatter | solution.py:96
  179.4 24.4 %copy-start.11 = (bf16[12,64,8,64]{3,2,1,0:T(8,128)(2,1)S(1)}, bf16[12,64,8,64]{3,2,1,0:T(8,128)(2,1)}, u32[]{:S(2)}) copy-start(bf16[12,64,8,64]{3,2,1,0:T(8,128)(2,1)} %copy.163) | copy-start | bytes 2359300
  203.8 3.2 %copy-start = (f32[8,2,48,2304]{3,2,1,0:T(8,128)S(1)}, f32[8,2,48,2304]{3,2,1,0:T(8,128)}, u32[]{:S(2)}) copy-start(f32[8,2,48,2304]{3,2,1,0:T(8,128)} %copy.195) | copy-start | bytes 21233668
  207.4 4.6 %collective-permute-start = (bf16[8,48,3072]{2,1,0:T(8,128)(2,1)S(1)}, bf16[8,48,3072]{2,1,0:T(8,128)(2,1)S(1)}, u32[]{:S(2)}, u32[]{:S(2)}) collective-permute-start(bf16[8,48,3072]{2,1,0:T(8,128)(2,1)S(1)} %fusion.30), channel_id=1, source_target_pairs={{0,1},{1,0},{2,3},{3,2},{4,5},{5,4},{6,7},{7,6},{8,9},{9,8},{10,11... | collective-permute-start | bytes 7077896 | tf_op jit(solution)/shard_map/ppermute | solution.py:93
  214.3 6.5 %copy-start.23 = (f32[8,64]{1,0:T(8,128)S(1)}, f32[8,64]{1,0:T(8,128)}, u32[]{:S(2)}) copy-start(f32[8,64]{1,0:T(8,128)} %copy-done.22) | copy-start | bytes 6148
Sparse Core Ops, SparseCore 0:
  133.8 69.9 reduce-scatter.4
  214.3 69.7 reduce-scatter.2

commit v2 on v0

--- a/solution.py
+++ b/solution.py
@@ -82,15 +82,31 @@
     return jnp.concatenate([first, second], axis=1)
 
 
+def pair_then_exchange(term, axis_name):
+    count = lax.axis_size(axis_name)
+    block = term.shape[0] // count
+    index = lax.axis_index(axis_name)
+    sent = lax.optimization_barrier(term.astype(jnp.bfloat16))
+    pairs = sent.reshape((count // 2, 2, block) + term.shape[1:])
+    mine = index & 1
+    keep = lax.dynamic_index_in_dim(pairs, mine, axis=1, keepdims=False)
+    send = lax.dynamic_index_in_dim(pairs, 1 - mine, axis=1, keepdims=False)
+    received = lax.ppermute(send, axis_name, perm=[(i, i ^ 1) for i in range(count)])
+    summed = (keep.astype(jnp.float32) + received.astype(jnp.float32)).astype(jnp.bfloat16)
+    groups = [list(range(low, count, 2)) for low in range(2)]
+    gathered = lax.all_to_all(
+        summed, axis_name, split_axis=0, concat_axis=0, axis_index_groups=groups, tiled=True
+    )
+    return jnp.sum(gathered.astype(jnp.float32), axis=0)
+
+
 def body(cells, cotangent, row_weight, col_weight):
     row_saved = forward(cells, row_weight, 1, True)
     mid_columns = lax.all_to_all(row_saved[4], "cell", split_axis=1, concat_axis=0, tiled=True)
     col_saved = forward(mid_columns, col_weight, 0, False)
     grad_mid_columns, grad_col_proj = backward(col_saved, col_weight, cotangent, 0)
     col_term = weight_term(col_saved[1], grad_col_proj, col_saved[3], cotangent, 0)
-    col_grad = lax.psum_scatter(
-        col_term.astype(jnp.bfloat16), "cell", scatter_dimension=0, tiled=True
-    ).astype(jnp.float32)
+    col_grad = pair_then_exchange(col_term, "cell")
     grad_mid = lax.all_to_all(grad_mid_columns, "cell", split_axis=0, concat_axis=1, tiled=True)
     grad_cells, grad_row_proj = backward(row_saved, row_weight, grad_mid, 1)
     row_term = weight_term(row_saved[1], grad_row_proj, row_saved[3], grad_mid, 1)

time: 272 us -> 244 us (0.90)
  waiting for transfers between devices: 109 us -> 92 us
  local copies, waits for them, and re-layouts: 45.9 us -> 37 us
  starting transfers between devices: 13.2 us -> 18.9 us
  matrix products: 59.9 us -> 55.3 us
    all_to_all x0 -> x1, waiting for transfers between devices: none -> 65 us  [pair_then_exchange(): lax.all_to_all(summed, axis_name, split_axis=0, concat_axis=0, axis_index...]
    reduce_scatter x1, waiting for transfers between devices: 77.2 us -> 14.9 us  [body(): lax.psum_scatter(row_term.astype(jnp.bfloat16), 'cell', scatter_dimension...]
    reduce_scatter x1 -> x0, waiting for transfers between devices: 11.3 us -> none  [body(): lax.psum_scatter(col_term.astype(jnp.bfloat16), 'cell', scatter_dimension...]
    all_to_all x1, waiting for transfers between devices: 13.1 us -> 7.1 us  [body(): lax.all_to_all(grad_mid_columns, 'cell', split_axis=0, concat_axis=1, til...]
    all_to_all x0 -> x1, starting transfers between devices: none -> 5.5 us  [pair_then_exchange(): lax.all_to_all(summed, axis_name, split_axis=0, concat_axis=0, axis_index...]
    unnamed x82 -> x52, local copies, waits for them, and re-layouts: 11.5 us -> 6.61 us
    dot_general x2, matrix products: 7.42 us -> 10.8 us  [weight_term(): jnp.einsum(cell_form + ',tbhle->dthe', normed, grad_projected, preferred_...]
    dot_general x6, matrix products: 11 us -> 7.75 us  [attend_heads(): jnp.einsum('bhle,bhme->bhlm', queries, keys_part, preferred_element_type=...]
  transfers between devices with their start and end apart: 4 -> 5, of which waited for: 4 -> 4; matrix products, arithmetic and copies ran while one was open for 19% -> 25% of each run, Pallas kernels for 0% -> 0%
where the time goes in v2:
time: 244 us; the launch traced here: 243 us
  waiting for transfers between devices  92 us (38%)
  matrix products  55.3 us (23%)
  local copies, waits for them, and re-layouts  37 us (15%)
  other arithmetic  25.4 us (10%)
  starting transfers between devices  18.9 us (8%)
  between operations  14.5 us (6%)
    all_to_all x1, waiting for transfers between devices, pair_then_exchange(): lax.all_to_all(summed, axis_name, split_axis=0, concat_axis=0, axis_index...  65 us
    reduce_scatter x1, waiting for transfers between devices, body(): lax.psum_scatter(row_term.astype(jnp.bfloat16), 'cell', scatter_dimension...  14.9 us
    dot_general x2, matrix products, weight_term(): jnp.einsum(cell_form + ',tbhle->dthe', normed, grad_projected, preferred_...  10.8 us
    dot_general x2, matrix products, forward(): jnp.einsum(cell_form + ',dthe->tbhle', normed, projection, preferred_elem...  10.4 us
    dot_general x2, matrix products, backward(): jnp.einsum('tbhle,dthe->' + cell_form, grad_projected, projection, prefer...  10.3 us
    slice x6, local copies, waits for them, and re-layouts, split_weight(): weight[:, :3 * model_width].reshape(model_width, 3, HEADS, head_size)  10.1 us
    dot_general x6, matrix products, attend_heads(): jnp.einsum('bhle,bhme->bhlm', queries, keys_part, preferred_element_type=...  7.75 us
    sub x2, other arithmetic, attend_heads(): weights = jax.nn.softmax(scores, axis=-1).astype(jnp.bfloat16)  7.69 us
  transfers between devices with their start and end apart: 5, of which 4 were waited for; matrix products, arithmetic and copies ran while one was open for 25% of the time, Pallas kernels for 0%

profile of v2, /device:TPU:0, one launch (start us, length us, event | category | flops | bytes accessed | tf_op | source)
XLA Modules:
  0.0 243.0 jit_solution(5556671721840393663)
XLA Ops:
  7.2 2.4 slice.44
  9.5 1.1 copy-done.5
  11.8 3.6 %copy.139 = bf16[768,2304]{0,1:T(8,128)(2,1)} copy(bf16[768,2304]{1,0:T(8,128)(2,1)S(1)} %slice-done.2) | data formatting | bytes 7077888 | tf_op jit(solution)/shard_map/slice | solution.py:33
  15.4 5.8 %convert_bitcast_fusion = bf16[3,8,12,64,64]{4,3,2,0,1:T(8,128)(2,1)S(1)} fusion(bf16[768,3,12,64,1]{0,3,2,1,4:T(8,128)(2,1)} %bitcast.205, bf16[8,64,768]{2,1,0:T(8,128)(2,1)} %param.4, f32[8,64]{1,0:T(8,128)S(1)} %fusion.71), kind=kOutput, calls=%fused_computation.10 | convolution fusion | flops 1814298624 | bytes 6686720 | tf_op jit(solution)/shard_map/bld,dthe->tbhle/dot_general | solution.py:43
  22.2 4.7 %fusion.83 = (f32[8,12,64]{2,1,0:T(8,128)S(1)}, f32[8,12,64,64]{2,3,1,0:T(8,128)S(1)}) fusion(f32[8,12,64,64]{2,3,1,0:T(8,128)S(1)} %fusion.44), kind=kOutput, calls=%fused_computation.127 | output fusion | flops 1572927 | bytes 3170304 | tf_op jit(solution)/shard_map/sub | solution.py:21
  28.6 1.2 copy-done.13
  30.6 1.3 copy.141
  31.9 7.4 %all-to-all-start = ((bf16[8,64,768]{2,0,1:T(8,128)(2,1)}), bf16[8,64,768]{2,0,1:T(8,128)(2,1)}, u32[]{:S(2)}, u32[]{:S(2)}) async-start(bf16[8,64,768]{2,0,1:T(8,128)(2,1)} %copy.141), calls=%async_computation | async-start | bytes 1572864 | tf_op jit(solution)/shard_map/all_to_all | solution.py:105
  39.4 2.0 slice-done.1
  41.4 3.7 %copy.146 = bf16[768,2304]{0,1:T(8,128)(2,1)} copy(bf16[768,2304]{1,0:T(8,128)(2,1)S(1)} %slice-done.1) | data formatting | bytes 7077888 | tf_op jit(solution)/shard_map/slice | solution.py:33
  45.0 2.5 %copy.158 = bf16[12,64,8,64]{1,0,3,2:T(8,128)(2,1)S(1)} copy(bf16[12,64,8,64]{1,3,0,2:T(8,128)(2,1)} %bitcast.212) | data formatting | bytes 1572864 | tf_op jit(solution)/shard_map/convert_element_type | solution.py:23
  47.5 2.0 dot_general.96
  50.2 2.8 %fusion.48 = bf16[4,12,128,64]{2,3,0,1:T(8,128)(2,1)} fusion(bf16[12,64,768,1]{2,1,3,0:T(8,128)(2,1)S(1)} %bitcast.200, bf16[128,4,768]{2,1,0:T(4,128)(2,1)} %param.5), kind=kOutput, calls=%fused_computation.90 | convolution fusion | flops 604372992 | bytes 2752512 | tf_op jit(solution)/shard_map/lbf,hef->bhle/dot_general | solution.py:60
  53.1 5.1 %all-to-all-done = bf16[8,64,768]{2,0,1:T(8,128)(2,1)} async-done(((bf16[8,64,768]{2,0,1:T(8,128)(2,1)}), bf16[8,64,768]{2,0,1:T(8,128)(2,1)}, u32[]{:S(2)}, u32[]{:S(2)}) %all-to-all-start) | async-done | bytes 786464 | tf_op jit(solution)/shard_map/all_to_all | solution.py:105
  58.1 1.4 multiply_reduce_fusion.2
  59.7 4.6 %convert_bitcast_fusion.1 = bf16[3,4,12,128,64]{3,4,2,0,1:T(8,128)(2,1)S(1)} fusion(bf16[768,3,12,64,1]{0,3,2,1,4:T(8,128)(2,1)} %bitcast.207, f32[16,8,4]{1,2,0:T(4,128)S(1)} %copy.144, bf16[8,64,768]{2,0,1:T(8,128)(2,1)} %all-to-all-done), kind=kOutput, calls=%fused_computation.44 | convolution fusion | flops 1814298624 | bytes 6686720 | tf_op jit(solution)/shard_map/lbd,dthe->tbhle/dot_general | solution.py:43
  64.9 3.0 %fusion.84 = (f32[4,12,128]{2,1,0:T(8,128)S(1)}, f32[4,12,128,128]{2,3,1,0:T(8,128)S(1)}) fusion(f32[4,12,128,128]{2,3,1,0:T(8,128)S(1)} %fusion.64), kind=kOutput, calls=%fused_computation.128 | output fusion | flops 3145855 | bytes 6316032 | tf_op jit(solution)/shard_map/jvp()/sub | solution.py:21
  68.0 1.1 fusion.7
  69.1 1.2 fusion.50
  71.2 2.3 fusion.47
  73.8 1.9 copy.161
  75.7 1.0 copy-done.4
  76.7 3.4 %fusion.32 = (f32[128,4]{0,1:T(4,128)S(1)}, f32[4,128,768,1,1]{2,1,3,0,4:T(8,128)S(1)}) fusion(bf16[768,3,12,64,1]{0,3,2,4,1:T(8,128)(2,1)S(1)} %bitcast.208, bf16[1,4,12,128,64]{3,4,2,1,0:T(8,128)(2,1)S(1)} %fusion.47, bf16[1,4,12,128,64]{3,4,2,1,0:T(8,128)(2,1)S(1)} %fusion.50, bf16[1,4,12,128,64]{3,4,2,1,0:T(8,128)(2,1)S(1)} %fusion.49, ...), kind=kOutput, calls=%fused_computation.71 | convolution fusion | flops 1815477760 | bytes 8259584 | tf_op jit(solution)/shard_map/tbhle,dthe->lbd/dot_general | solution.py:65
  80.1 1.5 fusion.21
  81.6 1.5 copy.154
  83.1 5.5 %all-to-all-start.1 = ((bf16[128,4,768]{2,1,0:T(4,128)(2,1)}), bf16[128,4,768]{2,1,0:T(4,128)(2,1)S(1)}, u32[]{:S(2)}, u32[]{:S(2)}) async-start(bf16[128,4,768]{2,1,0:T(4,128)(2,1)} %copy.154), calls=%async_computation.1 | async-start | bytes 1572864 | tf_op jit(solution)/shard_map/all_to_all | solution.py:110
  88.7 3.4 %bitcast_convert_fusion.2 = bf16[12,64,768]{2,1,0:T(8,128)(2,1)} fusion(bf16[4,12,128,128]{2,3,1,0:T(8,128)(2,1)S(1)} %get-tuple-element.4, bf16[128,4,768]{2,1,0:T(4,128)(2,1)S(1)} %copy-done.17, bf16[3,4,12,128,64]{3,4,2,0,1:T(8,128)(2,1)} %copy-done.15), kind=kOutput, calls=%fused_computation.41 | convolution fusion | flops 705626112 | bytes 4325376 | tf_op jit(solution)/shard_map/bhle,lbf->hef/dot_general | solution.py:79
  92.0 4.2 %bitcast_convert_fusion.1 = bf16[768,2304]{1,0:T(8,128)(2,1)S(1)} fusion(bf16[2304,4,128]{2,0,1:T(8,128)(2,1)} %bitcast.211, f32[128,4]{0,1:T(4,128)S(1)} %get-tuple-element.7, bf16[8,64,768]{2,0,1:T(8,128)(2,1)} %all-to-all-done), kind=kOutput, calls=%fused_computation.3 | convolution fusion | flops 1814888448 | bytes 6686720 | tf_op jit(solution)/shard_map/lbd,tbhle->dthe/dot_general | solution.py:76
  96.9 1.7 dynamic-slice_bitcast_fusion
  98.6 1.2 copy-done
  100.2 7.1 %all-to-all-done.1 = bf16[128,4,768]{2,1,0:T(4,128)(2,1)S(1)} async-done(((bf16[128,4,768]{2,1,0:T(4,128)(2,1)}), bf16[128,4,768]{2,1,0:T(4,128)(2,1)S(1)}, u32[]{:S(2)}, u32[]{:S(2)}) %all-to-all-start.1) | async-done | bytes 786464 | tf_op jit(solution)/shard_map/all_to_all | solution.py:110
  108.6 1.4 convolution_convert_fusion
  110.5 1.7 fusion.38
  112.2 1.0 fusion.12
  113.2 2.0 fusion.37
  115.2 2.2 fusion.36
  118.2 1.7 copy.160
  120.0 6.5 %bitcast_convert_fusion = bf16[768,3,12,64]{0,3,2,1:T(8,128)(2,1)} fusion(bf16[1,8,12,64,64]{4,3,2,1,0:T(8,128)(2,1)} %fusion.38, bf16[1,8,12,64,64]{4,3,2,1,0:T(8,128)(2,1)} %fusion.37, bf16[1,8,12,64,64]{4,3,2,1,0:T(8,128)(2,1)} %fusion.36, bf16[8,64,768]{2,1,0:T(8,128)(2,1)S(1)} %copy-done.7, f32[8,64]{1,0:T(8,128)S(1)} %fusion.71), kind=kOutput, calls=%fused_computation.2 | convolution fusion | flops 1821966336 | bytes 6686720 | tf_op jit(solution)/shard_map/bld,tbhle->dthe/dot_general | solution.py:76
  126.5 4.3 %copy.159 = bf16[768,2304]{1,0:T(8,128)(2,1)S(1)} copy(bf16[768,2304]{0,1:T(8,128)(2,1)} %bitcast.209) | data formatting | bytes 7077888 | tf_op jit(solution)/shard_map/reshape | solution.py:78
  130.8 4.0 %pad_maximum_fusion.1 = bf16[768,3072]{1,0:T(8,128)(2,1)} fusion(bf16[768,768]{1,0:T(8,128)(2,1)} %copy.160, bf16[768,2304]{1,0:T(8,128)(2,1)S(1)} %copy.159), kind=kLoop, calls=%fused_computation.5 | loop fusion | flops 9437184 | bytes 9437184 | tf_op jit(solution)/shard_map/concatenate | solution.py:82
  134.9 4.7 %fusion.2 = bf16[8,48,3072]{2,1,0:T(8,128)(2,1)} fusion(bf16[8,48,3072]{2,1,0:T(8,128)(2,1)} %collective-permute-done, bf16[8,2,48,3072]{3,2,1,0:T(8,128)(2,1)} %bitcast.199, s32[]{:T(128)S(6)} %select_n.7), kind=kLoop, calls=%fused_computation.8 | loop fusion | flops 4718592 | bytes 7077892 | tf_op jit(solution)/shard_map/convert_element_type | solution.py:95
  139.6 5.5 %all-to-all-start.2 = ((bf16[8,48,3072]{2,1,0:T(8,128)(2,1)}), bf16[8,48,3072]{2,1,0:T(8,128)(2,1)S(1)}, u32[]{:S(2)}, u32[]{:S(2)}) async-start(bf16[8,48,3072]{2,1,0:T(8,128)(2,1)} %fusion.2), calls=%async_computation.3 | async-start | bytes 4718592 | tf_op jit(solution)/shard_map/all_to_all | solution.py:97
  145.1 6.9 %fusion.27 = (f32[8,64]{1,0:T(8,128)S(1)}, f32[8,64,768,1,1]{2,1,3,0,4:T(8,128)S(1)}) fusion(bf16[8,64,768]{2,1,0:T(8,128)(2,1)S(1)} %copy-done.8, bf16[768,3,12,64,1]{0,3,2,4,1:T(8,128)(2,1)} %bitcast.206, bf16[1,8,12,64,64]{4,3,2,1,0:T(8,128)(2,1)} %fusion.38, bf16[1,8,12,64,64]{4,3,2,1,0:T(8,128)(2,1)} %fusion.37, bf16[1,8,12,64,64]{4,3,2,1,0:T(8,128)(2,1)} %fusion.36), kind=kOutput, calls=%fused_computation.60 | convolution fusion | flops 1815477760 | bytes 8259584 | tf_op jit(solution)/shard_map/tbhle,dthe->bld/dot_general | solution.py:65
  152.0 1.3 fusion.23
  153.4 65.0 %all-to-all-done.2 = bf16[8,48,3072]{2,1,0:T(8,128)(2,1)S(1)} async-done(((bf16[8,48,3072]{2,1,0:T(8,128)(2,1)}), bf16[8,48,3072]{2,1,0:T(8,128)(2,1)S(1)}, u32[]{:S(2)}, u32[]{:S(2)}) %all-to-all-start.2) | async-done | bytes 2359328 | tf_op jit(solution)/shard_map/all_to_all | solution.py:97
  218.3 1.1 convert_reduce_fusion
  219.5 14.9 %reduce-scatter.2.cloned.1.call-done = bf16[48,3072]{1,0:T(8,128)(2,1)} async-done(((bf16[768,3072]{1,0:T(8,128)(2,1)}), bf16[48,3072]{1,0:T(8,128)(2,1)}) %reduce-scatter.2.cloned.1.call-update) | async-done | bytes 294928 | tf_op jit(solution)/shard_map/reduce_scatter | solution.py:113
  234.4 1.8 convert_element_type.177
  (82 shorter events, 11.1 us)
Async XLA Ops:
  9.5 1.1 copy-start.5
  9.5 2.2 slice-start.2
  21.2 5.6 %copy-start.3 = (bf16[3,8,12,64,64]{4,3,2,0,1:T(8,128)(2,1)}, bf16[3,8,12,64,64]{4,3,2,0,1:T(8,128)(2,1)S(1)}, u32[]{:S(2)}) copy-start(bf16[3,8,12,64,64]{4,3,2,0,1:T(8,128)(2,1)S(1)} %convert_bitcast_fusion) | copy-start | bytes 7077892
  26.8 1.6 copy-start.1
  26.8 1.7 copy-start.20
  26.9 1.7 copy-start.6
  26.9 2.9 %copy-start.13 = (bf16[768,768]{1,0:T(8,128)(2,1)S(1)}, bf16[768,768]{1,0:T(8,128)(2,1)}, u32[]{:S(2)}) copy-start(bf16[768,768]{1,0:T(8,128)(2,1)} %slice.44) | copy-start | bytes 3538948
  28.5 2.1 copy-start.11
  31.9 26.2 %all-to-all-start = ((bf16[8,64,768]{2,0,1:T(8,128)(2,1)}), bf16[8,64,768]{2,0,1:T(8,128)(2,1)}, u32[]{:S(2)}, u32[]{:S(2)}) async-start(bf16[8,64,768]{2,0,1:T(8,128)(2,1)} %copy.141), calls=%async_computation | async-start | bytes 1572864 | tf_op jit(solution)/shard_map/all_to_all | solution.py:105
  39.4 2.0 slice-start.1
  47.5 2.1 copy-start.21
  47.5 2.7 %slice-start = ((bf16[768,3072]{1,0:T(8,128)(2,1)}), bf16[768,768]{1,0:T(8,128)(2,1)S(1)}, s32[]{:S(2)}) async-start(bf16[768,3072]{1,0:T(8,128)(2,1)} %param.7), calls=%async_computation.5 | async-start | bytes 2359296 | tf_op jit(solution)/shard_map/slice | solution.py:34
  64.3 6.0 %copy-start.15 = (bf16[3,4,12,128,64]{3,4,2,0,1:T(8,128)(2,1)}, bf16[3,4,12,128,64]{3,4,2,0,1:T(8,128)(2,1)S(1)}, u32[]{:S(2)}) copy-start(bf16[3,4,12,128,64]{3,4,2,0,1:T(8,128)(2,1)S(1)} %convert_bitcast_fusion.1) | copy-start | bytes 7077892
  64.9 3.1 %copy-start.19 = (bf16[4,12,128,64]{2,3,0,1:T(8,128)(2,1)S(1)}, bf16[4,12,128,64]{2,3,0,1:T(8,128)(2,1)}, u32[]{:S(2)}) copy-start(bf16[4,12,128,64]{2,3,0,1:T(8,128)(2,1)} %fusion.48) | copy-start | bytes 2359300
  73.8 2.9 %copy-start.4 = (bf16[768,2304]{0,1:T(8,128)(2,1)S(1)}, bf16[768,2304]{0,1:T(8,128)(2,1)}, u32[]{:S(2)}) copy-start(bf16[768,2304]{0,1:T(8,128)(2,1)} %copy.146) | copy-start | bytes 10616836
  76.6 3.4 %copy-start.16 = (bf16[128,4,768]{2,1,0:T(4,128)(2,1)S(1)}, bf16[128,4,768]{2,1,0:T(4,128)(2,1)}, u32[]{:S(2)}) copy-start(bf16[128,4,768]{2,1,0:T(4,128)(2,1)} %param.5) | copy-start | bytes 2359300
  81.6 7.0 %copy-start.17 = (bf16[128,4,768]{2,1,0:T(4,128)(2,1)S(1)}, bf16[128,4,768]{2,1,0:T(4,128)(2,1)}, u32[]{:S(2)}) copy-start(bf16[128,4,768]{2,1,0:T(4,128)(2,1)} %param.5) | copy-start | bytes 2359300
  83.1 24.2 %all-to-all-start.1 = ((bf16[128,4,768]{2,1,0:T(4,128)(2,1)}), bf16[128,4,768]{2,1,0:T(4,128)(2,1)S(1)}, u32[]{:S(2)}, u32[]{:S(2)}) async-start(bf16[128,4,768]{2,1,0:T(4,128)(2,1)} %copy.154), calls=%async_computation.1 | async-start | bytes 1572864 | tf_op jit(solution)/shard_map/all_to_all | solution.py:110
  88.6 145.8 %reduce-scatter.2.cloned.1.call-start = ((), (), s32[]{:S(2)}) async-start(), calls=%async_computation.4 | async-start | bytes 5013504 | tf_op jit(solution)/shard_map/reduce_scatter | solution.py:113
  92.0 4.2 %copy-start.12 = (bf16[12,64,768]{2,1,0:T(8,128)(2,1)S(1)}, bf16[12,64,768]{2,1,0:T(8,128)(2,1)}, u32[]{:S(2)}) copy-start(bf16[12,64,768]{2,1,0:T(8,128)(2,1)} %bitcast_convert_fusion.2) | copy-start | bytes 3538948
  96.9 2.9 %copy-start = (bf16[768,3072]{1,0:T(8,128)(2,1)}, bf16[768,3072]{1,0:T(8,128)(2,1)S(1)}, u32[]{:S(2)}) copy-start(bf16[768,3072]{1,0:T(8,128)(2,1)S(1)} %pad_maximum_fusion.2) | copy-start | bytes 14155780
  99.8 35.1 %collective-permute-start = (bf16[8,48,3072]{2,1,0:T(8,128)(2,1)}, bf16[8,48,3072]{2,1,0:T(8,128)(2,1)}, u32[]{:S(2)}, u32[]{:S(2)}) collective-permute-start(bf16[8,48,3072]{2,1,0:T(8,128)(2,1)} %dynamic-slice_bitcast_fusion), channel_id=1, source_target_pairs={{0,1},{1,0},{2,3},{3,2},{4,5},{5,4},{6,7},{7,6},{8,9},{9,8},{10,11... | collective-permute-start | bytes 7077896 | tf_op jit(solution)/shard_map/ppermute | solution.py:94
  107.3 1.3 copy-start.14
  107.8 9.6 %copy-start.9 = (bf16[8,64,768]{2,1,0:T(8,128)(2,1)}, bf16[8,64,768]{2,1,0:T(8,128)(2,1)S(1)}, u32[]{:S(2)}) copy-start(bf16[8,64,768]{2,1,0:T(8,128)(2,1)S(1)} %all_to_all.27) | copy-start | bytes 2359300
  108.6 1.9 copy-start.2
  108.6 1.9 copy-start.22
  108.6 3.6 %slice-start.3 = ((s8[4718592]{0:T(1024)(128)(4,1)}), s8[4194304]{0:T(1024)(128)(4,1)S(1)}, s32[]{:S(2)}) async-start(s8[4718592]{0:T(1024)(128)(4,1)} %bitcast.203), calls=%async_computation.8 | async-start | bytes 8388608
  110.5 1.7 slice-start.4
  110.5 1.7 copy-start.23
  115.2 2.2 copy-start.18
  117.4 2.6 %copy-start.7 = (bf16[8,64,768]{2,1,0:T(8,128)(2,1)S(1)}, bf16[8,64,768]{2,1,0:T(8,128)(2,1)}, u32[]{:S(2)}) copy-start(bf16[8,64,768]{2,1,0:T(8,128)(2,1)} %param.4) | copy-start | bytes 2359300
  139.6 5.5 %copy-start.8 = (bf16[8,64,768]{2,1,0:T(8,128)(2,1)S(1)}, bf16[8,64,768]{2,1,0:T(8,128)(2,1)}, u32[]{:S(2)}) copy-start(bf16[8,64,768]{2,1,0:T(8,128)(2,1)} %param.4) | copy-start | bytes 2359300
  139.6 78.8 %all-to-all-start.2 = ((bf16[8,48,3072]{2,1,0:T(8,128)(2,1)}), bf16[8,48,3072]{2,1,0:T(8,128)(2,1)S(1)}, u32[]{:S(2)}, u32[]{:S(2)}) async-start(bf16[8,48,3072]{2,1,0:T(8,128)(2,1)} %fusion.2), calls=%async_computation.3 | async-start | bytes 4718592 | tf_op jit(solution)/shard_map/all_to_all | solution.py:97
  145.1 7.0 %copy-start.10 = (bf16[8,64,768]{2,1,0:T(8,128)(2,1)S(1)}, bf16[8,64,768]{2,1,0:T(8,128)(2,1)}, u32[]{:S(2)}) copy-start(bf16[8,64,768]{2,1,0:T(8,128)(2,1)} %copy-done.9) | copy-start | bytes 2359300
Sparse Core Ops, SparseCore 0:
  135.0 99.3 reduce-scatter.1

commit v3 on v2

--- a/solution.py
+++ b/solution.py
@@ -82,7 +82,7 @@
     return jnp.concatenate([first, second], axis=1)
 
 
-def pair_then_exchange(term, axis_name):
+def pair_presum(term, axis_name):
     count = lax.axis_size(axis_name)
     block = term.shape[0] // count
     index = lax.axis_index(axis_name)
@@ -92,7 +92,11 @@
     keep = lax.dynamic_index_in_dim(pairs, mine, axis=1, keepdims=False)
     send = lax.dynamic_index_in_dim(pairs, 1 - mine, axis=1, keepdims=False)
     received = lax.ppermute(send, axis_name, perm=[(i, i ^ 1) for i in range(count)])
-    summed = (keep.astype(jnp.float32) + received.astype(jnp.float32)).astype(jnp.bfloat16)
+    return (keep.astype(jnp.float32) + received.astype(jnp.float32)).astype(jnp.bfloat16)
+
+
+def exchange_blocks(summed, axis_name):
+    count = lax.axis_size(axis_name)
     groups = [list(range(low, count, 2)) for low in range(2)]
     gathered = lax.all_to_all(
         summed, axis_name, split_axis=0, concat_axis=0, axis_index_groups=groups, tiled=True
@@ -106,13 +110,13 @@
     col_saved = forward(mid_columns, col_weight, 0, False)
     grad_mid_columns, grad_col_proj = backward(col_saved, col_weight, cotangent, 0)
     col_term = weight_term(col_saved[1], grad_col_proj, col_saved[3], cotangent, 0)
-    col_grad = pair_then_exchange(col_term, "cell")
+    col_summed = pair_presum(col_term, "cell")
     grad_mid = lax.all_to_all(grad_mid_columns, "cell", split_axis=0, concat_axis=1, tiled=True)
+    col_summed, grad_mid = lax.optimization_barrier((col_summed, grad_mid))
+    col_grad = exchange_blocks(col_summed, "cell")
     grad_cells, grad_row_proj = backward(row_saved, row_weight, grad_mid, 1)
     row_term = weight_term(row_saved[1], grad_row_proj, row_saved[3], grad_mid, 1)
-    row_grad = lax.psum_scatter(
-        row_term.astype(jnp.bfloat16), "cell", scatter_dimension=0, tiled=True
-    ).astype(jnp.float32)
+    row_grad = exchange_blocks(pair_presum(row_term, "cell"), "cell")
     return (grad_cells, row_grad, col_grad)
 
 

time: 244 us -> 261 us (1.070)
  waiting for transfers between devices: 92 us -> 107 us
  between operations: 14.5 us -> 1.15 us
  matrix products: 55.3 us -> 61.2 us
  other arithmetic: 25.4 us -> 30.8 us
  starting transfers between devices: 18.9 us -> 22.7 us
    reduce_scatter x1 -> x0, waiting for transfers between devices: 14.9 us -> none  [body(): lax.psum_scatter(row_term.astype(jnp.bfloat16), 'cell', scatter_dimension...]
    all_to_all x1, waiting for transfers between devices: 7.1 us -> 18.7 us  [body(): lax.all_to_all(grad_mid_columns, 'cell', split_axis=0, concat_axis=1, til...]
    all_to_all x1 -> x2, waiting for transfers between devices: 65 us -> 76.1 us  [exchange_blocks(): lax.all_to_all(summed, axis_name, split_axis=0, concat_axis=0, axis_index...]
    dot_general x6, matrix products: 7.75 us -> 13.4 us  [attend_heads(): jnp.einsum('bhle,bhme->bhlm', queries, keys_part, preferred_element_type=...]
    ppermute x1 -> x2, waiting for transfers between devices: 0.01 us -> 4.52 us  [pair_presum(): lax.ppermute(send, axis_name, perm=[(i, i ^ 1) for i in range(count)])]
    all_to_all x1 -> x2, starting transfers between devices: 5.5 us -> 9.38 us  [exchange_blocks(): lax.all_to_all(summed, axis_name, split_axis=0, concat_axis=0, axis_index...]
    reduce_sum x1 -> x2, other arithmetic: 1.15 us -> 4.01 us  [exchange_blocks(): return jnp.sum(gathered.astype(jnp.float32), axis=0)]
    unnamed x52 -> x74, local copies, waits for them, and re-layouts: 6.61 us -> 8.9 us
  transfers between devices with their start and end apart: 5 -> 6, of which waited for: 4 -> 5; matrix products, arithmetic and copies ran while one was open for 25% -> 15% of each run, Pallas kernels for 0% -> 0%
where the time goes in v3:
time: 261 us; the launch traced here: 260 us
  waiting for transfers between devices  107 us (41%)
  matrix products  61.2 us (23%)
  local copies, waits for them, and re-layouts  37.5 us (14%)
  other arithmetic  30.8 us (12%)
  starting transfers between devices  22.7 us (9%)
    all_to_all x2, waiting for transfers between devices, exchange_blocks(): lax.all_to_all(summed, axis_name, split_axis=0, concat_axis=0, axis_index...  76.1 us
    all_to_all x1, waiting for transfers between devices, body(): lax.all_to_all(grad_mid_columns, 'cell', split_axis=0, concat_axis=1, til...  18.7 us
    dot_general x6, matrix products, attend_heads(): jnp.einsum('bhle,bhme->bhlm', queries, keys_part, preferred_element_type=...  13.4 us
    dot_general x2, matrix products, backward(): jnp.einsum('tbhle,dthe->' + cell_form, grad_projected, projection, prefer...  9.87 us
    dot_general x2, matrix products, weight_term(): jnp.einsum(cell_form + ',tbhle->dthe', normed, grad_projected, preferred_...  9.64 us
    slice x6, local copies, waits for them, and re-layouts, split_weight(): weight[:, :3 * model_width].reshape(model_width, 3, HEADS, head_size)  9.52 us
    dot_general x2, matrix products, forward(): jnp.einsum(cell_form + ',dthe->tbhle', normed, projection, preferred_elem...  9.46 us
    all_to_all x2, starting transfers between devices, exchange_blocks(): lax.all_to_all(summed, axis_name, split_axis=0, concat_axis=0, axis_index...  9.38 us
  transfers between devices with their start and end apart: 6, of which 5 were waited for; matrix products, arithmetic and copies ran while one was open for 15% of the time, Pallas kernels for 0%

profile of v3, /device:TPU:0, one launch (start us, length us, event | category | flops | bytes accessed | tf_op | source)
XLA Modules:
  0.0 259.9 jit_solution(11718794099460534384)
XLA Ops:
  0.6 2.4 slice.43
  5.3 3.6 %copy.133 = bf16[768,2304]{0,1:T(8,128)(2,1)} copy(bf16[768,2304]{1,0:T(8,128)(2,1)S(1)} %slice-done.1) | data formatting | bytes 7077888 | tf_op jit(solution)/shard_map/slice | solution.py:33
  8.9 5.8 %convert_bitcast_fusion = bf16[3,8,12,64,64]{4,3,2,0,1:T(8,128)(2,1)S(1)} fusion(bf16[768,3,12,64,1]{0,3,2,1,4:T(8,128)(2,1)} %bitcast.212, bf16[8,64,768]{2,1,0:T(8,128)(2,1)} %param.4, f32[8,64]{1,0:T(8,128)S(1)} %fusion.73), kind=kOutput, calls=%fused_computation.13 | convolution fusion | flops 1814298624 | bytes 6686720 | tf_op jit(solution)/shard_map/bld,dthe->tbhle/dot_general | solution.py:43
  15.7 4.7 %fusion.84 = (f32[8,12,64]{2,1,0:T(8,128)S(1)}, f32[8,12,64,64]{2,3,1,0:T(8,128)S(1)}) fusion(f32[8,12,64,64]{2,3,1,0:T(8,128)S(1)} %fusion.45), kind=kOutput, calls=%fused_computation.131 | output fusion | flops 1572927 | bytes 3170304 | tf_op jit(solution)/shard_map/sub | solution.py:21
  24.1 1.3 copy.135
  25.4 7.4 %all-to-all-start = ((bf16[8,64,768]{2,0,1:T(8,128)(2,1)}), bf16[8,64,768]{2,0,1:T(8,128)(2,1)}, u32[]{:S(2)}, u32[]{:S(2)}) async-start(bf16[8,64,768]{2,0,1:T(8,128)(2,1)} %copy.135), calls=%async_computation | async-start | bytes 1572864 | tf_op jit(solution)/shard_map/all_to_all | solution.py:109
  32.9 2.5 slice.44
  35.3 2.0 slice-done
  37.3 3.6 %copy.143 = bf16[768,2304]{0,1:T(8,128)(2,1)} copy(bf16[768,2304]{1,0:T(8,128)(2,1)S(1)} %slice-done) | data formatting | bytes 7077888 | tf_op jit(solution)/shard_map/slice | solution.py:33
  41.0 3.3 %fusion.49 = bf16[4,12,128,64]{2,3,0,1:T(8,128)(2,1)} fusion(bf16[12,64,768,1]{2,1,3,0:T(8,128)(2,1)} %bitcast.223, bf16[128,4,768]{2,1,0:T(4,128)(2,1)} %param.5), kind=kOutput, calls=%fused_computation.94 | convolution fusion | flops 604372992 | bytes 2752512 | tf_op jit(solution)/shard_map/lbf,hef->bhle/dot_general | solution.py:60
  44.3 7.3 %all-to-all-done = bf16[8,64,768]{2,0,1:T(8,128)(2,1)} async-done(((bf16[8,64,768]{2,0,1:T(8,128)(2,1)}), bf16[8,64,768]{2,0,1:T(8,128)(2,1)}, u32[]{:S(2)}, u32[]{:S(2)}) %all-to-all-start) | async-done | bytes 786464 | tf_op jit(solution)/shard_map/all_to_all | solution.py:109
  51.6 2.0 multiply_reduce_fusion.2
  53.6 1.4 copy.138
  55.0 1.3 multiply_add_fusion
  56.4 1.4 copy.141
  57.8 3.6 %convert_bitcast_fusion.1 = bf16[3,4,12,128,64]{3,4,2,0,1:T(8,128)(2,1)S(1)} fusion(bf16[768,3,12,64,1]{0,3,2,1,4:T(8,128)(2,1)S(1)} %bitcast.214, f32[16,8,4]{1,2,0:T(4,128)} %copy.141, bf16[8,64,768]{2,0,1:T(8,128)(2,1)} %all-to-all-done), kind=kOutput, calls=%fused_computation.48 | convolution fusion | flops 1814298624 | bytes 6686720 | tf_op jit(solution)/shard_map/lbd,dthe->tbhle/dot_general | solution.py:43
  62.1 3.2 %fusion.85 = (f32[4,12,128]{2,1,0:T(8,128)S(1)}, f32[4,12,128,128]{2,3,1,0:T(8,128)S(1)}) fusion(f32[4,12,128,128]{2,3,1,0:T(8,128)S(1)} %fusion.66), kind=kOutput, calls=%fused_computation.132 | output fusion | flops 3145855 | bytes 6316032 | tf_op jit(solution)/shard_map/jvp()/sub | solution.py:21
  65.4 3.0 %fusion.8 = (f32[4,12,128]{2,1,0:T(8,128)}, bf16[4,12,128,128]{2,3,1,0:T(8,128)(2,1)S(1)}, bf16[4,12,128,128]{2,3,1,0:T(8,128)(2,1)}) fusion(f32[4,12,128,128]{2,3,1,0:T(8,128)S(1)} %get-tuple-element.16, f32[4,12,128]{2,1,0:T(8,128)S(1)} %multiply_divide_fusion.1, f32[4,12,128]{2,1,0:T(8,128)S(1)} %get-tuple-element.15, ...), kind=kOutput, calls=%fused_computation.22 | convolution fusion | flops 106162176 | bytes 7954432 | tf_op jit(solution)/shard_map/transpose(jvp(bhlm,bhme->bhle))/dot_general | solution.py:22
  69.5 2.1 fusion.48
  71.5 4.1 %bitcast_convert_fusion.3 = bf16[12,64,768]{2,1,0:T(8,128)(2,1)} fusion(bf16[4,12,128,128]{2,3,1,0:T(8,128)(2,1)} %copy-done.16, bf16[128,4,768]{2,1,0:T(4,128)(2,1)} %param.5, bf16[3,4,12,128,64]{3,4,2,0,1:T(8,128)(2,1)} %copy-done.20), kind=kOutput, calls=%fused_computation.45 | convolution fusion | flops 705626112 | bytes 4325376 | tf_op jit(solution)/shard_map/bhle,lbf->hef/dot_general | solution.py:79
  76.4 4.8 %fusion.51 = bf16[1,4,12,128,64]{3,4,2,1,0:T(8,128)(2,1)} fusion(bf16[3,4,12,128,64]{3,4,2,0,1:T(8,128)(2,1)} %copy-done.20, f32[4,12,128,128]{2,3,1,0:T(8,128)} %copy-done.7, bf16[4,12,128,128]{2,3,1,0:T(8,128)(2,1)} %get-tuple-element.17, f32[4,12,128]{2,1,0:T(8,128)S(1)} %neg.12, f32[4,12,128]{2,1,0:T(8,128)} %copy-done.27), kind=kOutput, calls=%fused_computation.96 | convolution fusion | flops 104988672 | bytes 6348800 | tf_op jit(solution)/shard_map/transpose(jvp(bhle,bhme->bhlm))/dot_general | solution.py:18
  81.2 2.8 %fusion.50 = bf16[1,4,12,128,64]{3,4,2,1,0:T(8,128)(2,1)} fusion(bf16[3,4,12,128,64]{3,4,2,0,1:T(8,128)(2,1)} %copy-done.20, f32[4,12,128,128]{2,3,1,0:T(8,128)S(1)} %copy-done.8, bf16[4,12,128,128]{2,3,1,0:T(8,128)(2,1)S(1)} %copy-done.34, f32[4,12,128]{2,1,0:T(8,128)S(1)} %neg.12, f32[4,12,128]{2,1,0:T(8,128)S(1)} %copy-done.28), kind=kOutput, calls=%fused_computation.95 | convolution fusion | flops 104988672 | bytes 6340608 | tf_op jit(solution)/shard_map/transpose(jvp(bhle,bhme->bhlm))/dot_general | solution.py:18
  85.6 1.9 fusion.53
  89.0 3.3 %fusion.31 = (f32[128,4]{0,1:T(4,128)S(1)}, f32[4,128,768,1,1]{2,1,3,0,4:T(8,128)S(1)}) fusion(bf16[768,3,12,64,1]{0,3,2,4,1:T(8,128)(2,1)S(1)} %bitcast.215, bf16[1,4,12,128,64]{3,4,2,1,0:T(8,128)(2,1)S(1)} %copy-done.9, bf16[1,4,12,128,64]{3,4,2,1,0:T(8,128)(2,1)S(1)} %copy-done.21, bf16[1,4,12,128,64]{3,4,2,1,0:T(8,128)(2,1)S(1)} %copy-done.22, ...), kind=kOutput, calls=%fused_computation.73 | convolution fusion | flops 1815477760 | bytes 8259584 | tf_op jit(solution)/shard_map/tbhle,dthe->lbd/dot_general | solution.py:65
  92.4 3.5 %bitcast_convert_fusion.1 = bf16[768,2304]{1,0:T(8,128)(2,1)S(1)} fusion(bf16[2304,4,128]{2,0,1:T(8,128)(2,1)S(1)} %bitcast.219, f32[128,4]{0,1:T(4,128)S(1)} %get-tuple-element.12, bf16[8,64,768]{2,0,1:T(8,128)(2,1)} %all-to-all-done), kind=kOutput, calls=%fused_computation.3 | convolution fusion | flops 1814888448 | bytes 6686720 | tf_op jit(solution)/shard_map/lbd,tbhle->dthe/dot_general | solution.py:76
  96.5 1.6 dynamic-slice_bitcast_fusion.1
  98.1 1.3 copy-done
  99.7 1.5 fusion.22
  101.2 1.5 copy.155
  102.7 5.5 %all-to-all-start.1 = ((bf16[128,4,768]{2,1,0:T(4,128)(2,1)}), bf16[128,4,768]{2,1,0:T(4,128)(2,1)S(1)}, u32[]{:S(2)}, u32[]{:S(2)}) async-start(bf16[128,4,768]{2,1,0:T(4,128)(2,1)} %copy.155), calls=%async_computation.1 | async-start | bytes 1572864 | tf_op jit(solution)/shard_map/all_to_all | solution.py:114
  108.3 18.7 %all-to-all-done.1 = bf16[128,4,768]{2,1,0:T(4,128)(2,1)S(1)} async-done(((bf16[128,4,768]{2,1,0:T(4,128)(2,1)}), bf16[128,4,768]{2,1,0:T(4,128)(2,1)S(1)}, u32[]{:S(2)}, u32[]{:S(2)}) %all-to-all-start.1) | async-done | bytes 786464 | tf_op jit(solution)/shard_map/all_to_all | solution.py:114
  127.5 5.1 %fusion.3 = bf16[8,48,3072]{2,1,0:T(8,128)(2,1)} fusion(bf16[8,48,3072]{2,1,0:T(8,128)(2,1)} %collective-permute-done, bf16[8,2,48,3072]{3,2,1,0:T(8,128)(2,1)} %bitcast.206, s32[]{:T(128)S(6)} %select_n.9), kind=kLoop, calls=%fused_computation.10 | loop fusion | flops 4718592 | bytes 7077892 | tf_op jit(solution)/shard_map/convert_element_type | solution.py:95
  132.5 1.4 convolution_convert_fusion
  136.9 2.0 fusion.38
  138.9 2.1 fusion.37
  141.1 5.5 %all-to-all-start.3 = ((bf16[8,48,3072]{2,1,0:T(8,128)(2,1)}), bf16[8,48,3072]{2,1,0:T(8,128)(2,1)}, u32[]{:S(2)}, u32[]{:S(2)}) async-start(bf16[8,48,3072]{2,1,0:T(8,128)(2,1)} %fusion.3), calls=%async_computation.3 | async-start | bytes 4718592 | tf_op jit(solution)/shard_map/all_to_all | solution.py:101
  146.6 6.2 %bitcast_convert_fusion = bf16[768,3,12,64]{0,3,2,1:T(8,128)(2,1)} fusion(bf16[1,8,12,64,64]{4,3,2,1,0:T(8,128)(2,1)S(1)} %fusion.39, bf16[1,8,12,64,64]{4,3,2,1,0:T(8,128)(2,1)} %fusion.38, bf16[1,8,12,64,64]{4,3,2,1,0:T(8,128)(2,1)} %fusion.37, bf16[8,64,768]{2,1,0:T(8,128)(2,1)S(1)} %copy-done.12, f32[8,64]{1,0:T(8,128)S(1)} %copy-done.32), kind=kOutput, calls=%fused_computation.2 | convolution fusion | flops 1821966336 | bytes 6686720 | tf_op jit(solution)/shard_map/bld,tbhle->dthe/dot_general | solution.py:76
  152.8 1.8 bitcast_convert_fusion.2
  154.6 4.3 %copy.160 = bf16[768,2304]{1,0:T(8,128)(2,1)S(1)} copy(bf16[768,2304]{0,1:T(8,128)(2,1)} %bitcast.216) | data formatting | bytes 7077888 | tf_op jit(solution)/shard_map/reshape | solution.py:78
  159.0 1.9 pad_maximum_fusion.2
  161.1 4.5 %collective-permute-done.1 = bf16[8,48,3072]{2,1,0:T(8,128)(2,1)S(1)} collective-permute-done((bf16[8,48,3072]{2,1,0:T(8,128)(2,1)S(1)}, bf16[8,48,3072]{2,1,0:T(8,128)(2,1)S(1)}, u32[]{:S(2)}, u32[]{:S(2)}) %collective-permute-start.1) | collective-permute-done | bytes 2359328 | tf_op jit(solution)/shard_map/ppermute | solution.py:94
  165.6 2.3 fusion.2
  167.9 33.1 %all-to-all-done.3 = bf16[8,48,3072]{2,1,0:T(8,128)(2,1)} async-done(((bf16[8,48,3072]{2,1,0:T(8,128)(2,1)}), bf16[8,48,3072]{2,1,0:T(8,128)(2,1)}, u32[]{:S(2)}, u32[]{:S(2)}) %all-to-all-start.3) | async-done | bytes 2359328 | tf_op jit(solution)/shard_map/all_to_all | solution.py:101
  201.0 3.9 %all-to-all-start.2 = ((bf16[8,48,3072]{2,1,0:T(8,128)(2,1)}), bf16[8,48,3072]{2,1,0:T(8,128)(2,1)S(1)}, u32[]{:S(2)}, u32[]{:S(2)}) async-start(bf16[8,48,3072]{2,1,0:T(8,128)(2,1)} %fusion.2), calls=%async_computation.2 | async-start | bytes 4718592 | tf_op jit(solution)/shard_map/all_to_all | solution.py:101
  204.9 6.5 %fusion.28 = (f32[8,64]{1,0:T(8,128)S(1)}, f32[8,64,768,1,1]{2,1,3,0,4:T(8,128)S(1)}) fusion(bf16[8,64,768]{2,1,0:T(8,128)(2,1)S(1)} %copy-done.13, bf16[768,3,12,64,1]{0,3,2,4,1:T(8,128)(2,1)} %bitcast.213, bf16[1,8,12,64,64]{4,3,2,1,0:T(8,128)(2,1)} %copy-done.33, bf16[1,8,12,64,64]{4,3,2,1,0:T(8,128)(2,1)} %fusion.38, bf16[1,8,12,64,64]{4,3,2,1,0:T(8,128)(2,1)} %fusion.37), kind=kOutput, calls=%fused_computation.64 | convolution fusion | flops 1815477760 | bytes 8259584 | tf_op jit(solution)/shard_map/tbhle,dthe->bld/dot_general | solution.py:65
  211.5 1.3 fusion.24
  212.8 2.9 %convert_reduce_fusion = f32[48,3072]{1,0:T(8,128)} fusion(bf16[8,48,3072]{2,1,0:T(8,128)(2,1)} %all-to-all-done.3), kind=kLoop, calls=%fused_computation.11 | loop fusion | flops 2211840 | bytes 2949120 | tf_op jit(solution)/shard_map/reduce_sum | solution.py:104
  215.7 43.1 %all-to-all-done.2 = bf16[8,48,3072]{2,1,0:T(8,128)(2,1)S(1)} async-done(((bf16[8,48,3072]{2,1,0:T(8,128)(2,1)}), bf16[8,48,3072]{2,1,0:T(8,128)(2,1)S(1)}, u32[]{:S(2)}, u32[]{:S(2)}) %all-to-all-start.2) | async-done | bytes 2359328 | tf_op jit(solution)/shard_map/all_to_all | solution.py:101
  (102 shorter events, 18.4 us)
Async XLA Ops:
  3.0 1.1 copy-start.10
  3.0 2.2 slice-start.1
  4.4 0.6 copy-start.29
  5.3 3.6 %copy-start.31 = (f32[8,64]{1,0:T(8,128)}, f32[8,64]{1,0:T(8,128)S(1)}, u32[]{:S(2)}) copy-start(f32[8,64]{1,0:T(8,128)S(1)} %fusion.73) | copy-start | bytes 6148
  14.7 5.6 %copy-start.5 = (bf16[3,8,12,64,64]{4,3,2,0,1:T(8,128)(2,1)}, bf16[3,8,12,64,64]{4,3,2,0,1:T(8,128)(2,1)S(1)}, u32[]{:S(2)}) copy-start(bf16[3,8,12,64,64]{4,3,2,0,1:T(8,128)(2,1)S(1)} %convert_bitcast_fusion) | copy-start | bytes 7077892
  20.3 1.6 copy-start.1
  20.3 1.7 copy-start.25
  20.3 1.7 copy-start.11
  20.4 2.9 %copy-start.18 = (bf16[768,768]{1,0:T(8,128)(2,1)S(1)}, bf16[768,768]{1,0:T(8,128)(2,1)}, u32[]{:S(2)}) copy-start(bf16[768,768]{1,0:T(8,128)(2,1)} %slice.43) | copy-start | bytes 3538948
  22.0 2.1 copy-start.14
  25.4 26.2 %all-to-all-start = ((bf16[8,64,768]{2,0,1:T(8,128)(2,1)}), bf16[8,64,768]{2,0,1:T(8,128)(2,1)}, u32[]{:S(2)}, u32[]{:S(2)}) async-start(bf16[8,64,768]{2,0,1:T(8,128)(2,1)} %copy.135), calls=%async_computation | async-start | bytes 1572864 | tf_op jit(solution)/shard_map/all_to_all | solution.py:109
  35.3 2.0 slice-start
  41.0 16.8 %copy-start.6 = (bf16[768,2304]{0,1:T(8,128)(2,1)S(1)}, bf16[768,2304]{0,1:T(8,128)(2,1)}, u32[]{:S(2)}) copy-start(bf16[768,2304]{0,1:T(8,128)(2,1)} %copy.143) | copy-start | bytes 10616836
  61.4 3.9 %copy-start.20 = (bf16[3,4,12,128,64]{3,4,2,0,1:T(8,128)(2,1)}, bf16[3,4,12,128,64]{3,4,2,0,1:T(8,128)(2,1)S(1)}, u32[]{:S(2)}) copy-start(bf16[3,4,12,128,64]{3,4,2,0,1:T(8,128)(2,1)S(1)} %convert_bitcast_fusion.1) | copy-start | bytes 7077892
  62.1 3.3 %copy-start.24 = (bf16[4,12,128,64]{2,3,0,1:T(8,128)(2,1)S(1)}, bf16[4,12,128,64]{2,3,0,1:T(8,128)(2,1)}, u32[]{:S(2)}) copy-start(bf16[4,12,128,64]{2,3,0,1:T(8,128)(2,1)} %fusion.49) | copy-start | bytes 2359300
  65.3 3.0 %copy-start.7 = (f32[4,12,128,128]{2,3,1,0:T(8,128)}, f32[4,12,128,128]{2,3,1,0:T(8,128)S(1)}, u32[]{:S(2)}) copy-start(f32[4,12,128,128]{2,3,1,0:T(8,128)S(1)} %get-tuple-element.16) | copy-start | bytes 9437188
  65.3 3.0 %copy-start.27 = (f32[4,12,128]{2,1,0:T(8,128)}, f32[4,12,128]{2,1,0:T(8,128)S(1)}, u32[]{:S(2)}) copy-start(f32[4,12,128]{2,1,0:T(8,128)S(1)} %get-tuple-element.15) | copy-start | bytes 73732
  68.3 1.2 copy-start.16
  76.4 4.8 %copy-start.8 = (f32[4,12,128,128]{2,3,1,0:T(8,128)S(1)}, f32[4,12,128,128]{2,3,1,0:T(8,128)}, u32[]{:S(2)}) copy-start(f32[4,12,128,128]{2,3,1,0:T(8,128)} %copy-done.7) | copy-start | bytes 9437188
  76.4 4.8 %copy-start.28 = (f32[4,12,128]{2,1,0:T(8,128)S(1)}, f32[4,12,128]{2,1,0:T(8,128)}, u32[]{:S(2)}) copy-start(f32[4,12,128]{2,1,0:T(8,128)} %copy-done.27) | copy-start | bytes 73732
  76.4 4.8 %copy-start.34 = (bf16[4,12,128,128]{2,3,1,0:T(8,128)(2,1)S(1)}, bf16[4,12,128,128]{2,3,1,0:T(8,128)(2,1)}, u32[]{:S(2)}) copy-start(bf16[4,12,128,128]{2,3,1,0:T(8,128)(2,1)} %get-tuple-element.17) | copy-start | bytes 4718596
  87.4 1.1 copy-start.9
  87.4 1.4 copy-start.21
  87.5 1.6 copy-start.22
  92.4 3.5 %copy-start.17 = (bf16[12,64,768]{2,1,0:T(8,128)(2,1)S(1)}, bf16[12,64,768]{2,1,0:T(8,128)(2,1)}, u32[]{:S(2)}) copy-start(bf16[12,64,768]{2,1,0:T(8,128)(2,1)} %bitcast_convert_fusion.3) | copy-start | bytes 3538948
  96.5 2.9 %copy-start = (bf16[768,3072]{1,0:T(8,128)(2,1)}, bf16[768,3072]{1,0:T(8,128)(2,1)S(1)}, u32[]{:S(2)}) copy-start(bf16[768,3072]{1,0:T(8,128)(2,1)S(1)} %pad_maximum_fusion) | copy-start | bytes 14155780
  96.5 3.2 %copy-start.23 = (bf16[128,4,768]{2,1,0:T(4,128)(2,1)S(1)}, bf16[128,4,768]{2,1,0:T(4,128)(2,1)}, u32[]{:S(2)}) copy-start(bf16[128,4,768]{2,1,0:T(4,128)(2,1)} %param.5) | copy-start | bytes 2359300
  99.4 28.0 %collective-permute-start = (bf16[8,48,3072]{2,1,0:T(8,128)(2,1)}, bf16[8,48,3072]{2,1,0:T(8,128)(2,1)}, u32[]{:S(2)}, u32[]{:S(2)}) collective-permute-start(bf16[8,48,3072]{2,1,0:T(8,128)(2,1)} %dynamic-slice_bitcast_fusion.1), channel_id=1, source_target_pairs={{0,1},{1,0},{2,3},{3,2},{4,5},{5,4},{6,7},{7,6},{8,9},{9,8},{10,11... | collective-permute-start | bytes 7077896 | tf_op jit(solution)/shard_map/ppermute | solution.py:94
  101.2 7.0 %copy-start.26 = (f32[8,12,64]{2,1,0:T(8,128)S(1)}, f32[8,12,64]{2,1,0:T(8,128)}, u32[]{:S(2)}) copy-start(f32[8,12,64]{2,1,0:T(8,128)} %copy-done.25) | copy-start | bytes 73732
  102.7 24.2 %all-to-all-start.1 = ((bf16[128,4,768]{2,1,0:T(4,128)(2,1)}), bf16[128,4,768]{2,1,0:T(4,128)(2,1)S(1)}, u32[]{:S(2)}, u32[]{:S(2)}) async-start(bf16[128,4,768]{2,1,0:T(4,128)(2,1)} %copy.155), calls=%async_computation.1 | async-start | bytes 1572864 | tf_op jit(solution)/shard_map/all_to_all | solution.py:114
  127.4 25.4 %copy-start.3 = (bf16[8,64,768]{2,1,0:T(8,128)(2,1)}, bf16[8,64,768]{2,1,0:T(8,128)(2,1)S(1)}, u32[]{:S(2)}) copy-start(bf16[8,64,768]{2,1,0:T(8,128)(2,1)S(1)} %all_to_all.30) | copy-start | bytes 2359300
  127.4 5.1 %copy-start.19 = (bf16[768,768]{1,0:T(8,128)(2,1)S(1)}, bf16[768,768]{1,0:T(8,128)(2,1)}, u32[]{:S(2)}) copy-start(bf16[768,768]{1,0:T(8,128)(2,1)} %slice.43) | copy-start | bytes 3538948
  132.5 1.9 copy-start.2
  132.5 3.1 %slice-start.2 = ((s8[4718592]{0:T(1024)(128)(4,1)}), s8[4194304]{0:T(1024)(128)(4,1)S(1)}, s32[]{:S(2)}) async-start(s8[4718592]{0:T(1024)(128)(4,1)} %bitcast.210), calls=%async_computation.6 | async-start | bytes 8388608
  134.4 1.5 slice-start.3
  135.9 10.7 %copy-start.33 = (bf16[1,8,12,64,64]{4,3,2,1,0:T(8,128)(2,1)}, bf16[1,8,12,64,64]{4,3,2,1,0:T(8,128)(2,1)S(1)}, u32[]{:S(2)}) copy-start(bf16[1,8,12,64,64]{4,3,2,1,0:T(8,128)(2,1)S(1)} %fusion.39) | copy-start | bytes 2359300
  141.1 5.5 %copy-start.12 = (bf16[8,64,768]{2,1,0:T(8,128)(2,1)S(1)}, bf16[8,64,768]{2,1,0:T(8,128)(2,1)}, u32[]{:S(2)}) copy-start(bf16[8,64,768]{2,1,0:T(8,128)(2,1)} %param.4) | copy-start | bytes 2359300
  141.1 5.5 %copy-start.32 = (f32[8,64]{1,0:T(8,128)S(1)}, f32[8,64]{1,0:T(8,128)}, u32[]{:S(2)}) copy-start(f32[8,64]{1,0:T(8,128)} %copy-done.31) | copy-start | bytes 6148
  141.1 59.9 %all-to-all-start.3 = ((bf16[8,48,3072]{2,1,0:T(8,128)(2,1)}), bf16[8,48,3072]{2,1,0:T(8,128)(2,1)}, u32[]{:S(2)}, u32[]{:S(2)}) async-start(bf16[8,48,3072]{2,1,0:T(8,128)(2,1)} %fusion.3), calls=%async_computation.3 | async-start | bytes 4718592 | tf_op jit(solution)/shard_map/all_to_all | solution.py:101
  146.6 6.2 %copy-start.15 = (bf16[8,12,64,64]{3,2,1,0:T(8,128)(2,1)S(1)}, bf16[8,12,64,64]{3,2,1,0:T(8,128)(2,1)}, u32[]{:S(2)}) copy-start(bf16[8,12,64,64]{3,2,1,0:T(8,128)(2,1)} %copy-done.14) | copy-start | bytes 2359300
  161.0 4.6 %collective-permute-start.1 = (bf16[8,48,3072]{2,1,0:T(8,128)(2,1)S(1)}, bf16[8,48,3072]{2,1,0:T(8,128)(2,1)S(1)}, u32[]{:S(2)}, u32[]{:S(2)}) collective-permute-start(bf16[8,48,3072]{2,1,0:T(8,128)(2,1)S(1)} %dynamic-slice_bitcast_fusion), channel_id=1, source_target_pairs={{0,1},{1,0},{2,3},{3,2},{4,5},{5,4},{6,7},{7,6},{8,9},{9,8},{10,11... | collective-permute-start | bytes 7077896 | tf_op jit(solution)/shard_map/ppermute | solution.py:94
  167.9 37.0 %copy-start.13 = (bf16[8,64,768]{2,1,0:T(8,128)(2,1)S(1)}, bf16[8,64,768]{2,1,0:T(8,128)(2,1)}, u32[]{:S(2)}) copy-start(bf16[8,64,768]{2,1,0:T(8,128)(2,1)} %param.4) | copy-start | bytes 2359300
  201.0 57.8 %all-to-all-start.2 = ((bf16[8,48,3072]{2,1,0:T(8,128)(2,1)}), bf16[8,48,3072]{2,1,0:T(8,128)(2,1)S(1)}, u32[]{:S(2)}, u32[]{:S(2)}) async-start(bf16[8,48,3072]{2,1,0:T(8,128)(2,1)} %fusion.2), calls=%async_computation.2 | async-start | bytes 4718592 | tf_op jit(solution)/shard_map/all_to_all | solution.py:101
  204.9 6.6 %copy-start.30 = (f32[8,64]{1,0:T(8,128)S(1)}, f32[8,64]{1,0:T(8,128)}, u32[]{:S(2)}) copy-start(f32[8,64]{1,0:T(8,128)} %copy-done.29) | copy-start | bytes 6148
  204.9 6.6 %copy-start.4 = (bf16[8,64,768]{2,1,0:T(8,128)(2,1)S(1)}, bf16[8,64,768]{2,1,0:T(8,128)(2,1)}, u32[]{:S(2)}) copy-start(bf16[8,64,768]{2,1,0:T(8,128)(2,1)} %copy-done.3) | copy-start | bytes 2359300

commit v4 on v3

--- a/solution.py
+++ b/solution.py
@@ -88,11 +88,9 @@
     index = lax.axis_index(axis_name)
     sent = lax.optimization_barrier(term.astype(jnp.bfloat16))
     pairs = sent.reshape((count // 2, 2, block) + term.shape[1:])
-    mine = index & 1
-    keep = lax.dynamic_index_in_dim(pairs, mine, axis=1, keepdims=False)
-    send = lax.dynamic_index_in_dim(pairs, 1 - mine, axis=1, keepdims=False)
-    received = lax.ppermute(send, axis_name, perm=[(i, i ^ 1) for i in range(count)])
-    return (keep.astype(jnp.float32) + received.astype(jnp.float32)).astype(jnp.bfloat16)
+    couples = [[low, low + 1] for low in range(0, count, 2)]
+    swapped = lax.all_to_all(pairs, axis_name, split_axis=1, concat_axis=1, axis_index_groups=couples, tiled=True)
+    return jnp.sum(swapped.astype(jnp.float32), axis=1).astype(jnp.bfloat16)
 
 
 def exchange_blocks(summed, axis_name):
@@ -110,10 +108,10 @@
     col_saved = forward(mid_columns, col_weight, 0, False)
     grad_mid_columns, grad_col_proj = backward(col_saved, col_weight, cotangent, 0)
     col_term = weight_term(col_saved[1], grad_col_proj, col_saved[3], cotangent, 0)
-    col_summed = pair_presum(col_term, "cell")
+    col_grad = lax.psum_scatter(
+        col_term.astype(jnp.bfloat16), "cell", scatter_dimension=0, tiled=True
+    ).astype(jnp.float32)
     grad_mid = lax.all_to_all(grad_mid_columns, "cell", split_axis=0, concat_axis=1, tiled=True)
-    col_summed, grad_mid = lax.optimization_barrier((col_summed, grad_mid))
-    col_grad = exchange_blocks(col_summed, "cell")
     grad_cells, grad_row_proj = backward(row_saved, row_weight, grad_mid, 1)
     row_term = weight_term(row_saved[1], grad_row_proj, row_saved[3], grad_mid, 1)
     row_grad = exchange_blocks(pair_presum(row_term, "cell"), "cell")

time: 261 us -> 243 us (0.931)
  waiting for transfers between devices: 107 us -> 64.4 us
  between operations: 1.15 us -> 14.6 us
  blocking collectives: 0 us -> 8.62 us
  local copies, waits for them, and re-layouts: 37.5 us -> 41.8 us
  starting transfers between devices: 22.7 us -> 19 us
    all_to_all x2 -> x1, waiting for transfers between devices: 76.1 us -> 57 us  [exchange_blocks(): lax.all_to_all(summed, axis_name, split_axis=0, concat_axis=0, axis_index...]
    all_to_all x1, waiting for transfers between devices: 18.7 us -> 0.01 us  [body(): lax.all_to_all(grad_mid_columns, 'cell', split_axis=0, concat_axis=1, til...]
    all_to_all x0 -> x1, blocking collectives: none -> 8.62 us  [pair_presum(): lax.all_to_all(pairs, axis_name, split_axis=1, concat_axis=1, axis_index_...]
    convert_element_type x2 -> x1, other arithmetic: 7.38 us -> 1.82 us  [body(): col_grad = lax.psum_scatter(col_term.astype(jnp.bfloat16), 'cell', scatte...]
    reduce_sum x0 -> x1, other arithmetic: none -> 5.5 us  [pair_presum(): return jnp.sum(swapped.astype(jnp.float32), axis=1).astype(jnp.bfloat16)]
    unnamed x74 -> x62, local copies, waits for them, and re-layouts: 8.9 us -> 3.93 us
    ppermute x2 -> x0, waiting for transfers between devices: 4.52 us -> none  [pair_presum(): lax.ppermute(send, axis_name, perm=[(i, i ^ 1) for i in range(count)])]
    dot_general x5, matrix products: 7.3 us -> 11.4 us  [attend_heads(): jnp.einsum('bhlm,bhme->bhle', weights, values_part, preferred_element_typ...]
  transfers between devices with their start and end apart: 6 -> 4, of which waited for: 5 -> 2; matrix products, arithmetic and copies ran while one was open for 15% -> 31% of each run, Pallas kernels for 0% -> 0%
where the time goes in v4:
time: 243 us; the launch traced here: 241 us
  waiting for transfers between devices  64.4 us (27%)
  matrix products  63.6 us (26%)
  local copies, waits for them, and re-layouts  41.8 us (17%)
  other arithmetic  29.3 us (12%)
  starting transfers between devices  19 us (8%)
  between operations  14.6 us (6%)
  blocking collectives  8.62 us (4%)
    all_to_all x1, waiting for transfers between devices, exchange_blocks(): lax.all_to_all(summed, axis_name, split_axis=0, concat_axis=0, axis_index...  57 us
    dot_general x6, matrix products, attend_heads(): jnp.einsum('bhle,bhme->bhlm', queries, keys_part, preferred_element_type=...  11.4 us
    dot_general x5, matrix products, attend_heads(): jnp.einsum('bhlm,bhme->bhle', weights, values_part, preferred_element_typ...  11.4 us
    dot_general x2, matrix products, backward(): jnp.einsum('tbhle,dthe->' + cell_form, grad_projected, projection, prefer...  10.2 us
    slice x6, local copies, waits for them, and re-layouts, split_weight(): weight[:, :3 * model_width].reshape(model_width, 3, HEADS, head_size)  9.52 us
    dot_general x2, matrix products, forward(): jnp.einsum(cell_form + ',dthe->tbhle', normed, projection, preferred_elem...  9.46 us
    all_to_all x1, blocking collectives, pair_presum(): lax.all_to_all(pairs, axis_name, split_axis=1, concat_axis=1, axis_index_...  8.62 us
    dot_general x2, matrix products, weight_term(): jnp.einsum(cell_form + ',tbhle->dthe', normed, grad_projected, preferred_...  8.45 us
  transfers between devices with their start and end apart: 4, of which 2 were waited for; matrix products, arithmetic and copies ran while one was open for 31% of the time, Pallas kernels for 0%

profile of v4, /device:TPU:0, one launch (start us, length us, event | category | flops | bytes accessed | tf_op | source)
XLA Modules:
  0.0 241.2 jit_solution(18103521960341810783)
XLA Ops:
  7.2 2.4 %slice.44 = bf16[768,768]{1,0:T(8,128)(2,1)} slice(bf16[768,3072]{1,0:T(8,128)(2,1)} %param.6), slice={[0:768], [2304:3072]} | slice | bytes 2359296 | tf_op jit(solution)/shard_map/slice | solution.py:34
  11.8 3.6 %copy.169 = bf16[768,2304]{0,1:T(8,128)(2,1)} copy(bf16[768,2304]{1,0:T(8,128)(2,1)S(1)} %slice-done) | data formatting | bytes 7077888 | tf_op jit(solution)/shard_map/slice | solution.py:33
  15.4 5.8 %convert_bitcast_fusion = bf16[3,8,12,64,64]{4,3,2,0,1:T(8,128)(2,1)S(1)} fusion(bf16[768,3,12,64,1]{0,3,2,1,4:T(8,128)(2,1)} %bitcast.196, bf16[8,64,768]{2,1,0:T(8,128)(2,1)} %param.4, f32[8,64]{1,0:T(8,128)S(1)} %fusion.70), kind=kOutput, calls=%fused_computation.8 | convolution fusion | flops 1814298624 | bytes 6686720 | tf_op jit(solution)/shard_map/bld,dthe->tbhle/dot_general | solution.py:43
  22.2 4.7 %fusion.82 = (f32[8,12,64]{2,1,0:T(8,128)S(1)}, f32[8,12,64,64]{2,3,1,0:T(8,128)S(1)}) fusion(f32[8,12,64,64]{2,3,1,0:T(8,128)S(1)} %fusion.43), kind=kOutput, calls=%fused_computation.124 | output fusion | flops 1572927 | bytes 3170304 | tf_op jit(solution)/shard_map/sub | solution.py:21
  32.0 7.4 %all-to-all-start = ((bf16[8,64,768]{2,0,1:T(8,128)(2,1)}), bf16[8,64,768]{2,0,1:T(8,128)(2,1)}, u32[]{:S(2)}, u32[]{:S(2)}) async-start(bf16[8,64,768]{2,0,1:T(8,128)(2,1)} %copy.171), calls=%async_computation | async-start | bytes 1572864 | tf_op jit(solution)/shard_map/all_to_all | solution.py:107
  39.4 2.5 %slice.39 = bf16[768,768]{1,0:T(8,128)(2,1)} slice(bf16[768,3072]{1,0:T(8,128)(2,1)} %param.7), slice={[0:768], [2304:3072]} | slice | bytes 2359296 | tf_op jit(solution)/shard_map/slice | solution.py:34
  41.9 2.0 slice-done.1
  43.9 3.6 %copy.176 = bf16[768,2304]{0,1:T(8,128)(2,1)} copy(bf16[768,2304]{1,0:T(8,128)(2,1)S(1)} %slice-done.1) | data formatting | bytes 7077888 | tf_op jit(solution)/shard_map/slice | solution.py:33
  47.5 3.3 %fusion.47 = bf16[4,12,128,64]{2,3,0,1:T(8,128)(2,1)} fusion(bf16[12,64,768,1]{2,1,3,0:T(8,128)(2,1)} %bitcast.207, bf16[128,4,768]{2,1,0:T(4,128)(2,1)} %param.5), kind=kOutput, calls=%fused_computation.87 | convolution fusion | flops 604372992 | bytes 2752512 | tf_op jit(solution)/shard_map/lbf,hef->bhle/dot_general | solution.py:60
  50.8 7.3 %all-to-all-done = bf16[8,64,768]{2,0,1:T(8,128)(2,1)} async-done(((bf16[8,64,768]{2,0,1:T(8,128)(2,1)}), bf16[8,64,768]{2,0,1:T(8,128)(2,1)}, u32[]{:S(2)}, u32[]{:S(2)}) %all-to-all-start) | async-done | bytes 786464 | tf_op jit(solution)/shard_map/all_to_all | solution.py:107
  58.2 2.0 multiply_reduce_fusion.2
  60.1 1.4 copy.173
  61.6 1.3 multiply_add_fusion
  62.9 1.4 copy.174
  64.3 3.6 %convert_bitcast_fusion.1 = bf16[3,4,12,128,64]{3,4,2,0,1:T(8,128)(2,1)S(1)} fusion(bf16[768,3,12,64,1]{0,3,2,1,4:T(8,128)(2,1)S(1)} %bitcast.198, f32[16,8,4]{1,2,0:T(4,128)} %copy.174, bf16[8,64,768]{2,0,1:T(8,128)(2,1)} %all-to-all-done), kind=kOutput, calls=%fused_computation.41 | convolution fusion | flops 1814298624 | bytes 6686720 | tf_op jit(solution)/shard_map/lbd,dthe->tbhle/dot_general | solution.py:43
  68.6 3.0 %fusion.83 = (f32[4,12,128]{2,1,0:T(8,128)S(1)}, f32[4,12,128,128]{2,3,1,0:T(8,128)S(1)}) fusion(f32[4,12,128,128]{2,3,1,0:T(8,128)S(1)} %fusion.63), kind=kOutput, calls=%fused_computation.125 | output fusion | flops 3145855 | bytes 6316032 | tf_op jit(solution)/shard_map/jvp()/sub | solution.py:21
  71.7 2.2 fusion.6
  73.9 2.1 fusion.49
  76.0 1.7 fusion.48
  79.2 2.9 %fusion.46 = bf16[1,4,12,128,64]{3,4,2,1,0:T(8,128)(2,1)S(1)} fusion(bf16[4,12,128,128]{2,3,1,0:T(8,128)(2,1)} %get-tuple-element.4, bf16[4,12,128,64]{2,3,0,1:T(8,128)(2,1)} %fusion.47), kind=kOutput, calls=%fused_computation.86 | convolution fusion | flops 101056512 | bytes 3145728 | tf_op jit(solution)/shard_map/transpose(jvp(bhlm,bhme->bhle))/dot_general | solution.py:22
  82.2 3.6 %fusion.31 = (f32[128,4]{0,1:T(4,128)S(1)}, f32[4,128,768,1,1]{2,1,3,0,4:T(8,128)S(1)}) fusion(bf16[768,3,12,64,1]{0,3,2,4,1:T(8,128)(2,1)S(1)} %bitcast.199, bf16[1,4,12,128,64]{3,4,2,1,0:T(8,128)(2,1)S(1)} %fusion.46, bf16[1,4,12,128,64]{3,4,2,1,0:T(8,128)(2,1)S(1)} %copy-done.17, bf16[1,4,12,128,64]{3,4,2,1,0:T(8,128)(2,1)S(1)} %copy-done.18, ...), kind=kOutput, calls=%fused_computation.68 | convolution fusion | flops 1815477760 | bytes 8259584 | tf_op jit(solution)/shard_map/tbhle,dthe->lbd/dot_general | solution.py:65
  85.8 1.5 fusion.20
  87.4 1.5 copy.184
  88.9 5.5 %all-to-all-start.1 = ((bf16[128,4,768]{2,1,0:T(4,128)(2,1)}), bf16[128,4,768]{2,1,0:T(4,128)(2,1)S(1)}, u32[]{:S(2)}, u32[]{:S(2)}) async-start(bf16[128,4,768]{2,1,0:T(4,128)(2,1)} %copy.184), calls=%async_computation.1 | async-start | bytes 1572864 | tf_op jit(solution)/shard_map/all_to_all | solution.py:114
  94.5 2.5 %copy.188 = bf16[12,64,8,64]{1,0,3,2:T(8,128)(2,1)S(1)} copy(bf16[12,64,8,64]{1,3,0,2:T(8,128)(2,1)} %bitcast.203) | data formatting | bytes 1572864 | tf_op jit(solution)/shard_map/convert_element_type | solution.py:23
  97.0 2.3 dot_general.96
  99.2 1.9 fusion.50
  101.1 2.0 copy.192
  103.1 3.6 %bitcast_convert_fusion.2 = bf16[12,64,768]{2,1,0:T(8,128)(2,1)} fusion(bf16[4,12,128,128]{2,3,1,0:T(8,128)(2,1)S(1)} %copy-done.12, bf16[128,4,768]{2,1,0:T(4,128)(2,1)} %param.5, bf16[3,4,12,128,64]{3,4,2,0,1:T(8,128)(2,1)} %copy-done.16), kind=kOutput, calls=%fused_computation.39 | convolution fusion | flops 705626112 | bytes 4325376 | tf_op jit(solution)/shard_map/bhle,lbf->hef/dot_general | solution.py:79
  106.7 4.2 %bitcast_convert_fusion.1 = bf16[768,2304]{1,0:T(8,128)(2,1)S(1)} fusion(bf16[2304,4,128]{2,0,1:T(8,128)(2,1)} %bitcast.202, f32[128,4]{0,1:T(4,128)S(1)} %get-tuple-element.7, bf16[8,64,768]{2,0,1:T(8,128)(2,1)} %all-to-all-done), kind=kOutput, calls=%fused_computation.3 | convolution fusion | flops 1814888448 | bytes 6686720 | tf_op jit(solution)/shard_map/lbd,tbhle->dthe/dot_general | solution.py:76
  110.9 2.8 %pad_maximum_fusion.2 = bf16[768,3072]{1,0:T(8,128)(2,1)} fusion(bf16[768,768]{1,0:T(8,128)(2,1)S(1)} %bitcast.204, bf16[768,2304]{1,0:T(8,128)(2,1)S(1)} %bitcast_convert_fusion.1), kind=kLoop, calls=%fused_computation.6 | loop fusion | flops 9437184 | bytes 9437184 | tf_op jit(solution)/shard_map/concatenate | solution.py:82
  116.2 3.1 %convolution_convert_fusion = bf16[8,64,12,64]{3,1,2,0:T(8,128)(2,1)S(1)} fusion(bf16[12,64,768,1]{2,1,0,3:T(8,128)(2,1)} %bitcast.205, bf16[8,64,768,1]{2,1,0,3:T(8,128)(2,1)} %reshape.128), kind=kOutput, calls=%fused_computation.43 | convolution fusion | flops 604372992 | bytes 2752512 | tf_op jit(solution)/shard_map/blf,hef->bhle/dot_general | solution.py:60
  119.2 1.8 fusion.37
  121.0 3.7 %fusion.11 = (f32[8,12,64]{2,1,0:T(8,128)S(1)}, bf16[8,12,64,64]{2,3,1,0:T(8,128)(2,1)}) fusion(f32[8,12,64,64]{2,3,1,0:T(8,128)S(1)} %copy-done.1, f32[8,12,64]{2,1,0:T(8,128)S(1)} %multiply_divide_fusion, bf16[3,8,12,64,64]{4,3,2,0,1:T(8,128)(2,1)} %copy-done.2, bf16[8,64,12,64]{3,1,2,0:T(8,128)(2,1)S(1)} %convolution_convert_fusion), kind=kOutput, calls=%fused_computation.22 | convolution fusion | flops 52291584 | bytes 4767744 | tf_op jit(solution)/shard_map/transpose(jvp(bhlm,bhme->bhle))/dot_general | solution.py:22
  124.7 1.9 bitcast_convert_fusion.3
  126.6 2.4 %copy.190 = bf16[768,768]{1,0:T(8,128)(2,1)} copy(bf16[768,768]{0,1:T(8,128)(2,1)} %bitcast_convert_fusion.3) | data formatting | bytes 2359296 | tf_op jit(solution)/shard_map/convert.10
  129.0 3.1 %fusion.35 = bf16[1,8,12,64,64]{4,3,2,1,0:T(8,128)(2,1)S(1)} fusion(bf16[3,8,12,64,64]{4,3,2,0,1:T(8,128)(2,1)} %copy-done.2, f32[8,12,64,64]{2,3,1,0:T(8,128)S(1)} %copy-done.1, bf16[8,12,64,64]{2,3,1,0:T(8,128)(2,1)} %get-tuple-element.17, f32[8,12,64]{2,1,0:T(8,128)S(1)} %neg.13, f32[8,12,64]{2,1,0:T(8,128)S(1)} %copy-done.23), kind=kOutput, calls=%fused_computation.77 | convolution fusion | flops 52690944 | bytes 5554176 | tf_op jit(solution)/shard_map/transpose(jvp(bhle,bhme->bhlm))/dot_general | solution.py:18
  132.2 3.0 %fusion.36 = bf16[1,8,12,64,64]{4,3,2,1,0:T(8,128)(2,1)S(1)} fusion(bf16[3,8,12,64,64]{4,3,2,0,1:T(8,128)(2,1)} %copy-done.2, f32[8,12,64,64]{2,3,1,0:T(8,128)S(1)} %copy-done.1, bf16[8,12,64,64]{2,3,1,0:T(8,128)(2,1)S(1)} %copy-done.13, f32[8,12,64]{2,1,0:T(8,128)S(1)} %neg.13, f32[8,12,64]{2,1,0:T(8,128)S(1)} %copy-done.23), kind=kOutput, calls=%fused_computation.78 | convolution fusion | flops 52690944 | bytes 4767744 | tf_op jit(solution)/shard_map/transpose(jvp(bhle,bhme->bhlm))/dot_general | solution.py:18
  135.2 4.2 %bitcast_convert_fusion = bf16[768,3,12,64]{0,3,2,1:T(8,128)(2,1)} fusion(bf16[1,8,12,64,64]{4,3,2,1,0:T(8,128)(2,1)S(1)} %copy-done.28, bf16[1,8,12,64,64]{4,3,2,1,0:T(8,128)(2,1)S(1)} %fusion.36, bf16[1,8,12,64,64]{4,3,2,1,0:T(8,128)(2,1)S(1)} %fusion.35, bf16[8,64,768]{2,1,0:T(8,128)(2,1)S(1)} %copy-done.7, f32[8,64]{1,0:T(8,128)S(1)} %copy-done.27), kind=kOutput, calls=%fused_computation.2 | convolution fusion | flops 1821966336 | bytes 6686720 | tf_op jit(solution)/shard_map/bld,tbhle->dthe/dot_general | solution.py:76
  139.5 4.3 %copy.189 = bf16[768,2304]{1,0:T(8,128)(2,1)S(1)} copy(bf16[768,2304]{0,1:T(8,128)(2,1)} %bitcast.200) | data formatting | bytes 7077888 | tf_op jit(solution)/shard_map/reshape | solution.py:78
  143.8 2.0 pad_maximum_fusion.1
  146.2 8.6 %all_to_all.37 = bf16[8,2,48,3072]{3,2,0,1:T(8,128)(2,1)} all-to-all(bf16[8,2,48,3072]{3,2,0,1:T(8,128)(2,1)S(1)} %copy.191), channel_id=1, replica_groups={{0,1},{2,3},{4,5},{6,7},{8,9},{10,11},{12,13},{14,15},{16,17},{18,19},{..., dimensions={1} | all-to-all | bytes 9437184 | tf_op jit(solution)/shard_map/all_to_all | solution.py:92
  154.9 5.5 %reduce_sum.106 = bf16[8,48,3072]{2,1,0:T(8,128)(2,1)} reduce(bf16[8,2,48,3072]{3,2,0,1:T(8,128)(2,1)} %all_to_all.37, bf16[]{:T(256)} %constant.6.clone.1), dimensions={1}, to_apply=%region_10.0 | reduce | flops 1179648 | bytes 7077890 | tf_op jit(solution)/shard_map/reduce_sum | solution.py:93
  160.4 6.0 %all-to-all-start.3 = ((bf16[8,48,3072]{2,1,0:T(8,128)(2,1)}), bf16[8,48,3072]{2,1,0:T(8,128)(2,1)S(1)}, u32[]{:S(2)}, u32[]{:S(2)}) async-start(bf16[8,48,3072]{2,1,0:T(8,128)(2,1)} %reduce_sum.106), calls=%async_computation.3 | async-start | bytes 4718592 | tf_op jit(solution)/shard_map/all_to_all | solution.py:99
  166.4 6.6 %fusion.26 = (f32[8,64]{1,0:T(8,128)S(1)}, f32[8,64,768,1,1]{2,1,3,0,4:T(8,128)S(1)}) fusion(bf16[8,64,768]{2,1,0:T(8,128)(2,1)S(1)} %copy-done.8, bf16[768,3,12,64,1]{0,3,2,4,1:T(8,128)(2,1)} %bitcast.197, bf16[1,8,12,64,64]{4,3,2,1,0:T(8,128)(2,1)} %fusion.37, bf16[1,8,12,64,64]{4,3,2,1,0:T(8,128)(2,1)} %copy-done.30, ...), kind=kOutput, calls=%fused_computation.57 | convolution fusion | flops 1815477760 | bytes 8259584 | tf_op jit(solution)/shard_map/tbhle,dthe->bld/dot_general | solution.py:65
  173.1 1.3 fusion.22
  174.4 57.0 %all-to-all-done.3 = bf16[8,48,3072]{2,1,0:T(8,128)(2,1)S(1)} async-done(((bf16[8,48,3072]{2,1,0:T(8,128)(2,1)}), bf16[8,48,3072]{2,1,0:T(8,128)(2,1)S(1)}, u32[]{:S(2)}, u32[]{:S(2)}) %all-to-all-start.3) | async-done | bytes 2359328 | tf_op jit(solution)/shard_map/all_to_all | solution.py:99
  232.6 1.8 convert_element_type.170
  (89 shorter events, 14.6 us)
Async XLA Ops:
  9.6 1.1 copy-start.5
  9.6 2.2 slice-start
  10.9 0.6 copy-start.24
  11.8 3.6 %copy-start.26 = (f32[8,64]{1,0:T(8,128)}, f32[8,64]{1,0:T(8,128)S(1)}, u32[]{:S(2)}) copy-start(f32[8,64]{1,0:T(8,128)S(1)} %fusion.70) | copy-start | bytes 6148
  21.2 5.6 %copy-start.2 = (bf16[3,8,12,64,64]{4,3,2,0,1:T(8,128)(2,1)}, bf16[3,8,12,64,64]{4,3,2,0,1:T(8,128)(2,1)S(1)}, u32[]{:S(2)}) copy-start(bf16[3,8,12,64,64]{4,3,2,0,1:T(8,128)(2,1)S(1)} %convert_bitcast_fusion) | copy-start | bytes 7077892
  26.9 1.6 copy-start
  26.9 1.7 copy-start.22
  26.9 1.7 copy-start.6
  26.9 2.9 %copy-start.15 = (bf16[768,768]{1,0:T(8,128)(2,1)S(1)}, bf16[768,768]{1,0:T(8,128)(2,1)}, u32[]{:S(2)}) copy-start(bf16[768,768]{1,0:T(8,128)(2,1)} %slice.44) | copy-start | bytes 3538948
  28.5 2.1 copy-start.11
  32.0 26.2 %all-to-all-start = ((bf16[8,64,768]{2,0,1:T(8,128)(2,1)}), bf16[8,64,768]{2,0,1:T(8,128)(2,1)}, u32[]{:S(2)}, u32[]{:S(2)}) async-start(bf16[8,64,768]{2,0,1:T(8,128)(2,1)} %copy.171), calls=%async_computation | async-start | bytes 1572864 | tf_op jit(solution)/shard_map/all_to_all | solution.py:107
  41.9 2.0 slice-start.1
  47.5 16.8 %copy-start.3 = (bf16[768,2304]{0,1:T(8,128)(2,1)S(1)}, bf16[768,2304]{0,1:T(8,128)(2,1)}, u32[]{:S(2)}) copy-start(bf16[768,2304]{0,1:T(8,128)(2,1)} %copy.176) | copy-start | bytes 10616836
  68.0 8.1 %copy-start.16 = (bf16[3,4,12,128,64]{3,4,2,0,1:T(8,128)(2,1)}, bf16[3,4,12,128,64]{3,4,2,0,1:T(8,128)(2,1)S(1)}, u32[]{:S(2)}) copy-start(bf16[3,4,12,128,64]{3,4,2,0,1:T(8,128)(2,1)S(1)} %convert_bitcast_fusion.1) | copy-start | bytes 7077892
  68.6 3.1 %copy-start.21 = (bf16[4,12,128,64]{2,3,0,1:T(8,128)(2,1)S(1)}, bf16[4,12,128,64]{2,3,0,1:T(8,128)(2,1)}, u32[]{:S(2)}) copy-start(bf16[4,12,128,64]{2,3,0,1:T(8,128)(2,1)} %fusion.47) | copy-start | bytes 2359300
  79.2 2.9 %copy-start.17 = (bf16[1,4,12,128,64]{3,4,2,1,0:T(8,128)(2,1)S(1)}, bf16[1,4,12,128,64]{3,4,2,1,0:T(8,128)(2,1)}, u32[]{:S(2)}) copy-start(bf16[1,4,12,128,64]{3,4,2,1,0:T(8,128)(2,1)} %fusion.49) | copy-start | bytes 2359300
  79.2 2.9 %copy-start.18 = (bf16[1,4,12,128,64]{3,4,2,1,0:T(8,128)(2,1)S(1)}, bf16[1,4,12,128,64]{3,4,2,1,0:T(8,128)(2,1)}, u32[]{:S(2)}) copy-start(bf16[1,4,12,128,64]{3,4,2,1,0:T(8,128)(2,1)} %fusion.48) | copy-start | bytes 2359300
  82.1 3.7 %copy-start.4 = (bf16[1,4,12,128,64]{3,4,2,1,0:T(8,128)(2,1)}, bf16[1,4,12,128,64]{3,4,2,1,0:T(8,128)(2,1)S(1)}, u32[]{:S(2)}) copy-start(bf16[1,4,12,128,64]{3,4,2,1,0:T(8,128)(2,1)S(1)} %fusion.46) | copy-start | bytes 2359300
  82.2 3.6 %copy-start.19 = (bf16[128,4,768]{2,1,0:T(4,128)(2,1)S(1)}, bf16[128,4,768]{2,1,0:T(4,128)(2,1)}, u32[]{:S(2)}) copy-start(bf16[128,4,768]{2,1,0:T(4,128)(2,1)} %param.5) | copy-start | bytes 2359300
  87.4 7.0 %copy-start.23 = (f32[8,12,64]{2,1,0:T(8,128)S(1)}, f32[8,12,64]{2,1,0:T(8,128)}, u32[]{:S(2)}) copy-start(f32[8,12,64]{2,1,0:T(8,128)} %copy-done.22) | copy-start | bytes 73732
  88.9 24.9 %all-to-all-start.1 = ((bf16[128,4,768]{2,1,0:T(4,128)(2,1)}), bf16[128,4,768]{2,1,0:T(4,128)(2,1)S(1)}, u32[]{:S(2)}, u32[]{:S(2)}) async-start(bf16[128,4,768]{2,1,0:T(4,128)(2,1)} %copy.184), calls=%async_computation.1 | async-start | bytes 1572864 | tf_op jit(solution)/shard_map/all_to_all | solution.py:114
  94.4 138.2 %reduce-scatter.2.cloned.1.call-start = ((), (), s32[]{:S(2)}) async-start(), calls=%async_computation.5 | async-start | bytes 5013504 | tf_op jit(solution)/shard_map/reduce_scatter | solution.py:111
  101.1 2.0 copy-start.12
  106.7 4.2 %copy-start.14 = (bf16[12,64,768]{2,1,0:T(8,128)(2,1)S(1)}, bf16[12,64,768]{2,1,0:T(8,128)(2,1)}, u32[]{:S(2)}) copy-start(bf16[12,64,768]{2,1,0:T(8,128)(2,1)} %bitcast_convert_fusion.2) | copy-start | bytes 3538948
  116.2 3.1 %copy-start.1 = (f32[8,12,64,64]{2,3,1,0:T(8,128)S(1)}, f32[8,12,64,64]{2,3,1,0:T(8,128)}, u32[]{:S(2)}) copy-start(f32[8,12,64,64]{2,3,1,0:T(8,128)} %copy-done) | copy-start | bytes 4718596
  121.0 3.7 %copy-start.9 = (bf16[8,64,768]{2,1,0:T(8,128)(2,1)S(1)}, bf16[8,64,768]{2,1,0:T(8,128)(2,1)}, u32[]{:S(2)}) copy-start(bf16[8,64,768]{2,1,0:T(8,128)(2,1)} %all_to_all.30) | copy-start | bytes 2359300
  121.0 3.7 %copy-start.20 = (bf16[768,8,64]{0,2,1:T(8,128)(2,1)S(1)}, bf16[768,8,64]{0,2,1:T(8,128)(2,1)}, u32[]{:S(2)}) copy-start(bf16[768,8,64]{0,2,1:T(8,128)(2,1)} %dot_general.96) | copy-start | bytes 2359300
  129.0 3.1 %copy-start.13 = (bf16[8,12,64,64]{2,3,1,0:T(8,128)(2,1)S(1)}, bf16[8,12,64,64]{2,3,1,0:T(8,128)(2,1)}, u32[]{:S(2)}) copy-start(bf16[8,12,64,64]{2,3,1,0:T(8,128)(2,1)} %get-tuple-element.17) | copy-start | bytes 2359300
  132.2 3.0 %copy-start.29 = (bf16[1,8,12,64,64]{4,3,2,1,0:T(8,128)(2,1)}, bf16[1,8,12,64,64]{4,3,2,1,0:T(8,128)(2,1)S(1)}, u32[]{:S(2)}) copy-start(bf16[1,8,12,64,64]{4,3,2,1,0:T(8,128)(2,1)S(1)} %fusion.35) | copy-start | bytes 2359300
  132.2 3.0 %copy-start.7 = (bf16[8,64,768]{2,1,0:T(8,128)(2,1)S(1)}, bf16[8,64,768]{2,1,0:T(8,128)(2,1)}, u32[]{:S(2)}) copy-start(bf16[8,64,768]{2,1,0:T(8,128)(2,1)} %param.4) | copy-start | bytes 2359300
  132.2 3.0 %copy-start.27 = (f32[8,64]{1,0:T(8,128)S(1)}, f32[8,64]{1,0:T(8,128)}, u32[]{:S(2)}) copy-start(f32[8,64]{1,0:T(8,128)} %copy-done.26) | copy-start | bytes 6148
  132.2 3.0 %copy-start.28 = (bf16[1,8,12,64,64]{4,3,2,1,0:T(8,128)(2,1)S(1)}, bf16[1,8,12,64,64]{4,3,2,1,0:T(8,128)(2,1)}, u32[]{:S(2)}) copy-start(bf16[1,8,12,64,64]{4,3,2,1,0:T(8,128)(2,1)} %fusion.37) | copy-start | bytes 2359300
  135.2 4.2 %copy-start.30 = (bf16[1,8,12,64,64]{4,3,2,1,0:T(8,128)(2,1)}, bf16[1,8,12,64,64]{4,3,2,1,0:T(8,128)(2,1)S(1)}, u32[]{:S(2)}) copy-start(bf16[1,8,12,64,64]{4,3,2,1,0:T(8,128)(2,1)S(1)} %fusion.36) | copy-start | bytes 2359300
  160.3 6.0 %copy-start.8 = (bf16[8,64,768]{2,1,0:T(8,128)(2,1)S(1)}, bf16[8,64,768]{2,1,0:T(8,128)(2,1)}, u32[]{:S(2)}) copy-start(bf16[8,64,768]{2,1,0:T(8,128)(2,1)} %param.4) | copy-start | bytes 2359300
  160.4 71.1 %all-to-all-start.3 = ((bf16[8,48,3072]{2,1,0:T(8,128)(2,1)}), bf16[8,48,3072]{2,1,0:T(8,128)(2,1)S(1)}, u32[]{:S(2)}, u32[]{:S(2)}) async-start(bf16[8,48,3072]{2,1,0:T(8,128)(2,1)} %reduce_sum.106), calls=%async_computation.3 | async-start | bytes 4718592 | tf_op jit(solution)/shard_map/all_to_all | solution.py:99
  166.4 6.6 %copy-start.25 = (f32[8,64]{1,0:T(8,128)S(1)}, f32[8,64]{1,0:T(8,128)}, u32[]{:S(2)}) copy-start(f32[8,64]{1,0:T(8,128)} %copy-done.24) | copy-start | bytes 6148
  166.4 6.7 %copy-start.10 = (bf16[8,64,768]{2,1,0:T(8,128)(2,1)S(1)}, bf16[8,64,768]{2,1,0:T(8,128)(2,1)}, u32[]{:S(2)}) copy-start(bf16[8,64,768]{2,1,0:T(8,128)(2,1)} %all_to_all.30) | copy-start | bytes 2359300
Sparse Core Ops, SparseCore 0:
  113.9 111.1 reduce-scatter.1

commit v5 on v4

--- a/solution.py
+++ b/solution.py
@@ -87,10 +87,10 @@
     block = term.shape[0] // count
     index = lax.axis_index(axis_name)
     sent = lax.optimization_barrier(term.astype(jnp.bfloat16))
-    pairs = sent.reshape((count // 2, 2, block) + term.shape[1:])
+    pairs = jnp.swapaxes(sent.reshape((count // 2, 2, block) + term.shape[1:]), 0, 1)
     couples = [[low, low + 1] for low in range(0, count, 2)]
-    swapped = lax.all_to_all(pairs, axis_name, split_axis=1, concat_axis=1, axis_index_groups=couples, tiled=True)
-    return jnp.sum(swapped.astype(jnp.float32), axis=1).astype(jnp.bfloat16)
+    swapped = lax.all_to_all(pairs, axis_name, split_axis=0, concat_axis=0, axis_index_groups=couples, tiled=True)
+    return (swapped[0].astype(jnp.float32) + swapped[1].astype(jnp.float32)).astype(jnp.bfloat16)
 
 
 def exchange_blocks(summed, axis_name):

time: 243 us -> 242 us (level)
  waiting for transfers between devices: 64.4 us -> 71 us
  other arithmetic: 29.3 us -> 26 us
    all_to_all x1, waiting for transfers between devices: 57 us -> 63.5 us  [exchange_blocks(): lax.all_to_all(summed, axis_name, split_axis=0, concat_axis=0, axis_index...]
    reduce_sum x1 -> x0, other arithmetic: 5.5 us -> none  [pair_presum(): return jnp.sum(swapped.astype(jnp.float32), axis=1).astype(jnp.bfloat16)]
  transfers between devices with their start and end apart: 4 -> 4, of which waited for: 2 -> 3; matrix products, arithmetic and copies ran while one was open for 31% -> 29% of each run, Pallas kernels for 0% -> 0%
where the time goes in v5:
time: 242 us; the launch traced here: 241 us
  waiting for transfers between devices  71 us (29%)
  matrix products  62 us (26%)
  local copies, waits for them, and re-layouts  41 us (17%)
  other arithmetic  26 us (11%)
  starting transfers between devices  18.9 us (8%)
  between operations  14.6 us (6%)
  blocking collectives  7.52 us (3%)
    all_to_all x1, waiting for transfers between devices, exchange_blocks(): lax.all_to_all(summed, axis_name, split_axis=0, concat_axis=0, axis_index...  63.5 us
    dot_general x5, matrix products, attend_heads(): jnp.einsum('bhlm,bhme->bhle', weights, values_part, preferred_element_typ...  11.1 us
    dot_general x6, matrix products, attend_heads(): jnp.einsum('bhle,bhme->bhlm', queries, keys_part, preferred_element_type=...  10.7 us
    dot_general x2, matrix products, backward(): jnp.einsum('tbhle,dthe->' + cell_form, grad_projected, projection, prefer...  10.3 us
    slice x6, local copies, waits for them, and re-layouts, split_weight(): weight[:, :3 * model_width].reshape(model_width, 3, HEADS, head_size)  9.53 us
    dot_general x2, matrix products, forward(): jnp.einsum(cell_form + ',dthe->tbhle', normed, projection, preferred_elem...  9.46 us
    dot_general x2, matrix products, weight_term(): jnp.einsum(cell_form + ',tbhle->dthe', normed, grad_projected, preferred_...  8.2 us
    sub x2, other arithmetic, attend_heads(): weights = jax.nn.softmax(scores, axis=-1).astype(jnp.bfloat16)  7.69 us
  transfers between devices with their start and end apart: 4, of which 3 were waited for; matrix products, arithmetic and copies ran while one was open for 29% of the time, Pallas kernels for 0%

profile of v5, /device:TPU:0, one launch (start us, length us, event | category | flops | bytes accessed | tf_op | source)
XLA Modules:
  0.0 241.1 jit_solution(3123822917529742498)
XLA Ops:
  7.2 2.4 slice.50
  11.8 3.6 %copy.140 = bf16[768,2304]{0,1:T(8,128)(2,1)} copy(bf16[768,2304]{1,0:T(8,128)(2,1)S(1)} %slice-done) | data formatting | bytes 7077888 | tf_op jit(solution)/shard_map/slice | solution.py:33
  15.4 5.8 %convert_bitcast_fusion = bf16[3,8,12,64,64]{4,3,2,0,1:T(8,128)(2,1)S(1)} fusion(bf16[768,3,12,64,1]{0,3,2,1,4:T(8,128)(2,1)} %bitcast.200, bf16[8,64,768]{2,1,0:T(8,128)(2,1)} %param.4, f32[8,64]{1,0:T(8,128)S(1)} %fusion.71), kind=kOutput, calls=%fused_computation.9 | convolution fusion | flops 1814298624 | bytes 6686720 | tf_op jit(solution)/shard_map/bld,dthe->tbhle/dot_general | solution.py:43
  22.2 4.7 %fusion.83 = (f32[8,12,64]{2,1,0:T(8,128)S(1)}, f32[8,12,64,64]{2,3,1,0:T(8,128)S(1)}) fusion(f32[8,12,64,64]{2,3,1,0:T(8,128)S(1)} %fusion.44), kind=kOutput, calls=%fused_computation.126 | output fusion | flops 1572927 | bytes 3170304 | tf_op jit(solution)/shard_map/sub | solution.py:21
  31.9 7.4 %all-to-all-start = ((bf16[8,64,768]{2,0,1:T(8,128)(2,1)}), bf16[8,64,768]{2,0,1:T(8,128)(2,1)}, u32[]{:S(2)}, u32[]{:S(2)}) async-start(bf16[8,64,768]{2,0,1:T(8,128)(2,1)} %copy.142), calls=%async_computation | async-start | bytes 1572864 | tf_op jit(solution)/shard_map/all_to_all | solution.py:107
  39.4 2.4 %slice.45 = bf16[768,768]{1,0:T(8,128)(2,1)} slice(bf16[768,3072]{1,0:T(8,128)(2,1)} %param.7), slice={[0:768], [2304:3072]} | slice | bytes 2359296 | tf_op jit(solution)/shard_map/slice | solution.py:34
  41.8 2.0 slice-done.1
  43.8 3.7 %copy.147 = bf16[768,2304]{0,1:T(8,128)(2,1)} copy(bf16[768,2304]{1,0:T(8,128)(2,1)S(1)} %slice-done.1) | data formatting | bytes 7077888 | tf_op jit(solution)/shard_map/slice | solution.py:33
  47.5 3.3 %fusion.48 = bf16[4,12,128,64]{2,3,0,1:T(8,128)(2,1)} fusion(bf16[12,64,768,1]{2,1,3,0:T(8,128)(2,1)} %bitcast.211, bf16[128,4,768]{2,1,0:T(4,128)(2,1)} %param.5), kind=kOutput, calls=%fused_computation.89 | convolution fusion | flops 604372992 | bytes 2752512 | tf_op jit(solution)/shard_map/lbf,hef->bhle/dot_general | solution.py:60
  50.8 7.3 %all-to-all-done = bf16[8,64,768]{2,0,1:T(8,128)(2,1)} async-done(((bf16[8,64,768]{2,0,1:T(8,128)(2,1)}), bf16[8,64,768]{2,0,1:T(8,128)(2,1)}, u32[]{:S(2)}, u32[]{:S(2)}) %all-to-all-start) | async-done | bytes 786464 | tf_op jit(solution)/shard_map/all_to_all | solution.py:107
  58.1 2.0 multiply_reduce_fusion.2
  60.1 1.4 copy.144
  61.5 1.3 multiply_add_fusion
  62.9 1.4 copy.145
  64.3 3.6 %convert_bitcast_fusion.1 = bf16[3,4,12,128,64]{3,4,2,0,1:T(8,128)(2,1)S(1)} fusion(bf16[768,3,12,64,1]{0,3,2,1,4:T(8,128)(2,1)S(1)} %bitcast.202, f32[16,8,4]{1,2,0:T(4,128)} %copy.145, bf16[8,64,768]{2,0,1:T(8,128)(2,1)} %all-to-all-done), kind=kOutput, calls=%fused_computation.43 | convolution fusion | flops 1814298624 | bytes 6686720 | tf_op jit(solution)/shard_map/lbd,dthe->tbhle/dot_general | solution.py:43
  68.6 3.0 %fusion.84 = (f32[4,12,128]{2,1,0:T(8,128)S(1)}, f32[4,12,128,128]{2,3,1,0:T(8,128)S(1)}) fusion(f32[4,12,128,128]{2,3,1,0:T(8,128)S(1)} %fusion.64), kind=kOutput, calls=%fused_computation.127 | output fusion | flops 3145855 | bytes 6316032 | tf_op jit(solution)/shard_map/jvp()/sub | solution.py:21
  71.6 2.2 fusion.6
  73.9 2.1 fusion.50
  76.0 1.7 fusion.49
  79.2 2.9 %fusion.47 = bf16[1,4,12,128,64]{3,4,2,1,0:T(8,128)(2,1)S(1)} fusion(bf16[4,12,128,128]{2,3,1,0:T(8,128)(2,1)} %get-tuple-element.4, bf16[4,12,128,64]{2,3,0,1:T(8,128)(2,1)} %fusion.48), kind=kOutput, calls=%fused_computation.88 | convolution fusion | flops 101056512 | bytes 3145728 | tf_op jit(solution)/shard_map/transpose(jvp(bhlm,bhme->bhle))/dot_general | solution.py:22
  82.1 3.6 %fusion.32 = (f32[128,4]{0,1:T(4,128)S(1)}, f32[4,128,768,1,1]{2,1,3,0,4:T(8,128)S(1)}) fusion(bf16[768,3,12,64,1]{0,3,2,4,1:T(8,128)(2,1)S(1)} %bitcast.203, bf16[1,4,12,128,64]{3,4,2,1,0:T(8,128)(2,1)S(1)} %fusion.47, bf16[1,4,12,128,64]{3,4,2,1,0:T(8,128)(2,1)S(1)} %copy-done.18, bf16[1,4,12,128,64]{3,4,2,1,0:T(8,128)(2,1)S(1)} %copy-done.19, ...), kind=kOutput, calls=%fused_computation.70 | convolution fusion | flops 1815477760 | bytes 8259584 | tf_op jit(solution)/shard_map/tbhle,dthe->lbd/dot_general | solution.py:65
  85.8 1.5 fusion.21
  87.3 1.5 copy.155
  88.9 5.5 %all-to-all-start.1 = ((bf16[128,4,768]{2,1,0:T(4,128)(2,1)}), bf16[128,4,768]{2,1,0:T(4,128)(2,1)S(1)}, u32[]{:S(2)}, u32[]{:S(2)}) async-start(bf16[128,4,768]{2,1,0:T(4,128)(2,1)} %copy.155), calls=%async_computation.1 | async-start | bytes 1572864 | tf_op jit(solution)/shard_map/all_to_all | solution.py:114
  94.4 2.5 %copy.159 = bf16[12,64,8,64]{1,0,3,2:T(8,128)(2,1)S(1)} copy(bf16[12,64,8,64]{1,3,0,2:T(8,128)(2,1)} %bitcast.207) | data formatting | bytes 1572864 | tf_op jit(solution)/shard_map/convert_element_type | solution.py:23
  97.0 2.3 dot_general.96
  99.2 1.9 fusion.51
  101.1 2.0 copy.163
  103.1 3.6 %bitcast_convert_fusion.2 = bf16[12,64,768]{2,1,0:T(8,128)(2,1)} fusion(bf16[4,12,128,128]{2,3,1,0:T(8,128)(2,1)S(1)} %copy-done.12, bf16[128,4,768]{2,1,0:T(4,128)(2,1)} %param.5, bf16[3,4,12,128,64]{3,4,2,0,1:T(8,128)(2,1)} %copy-done.17), kind=kOutput, calls=%fused_computation.41 | convolution fusion | flops 705626112 | bytes 4325376 | tf_op jit(solution)/shard_map/bhle,lbf->hef/dot_general | solution.py:79
  106.6 4.2 %bitcast_convert_fusion.1 = bf16[768,2304]{1,0:T(8,128)(2,1)S(1)} fusion(bf16[2304,4,128]{2,0,1:T(8,128)(2,1)} %bitcast.206, f32[128,4]{0,1:T(4,128)S(1)} %get-tuple-element.7, bf16[8,64,768]{2,0,1:T(8,128)(2,1)} %all-to-all-done), kind=kOutput, calls=%fused_computation.3 | convolution fusion | flops 1814888448 | bytes 6686720 | tf_op jit(solution)/shard_map/lbd,tbhle->dthe/dot_general | solution.py:76
  110.9 2.8 %pad_maximum_fusion.2 = bf16[768,3072]{1,0:T(8,128)(2,1)} fusion(bf16[768,768]{1,0:T(8,128)(2,1)S(1)} %bitcast.208, bf16[768,2304]{1,0:T(8,128)(2,1)S(1)} %bitcast_convert_fusion.1), kind=kLoop, calls=%fused_computation.6 | loop fusion | flops 9437184 | bytes 9437184 | tf_op jit(solution)/shard_map/concatenate | solution.py:82
  115.3 2.5 %convolution_convert_fusion = bf16[8,64,12,64]{3,1,2,0:T(8,128)(2,1)} fusion(bf16[12,64,768,1]{2,1,0,3:T(8,128)(2,1)S(1)} %bitcast.210, bf16[8,64,768,1]{2,1,0,3:T(8,128)(2,1)S(1)} %reshape.132), kind=kOutput, calls=%fused_computation.45 | convolution fusion | flops 604372992 | bytes 2752512 | tf_op jit(solution)/shard_map/blf,hef->bhle/dot_general | solution.py:60
  117.8 1.9 bitcast_convert_fusion.3
  119.7 2.5 %copy.161 = bf16[768,768]{1,0:T(8,128)(2,1)} copy(bf16[768,768]{0,1:T(8,128)(2,1)} %bitcast_convert_fusion.3) | data formatting | bytes 2359296 | tf_op jit(solution)/shard_map/convert.9
  122.2 2.2 fusion.38
  124.4 3.1 %fusion.11 = (f32[8,12,64]{2,1,0:T(8,128)S(1)}, bf16[8,12,64,64]{2,3,1,0:T(8,128)(2,1)S(1)}) fusion(f32[8,12,64,64]{2,3,1,0:T(8,128)S(1)} %copy-done.1, f32[8,12,64]{2,1,0:T(8,128)S(1)} %multiply_divide_fusion, bf16[3,8,12,64,64]{4,3,2,0,1:T(8,128)(2,1)} %copy-done.2, bf16[8,64,12,64]{3,1,2,0:T(8,128)(2,1)S(1)} %copy-done.13), kind=kOutput, calls=%fused_computation.23 | convolution fusion | flops 52291584 | bytes 4767744 | tf_op jit(solution)/shard_map/transpose(jvp(bhlm,bhme->bhle))/dot_general | solution.py:22
  127.5 2.4 fusion.37
  129.9 3.0 %fusion.36 = bf16[1,8,12,64,64]{4,3,2,1,0:T(8,128)(2,1)S(1)} fusion(bf16[3,8,12,64,64]{4,3,2,0,1:T(8,128)(2,1)} %copy-done.2, f32[8,12,64,64]{2,3,1,0:T(8,128)S(1)} %copy-done.1, bf16[8,12,64,64]{2,3,1,0:T(8,128)(2,1)S(1)} %get-tuple-element.17, f32[8,12,64]{2,1,0:T(8,128)S(1)} %neg.13, f32[8,12,64]{2,1,0:T(8,128)S(1)} %copy-done.24), kind=kOutput, calls=%fused_computation.79 | convolution fusion | flops 52690944 | bytes 4767744 | tf_op jit(solution)/shard_map/transpose(jvp(bhle,bhme->bhlm))/dot_general | solution.py:18
  133.0 4.0 %bitcast_convert_fusion = bf16[768,3,12,64]{0,3,2,1:T(8,128)(2,1)} fusion(bf16[1,8,12,64,64]{4,3,2,1,0:T(8,128)(2,1)S(1)} %fusion.38, bf16[1,8,12,64,64]{4,3,2,1,0:T(8,128)(2,1)S(1)} %fusion.37, bf16[1,8,12,64,64]{4,3,2,1,0:T(8,128)(2,1)S(1)} %fusion.36, bf16[8,64,768]{2,1,0:T(8,128)(2,1)S(1)} %copy-done.7, f32[8,64]{1,0:T(8,128)S(1)} %copy-done.28), kind=kOutput, calls=%fused_computation.2 | convolution fusion | flops 1821966336 | bytes 6686720 | tf_op jit(solution)/shard_map/bld,tbhle->dthe/dot_general | solution.py:76
  137.0 4.3 %copy.160 = bf16[768,2304]{1,0:T(8,128)(2,1)S(1)} copy(bf16[768,2304]{0,1:T(8,128)(2,1)} %bitcast.204) | data formatting | bytes 7077888 | tf_op jit(solution)/shard_map/reshape | solution.py:78
  141.3 1.9 pad_maximum_fusion.1
  143.6 7.5 %all_to_all.37 = bf16[2,8,48,3072]{3,2,1,0:T(8,128)(2,1)S(1)} all-to-all(bf16[2,8,48,3072]{3,2,1,0:T(8,128)(2,1)S(1)} %copy.162), channel_id=1, replica_groups={{0,1},{2,3},{4,5},{6,7},{8,9},{10,11},{12,13},{14,15},{16,17},{18,19},{..., dimensions={0} | all-to-all | bytes 9437184 | tf_op jit(solution)/shard_map/all_to_all | solution.py:92
  151.1 2.4 fusion.18
  153.5 6.0 %all-to-all-start.3 = ((bf16[8,48,3072]{2,1,0:T(8,128)(2,1)}), bf16[8,48,3072]{2,1,0:T(8,128)(2,1)S(1)}, u32[]{:S(2)}, u32[]{:S(2)}) async-start(bf16[8,48,3072]{2,1,0:T(8,128)(2,1)} %fusion.18), calls=%async_computation.3 | async-start | bytes 4718592 | tf_op jit(solution)/shard_map/all_to_all | solution.py:99
  159.5 6.7 %fusion.27 = (f32[8,64]{1,0:T(8,128)S(1)}, f32[8,64,768,1,1]{2,1,3,0,4:T(8,128)S(1)}) fusion(bf16[8,64,768]{2,1,0:T(8,128)(2,1)S(1)} %copy-done.8, bf16[768,3,12,64,1]{0,3,2,4,1:T(8,128)(2,1)} %bitcast.201, bf16[1,8,12,64,64]{4,3,2,1,0:T(8,128)(2,1)} %copy-done.29, bf16[1,8,12,64,64]{4,3,2,1,0:T(8,128)(2,1)} %copy-done.31, ...), kind=kOutput, calls=%fused_computation.59 | convolution fusion | flops 1815477760 | bytes 8259584 | tf_op jit(solution)/shard_map/tbhle,dthe->bld/dot_general | solution.py:65
  166.3 1.3 fusion.23
  167.6 63.5 %all-to-all-done.3 = bf16[8,48,3072]{2,1,0:T(8,128)(2,1)S(1)} async-done(((bf16[8,48,3072]{2,1,0:T(8,128)(2,1)}), bf16[8,48,3072]{2,1,0:T(8,128)(2,1)S(1)}, u32[]{:S(2)}, u32[]{:S(2)}) %all-to-all-start.3) | async-done | bytes 2359328 | tf_op jit(solution)/shard_map/all_to_all | solution.py:99
  232.4 1.8 convert_element_type.186
  (91 shorter events, 13.9 us)
Async XLA Ops:
  9.5 1.1 copy-start.5
  9.5 2.2 slice-start
  10.9 0.6 copy-start.25
  11.8 3.6 %copy-start.27 = (f32[8,64]{1,0:T(8,128)}, f32[8,64]{1,0:T(8,128)S(1)}, u32[]{:S(2)}) copy-start(f32[8,64]{1,0:T(8,128)S(1)} %fusion.71) | copy-start | bytes 6148
  21.2 5.6 %copy-start.2 = (bf16[3,8,12,64,64]{4,3,2,0,1:T(8,128)(2,1)}, bf16[3,8,12,64,64]{4,3,2,0,1:T(8,128)(2,1)S(1)}, u32[]{:S(2)}) copy-start(bf16[3,8,12,64,64]{4,3,2,0,1:T(8,128)(2,1)S(1)} %convert_bitcast_fusion) | copy-start | bytes 7077892
  26.8 1.6 copy-start
  26.8 1.7 copy-start.23
  26.8 1.7 copy-start.6
  26.9 2.9 %copy-start.15 = (bf16[768,768]{1,0:T(8,128)(2,1)S(1)}, bf16[768,768]{1,0:T(8,128)(2,1)}, u32[]{:S(2)}) copy-start(bf16[768,768]{1,0:T(8,128)(2,1)} %slice.50) | copy-start | bytes 3538948
  28.5 2.1 copy-start.11
  31.9 26.2 %all-to-all-start = ((bf16[8,64,768]{2,0,1:T(8,128)(2,1)}), bf16[8,64,768]{2,0,1:T(8,128)(2,1)}, u32[]{:S(2)}, u32[]{:S(2)}) async-start(bf16[8,64,768]{2,0,1:T(8,128)(2,1)} %copy.142), calls=%async_computation | async-start | bytes 1572864 | tf_op jit(solution)/shard_map/all_to_all | solution.py:107
  41.8 2.0 slice-start.1
  47.5 16.8 %copy-start.3 = (bf16[768,2304]{0,1:T(8,128)(2,1)S(1)}, bf16[768,2304]{0,1:T(8,128)(2,1)}, u32[]{:S(2)}) copy-start(bf16[768,2304]{0,1:T(8,128)(2,1)} %copy.147) | copy-start | bytes 10616836
  67.9 8.1 %copy-start.17 = (bf16[3,4,12,128,64]{3,4,2,0,1:T(8,128)(2,1)}, bf16[3,4,12,128,64]{3,4,2,0,1:T(8,128)(2,1)S(1)}, u32[]{:S(2)}) copy-start(bf16[3,4,12,128,64]{3,4,2,0,1:T(8,128)(2,1)S(1)} %convert_bitcast_fusion.1) | copy-start | bytes 7077892
  68.6 3.1 %copy-start.21 = (bf16[4,12,128,64]{2,3,0,1:T(8,128)(2,1)S(1)}, bf16[4,12,128,64]{2,3,0,1:T(8,128)(2,1)}, u32[]{:S(2)}) copy-start(bf16[4,12,128,64]{2,3,0,1:T(8,128)(2,1)} %fusion.48) | copy-start | bytes 2359300
  79.2 2.9 %copy-start.18 = (bf16[1,4,12,128,64]{3,4,2,1,0:T(8,128)(2,1)S(1)}, bf16[1,4,12,128,64]{3,4,2,1,0:T(8,128)(2,1)}, u32[]{:S(2)}) copy-start(bf16[1,4,12,128,64]{3,4,2,1,0:T(8,128)(2,1)} %fusion.50) | copy-start | bytes 2359300
  79.2 2.9 %copy-start.19 = (bf16[1,4,12,128,64]{3,4,2,1,0:T(8,128)(2,1)S(1)}, bf16[1,4,12,128,64]{3,4,2,1,0:T(8,128)(2,1)}, u32[]{:S(2)}) copy-start(bf16[1,4,12,128,64]{3,4,2,1,0:T(8,128)(2,1)} %fusion.49) | copy-start | bytes 2359300
  82.1 3.7 %copy-start.4 = (bf16[1,4,12,128,64]{3,4,2,1,0:T(8,128)(2,1)}, bf16[1,4,12,128,64]{3,4,2,1,0:T(8,128)(2,1)S(1)}, u32[]{:S(2)}) copy-start(bf16[1,4,12,128,64]{3,4,2,1,0:T(8,128)(2,1)S(1)} %fusion.47) | copy-start | bytes 2359300
  82.1 3.6 %copy-start.20 = (bf16[128,4,768]{2,1,0:T(4,128)(2,1)S(1)}, bf16[128,4,768]{2,1,0:T(4,128)(2,1)}, u32[]{:S(2)}) copy-start(bf16[128,4,768]{2,1,0:T(4,128)(2,1)} %param.5) | copy-start | bytes 2359300
  87.3 7.1 %copy-start.24 = (f32[8,12,64]{2,1,0:T(8,128)S(1)}, f32[8,12,64]{2,1,0:T(8,128)}, u32[]{:S(2)}) copy-start(f32[8,12,64]{2,1,0:T(8,128)} %copy-done.23) | copy-start | bytes 73732
  88.9 24.8 %all-to-all-start.1 = ((bf16[128,4,768]{2,1,0:T(4,128)(2,1)}), bf16[128,4,768]{2,1,0:T(4,128)(2,1)S(1)}, u32[]{:S(2)}, u32[]{:S(2)}) async-start(bf16[128,4,768]{2,1,0:T(4,128)(2,1)} %copy.155), calls=%async_computation.1 | async-start | bytes 1572864 | tf_op jit(solution)/shard_map/all_to_all | solution.py:114
  94.4 138.1 %reduce-scatter.2.cloned.1.call-start = ((), (), s32[]{:S(2)}) async-start(), calls=%async_computation.5 | async-start | bytes 5013504 | tf_op jit(solution)/shard_map/reduce_scatter | solution.py:111
  101.1 2.0 copy-start.12
  106.6 4.2 %copy-start.14 = (bf16[12,64,768]{2,1,0:T(8,128)(2,1)S(1)}, bf16[12,64,768]{2,1,0:T(8,128)(2,1)}, u32[]{:S(2)}) copy-start(bf16[12,64,768]{2,1,0:T(8,128)(2,1)} %bitcast_convert_fusion.2) | copy-start | bytes 3538948
  113.7 1.5 copy-start.16
  115.3 2.5 %copy-start.9 = (bf16[8,64,768]{2,1,0:T(8,128)(2,1)S(1)}, bf16[8,64,768]{2,1,0:T(8,128)(2,1)}, u32[]{:S(2)}) copy-start(bf16[8,64,768]{2,1,0:T(8,128)(2,1)} %all_to_all.30) | copy-start | bytes 2359300
  115.3 2.5 %copy-start.22 = (bf16[768,8,64]{0,2,1:T(8,128)(2,1)S(1)}, bf16[768,8,64]{0,2,1:T(8,128)(2,1)}, u32[]{:S(2)}) copy-start(bf16[768,8,64]{0,2,1:T(8,128)(2,1)} %dot_general.96) | copy-start | bytes 2359300
  117.8 4.4 %copy-start.1 = (f32[8,12,64,64]{2,3,1,0:T(8,128)S(1)}, f32[8,12,64,64]{2,3,1,0:T(8,128)}, u32[]{:S(2)}) copy-start(f32[8,12,64,64]{2,3,1,0:T(8,128)} %copy-done) | copy-start | bytes 4718596
  122.2 2.2 copy-start.13
  124.4 8.5 %copy-start.29 = (bf16[1,8,12,64,64]{4,3,2,1,0:T(8,128)(2,1)}, bf16[1,8,12,64,64]{4,3,2,1,0:T(8,128)(2,1)S(1)}, u32[]{:S(2)}) copy-start(bf16[1,8,12,64,64]{4,3,2,1,0:T(8,128)(2,1)S(1)} %fusion.38) | copy-start | bytes 2359300
  129.9 3.1 %copy-start.31 = (bf16[1,8,12,64,64]{4,3,2,1,0:T(8,128)(2,1)}, bf16[1,8,12,64,64]{4,3,2,1,0:T(8,128)(2,1)S(1)}, u32[]{:S(2)}) copy-start(bf16[1,8,12,64,64]{4,3,2,1,0:T(8,128)(2,1)S(1)} %fusion.37) | copy-start | bytes 2359300
  129.9 3.1 %copy-start.7 = (bf16[8,64,768]{2,1,0:T(8,128)(2,1)S(1)}, bf16[8,64,768]{2,1,0:T(8,128)(2,1)}, u32[]{:S(2)}) copy-start(bf16[8,64,768]{2,1,0:T(8,128)(2,1)} %param.4) | copy-start | bytes 2359300
  129.9 3.1 %copy-start.28 = (f32[8,64]{1,0:T(8,128)S(1)}, f32[8,64]{1,0:T(8,128)}, u32[]{:S(2)}) copy-start(f32[8,64]{1,0:T(8,128)} %copy-done.27) | copy-start | bytes 6148
  133.0 4.0 %copy-start.30 = (bf16[1,8,12,64,64]{4,3,2,1,0:T(8,128)(2,1)}, bf16[1,8,12,64,64]{4,3,2,1,0:T(8,128)(2,1)S(1)}, u32[]{:S(2)}) copy-start(bf16[1,8,12,64,64]{4,3,2,1,0:T(8,128)(2,1)S(1)} %fusion.36) | copy-start | bytes 2359300
  153.5 6.0 %copy-start.8 = (bf16[8,64,768]{2,1,0:T(8,128)(2,1)S(1)}, bf16[8,64,768]{2,1,0:T(8,128)(2,1)}, u32[]{:S(2)}) copy-start(bf16[8,64,768]{2,1,0:T(8,128)(2,1)} %param.4) | copy-start | bytes 2359300
  153.5 77.6 %all-to-all-start.3 = ((bf16[8,48,3072]{2,1,0:T(8,128)(2,1)}), bf16[8,48,3072]{2,1,0:T(8,128)(2,1)S(1)}, u32[]{:S(2)}, u32[]{:S(2)}) async-start(bf16[8,48,3072]{2,1,0:T(8,128)(2,1)} %fusion.18), calls=%async_computation.3 | async-start | bytes 4718592 | tf_op jit(solution)/shard_map/all_to_all | solution.py:99
  159.5 6.8 %copy-start.26 = (f32[8,64]{1,0:T(8,128)S(1)}, f32[8,64]{1,0:T(8,128)}, u32[]{:S(2)}) copy-start(f32[8,64]{1,0:T(8,128)} %copy-done.25) | copy-start | bytes 6148
  159.5 6.8 %copy-start.10 = (bf16[8,64,768]{2,1,0:T(8,128)(2,1)S(1)}, bf16[8,64,768]{2,1,0:T(8,128)(2,1)}, u32[]{:S(2)}) copy-start(bf16[8,64,768]{2,1,0:T(8,128)(2,1)} %all_to_all.30) | copy-start | bytes 2359300
Sparse Core Ops, SparseCore 0:
  113.8 118.5 reduce-scatter.1

commit v6 on v0

--- a/solution.py
+++ b/solution.py
@@ -82,6 +82,32 @@
     return jnp.concatenate([first, second], axis=1)
 
 
+def swap_sum(parts, axis_name, groups):
+    received = lax.all_to_all(parts, axis_name, split_axis=0, concat_axis=0, axis_index_groups=groups, tiled=True)
+    total = received[0].astype(jnp.float32)
+    for part in range(1, received.shape[0]):
+        total = total + received[part].astype(jnp.float32)
+    return total
+
+
+def staged_scatter(term, axis_name):
+    count = lax.axis_size(axis_name)
+    if count % 4:
+        return lax.psum_scatter(
+            term.astype(jnp.bfloat16), axis_name, scatter_dimension=0, tiled=True
+        ).astype(jnp.float32)
+    block = term.shape[0] // count
+    rest = term.shape[1:]
+    sent = lax.optimization_barrier(term.astype(jnp.bfloat16))
+    blocks = sent.reshape((count // 4, 2, 2, block) + rest)
+    couples = [[low, low + 1] for low in range(0, count, 2)]
+    first = swap_sum(jnp.moveaxis(blocks, 2, 0), axis_name, couples).astype(jnp.bfloat16)
+    neighbours = [[low, low + 2] for low in range(count) if not (low >> 1) & 1]
+    second = swap_sum(jnp.moveaxis(first, 1, 0), axis_name, neighbours).astype(jnp.bfloat16)
+    others = [[high * 4 + low for high in range(count // 4)] for low in range(4)]
+    return swap_sum(second, axis_name, others)
+
+
 def body(cells, cotangent, row_weight, col_weight):
     row_saved = forward(cells, row_weight, 1, True)
     mid_columns = lax.all_to_all(row_saved[4], "cell", split_axis=1, concat_axis=0, tiled=True)
@@ -94,9 +120,7 @@
     grad_mid = lax.all_to_all(grad_mid_columns, "cell", split_axis=0, concat_axis=1, tiled=True)
     grad_cells, grad_row_proj = backward(row_saved, row_weight, grad_mid, 1)
     row_term = weight_term(row_saved[1], grad_row_proj, row_saved[3], grad_mid, 1)
-    row_grad = lax.psum_scatter(
-        row_term.astype(jnp.bfloat16), "cell", scatter_dimension=0, tiled=True
-    ).astype(jnp.float32)
+    row_grad = staged_scatter(row_term, "cell")
     return (grad_cells, row_grad, col_grad)
 
 

time: 272 us -> 234 us (0.86)
  waiting for transfers between devices: 109 us -> 27.9 us
  blocking collectives: 0 us -> 43.2 us
  local copies, waits for them, and re-layouts: 45.9 us -> 41.2 us
  starting transfers between devices: 13.2 us -> 17.5 us
    reduce_scatter x1 -> x0, waiting for transfers between devices: 77.2 us -> none  [body(): lax.psum_scatter(row_term.astype(jnp.bfloat16), 'cell', scatter_dimension...]
    all_to_all x0 -> x2, blocking collectives: none -> 43.2 us  [swap_sum(): lax.all_to_all(parts, axis_name, split_axis=0, concat_axis=0, axis_index_...]
    all_to_all x0 -> x1, waiting for transfers between devices: none -> 20.6 us  [swap_sum(): lax.all_to_all(parts, axis_name, split_axis=0, concat_axis=0, axis_index_...]
    all_to_all x1, waiting for transfers between devices: 13.1 us -> 0.01 us  [body(): lax.all_to_all(grad_mid_columns, 'cell', split_axis=0, concat_axis=1, til...]
    reduce_scatter x1, waiting for transfers between devices: 11.3 us -> 0.01 us  [body(): lax.psum_scatter(col_term.astype(jnp.bfloat16), 'cell', scatter_dimension...]
    unnamed x82 -> x64, local copies, waits for them, and re-layouts: 11.5 us -> 3.95 us
    all_to_all x0 -> x1, starting transfers between devices: none -> 4.6 us  [swap_sum(): lax.all_to_all(parts, axis_name, split_axis=0, concat_axis=0, axis_index_...]
  transfers between devices with their start and end apart: 4 -> 4, of which waited for: 4 -> 2; matrix products, arithmetic and copies ran while one was open for 19% -> 30% of each run, Pallas kernels for 0% -> 0%
where the time goes in v6:
time: 234 us; the launch traced here: 232 us
  matrix products  61.9 us (26%)
  blocking collectives  43.2 us (18%)
  local copies, waits for them, and re-layouts  41.2 us (18%)
  waiting for transfers between devices  27.9 us (12%)
  other arithmetic  25.9 us (11%)
  starting transfers between devices  17.5 us (7%)
  between operations  14.6 us (6%)
    all_to_all x2, blocking collectives, swap_sum(): lax.all_to_all(parts, axis_name, split_axis=0, concat_axis=0, axis_index_...  43.2 us
    all_to_all x1, waiting for transfers between devices, swap_sum(): lax.all_to_all(parts, axis_name, split_axis=0, concat_axis=0, axis_index_...  20.6 us
    dot_general x5, matrix products, attend_heads(): jnp.einsum('bhlm,bhme->bhle', weights, values_part, preferred_element_typ...  11.1 us
    dot_general x6, matrix products, attend_heads(): jnp.einsum('bhle,bhme->bhlm', queries, keys_part, preferred_element_type=...  10.7 us
    dot_general x2, matrix products, backward(): jnp.einsum('tbhle,dthe->' + cell_form, grad_projected, projection, prefer...  10.2 us
    slice x6, local copies, waits for them, and re-layouts, split_weight(): weight[:, :3 * model_width].reshape(model_width, 3, HEADS, head_size)  9.51 us
    dot_general x2, matrix products, forward(): jnp.einsum(cell_form + ',dthe->tbhle', normed, projection, preferred_elem...  9.47 us
    dot_general x2, matrix products, weight_term(): jnp.einsum(cell_form + ',tbhle->dthe', normed, grad_projected, preferred_...  8.2 us
  transfers between devices with their start and end apart: 4, of which 2 were waited for; matrix products, arithmetic and copies ran while one was open for 30% of the time, Pallas kernels for 0%

profile of v6, /device:TPU:0, one launch (start us, length us, event | category | flops | bytes accessed | tf_op | source)
XLA Modules:
  0.0 232.3 jit_solution(8963608945354688318)
XLA Ops:
  7.2 2.4 %slice.68 = bf16[768,768]{1,0:T(8,128)(2,1)} slice(bf16[768,3072]{1,0:T(8,128)(2,1)} %param.6), slice={[0:768], [2304:3072]} | slice | bytes 2359296 | tf_op jit(solution)/shard_map/slice | solution.py:34
  11.8 3.6 %copy.143 = bf16[768,2304]{0,1:T(8,128)(2,1)} copy(bf16[768,2304]{1,0:T(8,128)(2,1)S(1)} %slice-done) | data formatting | bytes 7077888 | tf_op jit(solution)/shard_map/slice | solution.py:33
  15.3 5.8 %convert_bitcast_fusion = bf16[3,8,12,64,64]{4,3,2,0,1:T(8,128)(2,1)S(1)} fusion(bf16[768,3,12,64,1]{0,3,2,1,4:T(8,128)(2,1)} %bitcast.206, bf16[8,64,768]{2,1,0:T(8,128)(2,1)} %param.4, f32[8,64]{1,0:T(8,128)S(1)} %fusion.72), kind=kOutput, calls=%fused_computation.8 | convolution fusion | flops 1814298624 | bytes 6686720 | tf_op jit(solution)/shard_map/bld,dthe->tbhle/dot_general | solution.py:43
  22.1 4.7 %fusion.84 = (f32[8,12,64]{2,1,0:T(8,128)S(1)}, f32[8,12,64,64]{2,3,1,0:T(8,128)S(1)}) fusion(f32[8,12,64,64]{2,3,1,0:T(8,128)S(1)} %fusion.44), kind=kOutput, calls=%fused_computation.128 | output fusion | flops 1572927 | bytes 3170304 | tf_op jit(solution)/shard_map/sub | solution.py:21
  31.9 7.4 %all-to-all-start = ((bf16[8,64,768]{2,0,1:T(8,128)(2,1)}), bf16[8,64,768]{2,0,1:T(8,128)(2,1)}, u32[]{:S(2)}, u32[]{:S(2)}) async-start(bf16[8,64,768]{2,0,1:T(8,128)(2,1)} %copy.145), calls=%async_computation | async-start | bytes 1572864 | tf_op jit(solution)/shard_map/all_to_all | solution.py:113
  39.3 2.5 %slice.63 = bf16[768,768]{1,0:T(8,128)(2,1)} slice(bf16[768,3072]{1,0:T(8,128)(2,1)} %param.7), slice={[0:768], [2304:3072]} | slice | bytes 2359296 | tf_op jit(solution)/shard_map/slice | solution.py:34
  41.8 2.0 slice-done.1
  43.8 3.7 %copy.150 = bf16[768,2304]{0,1:T(8,128)(2,1)} copy(bf16[768,2304]{1,0:T(8,128)(2,1)S(1)} %slice-done.1) | data formatting | bytes 7077888 | tf_op jit(solution)/shard_map/slice | solution.py:33
  47.5 3.4 %fusion.48 = bf16[4,12,128,64]{2,3,0,1:T(8,128)(2,1)} fusion(bf16[12,64,768,1]{2,1,3,0:T(8,128)(2,1)} %bitcast.217, bf16[128,4,768]{2,1,0:T(4,128)(2,1)} %param.5), kind=kOutput, calls=%fused_computation.89 | convolution fusion | flops 604372992 | bytes 2752512 | tf_op jit(solution)/shard_map/lbf,hef->bhle/dot_general | solution.py:60
  50.8 7.3 %all-to-all-done = bf16[8,64,768]{2,0,1:T(8,128)(2,1)} async-done(((bf16[8,64,768]{2,0,1:T(8,128)(2,1)}), bf16[8,64,768]{2,0,1:T(8,128)(2,1)}, u32[]{:S(2)}, u32[]{:S(2)}) %all-to-all-start) | async-done | bytes 786464 | tf_op jit(solution)/shard_map/all_to_all | solution.py:113
  58.1 2.0 multiply_reduce_fusion.2
  60.1 1.4 copy.147
  61.5 1.3 multiply_add_fusion
  62.8 1.4 copy.148
  64.2 3.6 %convert_bitcast_fusion.1 = bf16[3,4,12,128,64]{3,4,2,0,1:T(8,128)(2,1)S(1)} fusion(bf16[768,3,12,64,1]{0,3,2,1,4:T(8,128)(2,1)S(1)} %bitcast.208, f32[16,8,4]{1,2,0:T(4,128)} %copy.148, bf16[8,64,768]{2,0,1:T(8,128)(2,1)} %all-to-all-done), kind=kOutput, calls=%fused_computation.43 | convolution fusion | flops 1814298624 | bytes 6686720 | tf_op jit(solution)/shard_map/lbd,dthe->tbhle/dot_general | solution.py:43
  68.5 3.0 %fusion.85 = (f32[4,12,128]{2,1,0:T(8,128)S(1)}, f32[4,12,128,128]{2,3,1,0:T(8,128)S(1)}) fusion(f32[4,12,128,128]{2,3,1,0:T(8,128)S(1)} %fusion.65), kind=kOutput, calls=%fused_computation.129 | output fusion | flops 3145855 | bytes 6316032 | tf_op jit(solution)/shard_map/jvp()/sub | solution.py:21
  71.6 2.2 fusion.6
  73.9 2.1 fusion.50
  75.9 1.7 fusion.49
  79.2 2.9 %fusion.47 = bf16[1,4,12,128,64]{3,4,2,1,0:T(8,128)(2,1)S(1)} fusion(bf16[4,12,128,128]{2,3,1,0:T(8,128)(2,1)} %get-tuple-element.4, bf16[4,12,128,64]{2,3,0,1:T(8,128)(2,1)} %fusion.48), kind=kOutput, calls=%fused_computation.88 | convolution fusion | flops 101056512 | bytes 3145728 | tf_op jit(solution)/shard_map/transpose(jvp(bhlm,bhme->bhle))/dot_general | solution.py:22
  82.1 3.6 %fusion.32 = (f32[128,4]{0,1:T(4,128)S(1)}, f32[4,128,768,1,1]{2,1,3,0,4:T(8,128)S(1)}) fusion(bf16[768,3,12,64,1]{0,3,2,4,1:T(8,128)(2,1)S(1)} %bitcast.209, bf16[1,4,12,128,64]{3,4,2,1,0:T(8,128)(2,1)S(1)} %fusion.47, bf16[1,4,12,128,64]{3,4,2,1,0:T(8,128)(2,1)S(1)} %copy-done.18, bf16[1,4,12,128,64]{3,4,2,1,0:T(8,128)(2,1)S(1)} %copy-done.19, ...), kind=kOutput, calls=%fused_computation.70 | convolution fusion | flops 1815477760 | bytes 8259584 | tf_op jit(solution)/shard_map/tbhle,dthe->lbd/dot_general | solution.py:65
  85.8 1.5 fusion.21
  87.3 1.5 copy.158
  88.9 5.5 %all-to-all-start.1 = ((bf16[128,4,768]{2,1,0:T(4,128)(2,1)}), bf16[128,4,768]{2,1,0:T(4,128)(2,1)S(1)}, u32[]{:S(2)}, u32[]{:S(2)}) async-start(bf16[128,4,768]{2,1,0:T(4,128)(2,1)} %copy.158), calls=%async_computation.1 | async-start | bytes 1572864 | tf_op jit(solution)/shard_map/all_to_all | solution.py:120
  94.4 2.5 %copy.162 = bf16[12,64,8,64]{1,0,3,2:T(8,128)(2,1)S(1)} copy(bf16[12,64,8,64]{1,3,0,2:T(8,128)(2,1)} %bitcast.213) | data formatting | bytes 1572864 | tf_op jit(solution)/shard_map/convert_element_type | solution.py:23
  96.9 2.3 dot_general.96
  99.2 1.9 fusion.52
  101.0 2.0 copy.167
  103.0 3.6 %bitcast_convert_fusion.2 = bf16[12,64,768]{2,1,0:T(8,128)(2,1)} fusion(bf16[4,12,128,128]{2,3,1,0:T(8,128)(2,1)S(1)} %copy-done.12, bf16[128,4,768]{2,1,0:T(4,128)(2,1)} %param.5, bf16[3,4,12,128,64]{3,4,2,0,1:T(8,128)(2,1)} %copy-done.17), kind=kOutput, calls=%fused_computation.40 | convolution fusion | flops 705626112 | bytes 4325376 | tf_op jit(solution)/shard_map/bhle,lbf->hef/dot_general | solution.py:79
  106.6 4.2 %bitcast_convert_fusion.1 = bf16[768,2304]{1,0:T(8,128)(2,1)S(1)} fusion(bf16[2304,4,128]{2,0,1:T(8,128)(2,1)} %bitcast.212, f32[128,4]{0,1:T(4,128)S(1)} %get-tuple-element.7, bf16[8,64,768]{2,0,1:T(8,128)(2,1)} %all-to-all-done), kind=kOutput, calls=%fused_computation.3 | convolution fusion | flops 1814888448 | bytes 6686720 | tf_op jit(solution)/shard_map/lbd,tbhle->dthe/dot_general | solution.py:76
  110.9 2.8 %pad_maximum_fusion.2 = bf16[768,3072]{1,0:T(8,128)(2,1)} fusion(bf16[768,768]{1,0:T(8,128)(2,1)S(1)} %bitcast.214, bf16[768,2304]{1,0:T(8,128)(2,1)S(1)} %bitcast_convert_fusion.1), kind=kLoop, calls=%fused_computation.6 | loop fusion | flops 9437184 | bytes 9437184 | tf_op jit(solution)/shard_map/concatenate | solution.py:82
  115.3 2.5 %convolution_convert_fusion = bf16[8,64,12,64]{3,1,2,0:T(8,128)(2,1)} fusion(bf16[12,64,768,1]{2,1,0,3:T(8,128)(2,1)S(1)} %bitcast.216, bf16[8,64,768,1]{2,1,0,3:T(8,128)(2,1)S(1)} %reshape.143), kind=kOutput, calls=%fused_computation.45 | convolution fusion | flops 604372992 | bytes 2752512 | tf_op jit(solution)/shard_map/blf,hef->bhle/dot_general | solution.py:60
  117.8 1.9 bitcast_convert_fusion.3
  119.7 2.5 %copy.164 = bf16[768,768]{1,0:T(8,128)(2,1)} copy(bf16[768,768]{0,1:T(8,128)(2,1)} %bitcast_convert_fusion.3) | data formatting | bytes 2359296 | tf_op jit(solution)/shard_map/convert.9
  122.2 2.2 fusion.38
  124.5 3.1 %fusion.11 = (f32[8,12,64]{2,1,0:T(8,128)S(1)}, bf16[8,12,64,64]{2,3,1,0:T(8,128)(2,1)S(1)}) fusion(f32[8,12,64,64]{2,3,1,0:T(8,128)S(1)} %copy-done.1, f32[8,12,64]{2,1,0:T(8,128)S(1)} %multiply_divide_fusion, bf16[3,8,12,64,64]{4,3,2,0,1:T(8,128)(2,1)} %copy-done.2, bf16[8,64,12,64]{3,1,2,0:T(8,128)(2,1)S(1)} %copy-done.13), kind=kOutput, calls=%fused_computation.22 | convolution fusion | flops 52291584 | bytes 4767744 | tf_op jit(solution)/shard_map/transpose(jvp(bhlm,bhme->bhle))/dot_general | solution.py:22
  127.6 2.4 %fusion.37 = bf16[1,8,12,64,64]{4,3,2,1,0:T(8,128)(2,1)S(1)} fusion(bf16[3,8,12,64,64]{4,3,2,0,1:T(8,128)(2,1)} %copy-done.2, f32[8,12,64,64]{2,3,1,0:T(8,128)S(1)} %copy-done.1, bf16[8,12,64,64]{2,3,1,0:T(8,128)(2,1)S(1)} %get-tuple-element.17, f32[8,12,64]{2,1,0:T(8,128)S(1)} %neg.13, f32[8,12,64]{2,1,0:T(8,128)S(1)} %copy-done.24), kind=kOutput, calls=%fused_computation.80 | convolution fusion | flops 52690944 | bytes 4767744 | tf_op jit(solution)/shard_map/transpose(jvp(bhle,bhme->bhlm))/dot_general | solution.py:18
  130.0 3.0 %fusion.36 = bf16[1,8,12,64,64]{4,3,2,1,0:T(8,128)(2,1)S(1)} fusion(bf16[3,8,12,64,64]{4,3,2,0,1:T(8,128)(2,1)} %copy-done.2, f32[8,12,64,64]{2,3,1,0:T(8,128)S(1)} %copy-done.1, bf16[8,12,64,64]{2,3,1,0:T(8,128)(2,1)S(1)} %get-tuple-element.17, f32[8,12,64]{2,1,0:T(8,128)S(1)} %neg.13, f32[8,12,64]{2,1,0:T(8,128)S(1)} %copy-done.24), kind=kOutput, calls=%fused_computation.79 | convolution fusion | flops 52690944 | bytes 4767744 | tf_op jit(solution)/shard_map/transpose(jvp(bhle,bhme->bhlm))/dot_general | solution.py:18
  133.0 4.0 %bitcast_convert_fusion = bf16[768,3,12,64]{0,3,2,1:T(8,128)(2,1)} fusion(bf16[1,8,12,64,64]{4,3,2,1,0:T(8,128)(2,1)S(1)} %fusion.38, bf16[1,8,12,64,64]{4,3,2,1,0:T(8,128)(2,1)S(1)} %fusion.37, bf16[1,8,12,64,64]{4,3,2,1,0:T(8,128)(2,1)S(1)} %fusion.36, bf16[8,64,768]{2,1,0:T(8,128)(2,1)S(1)} %copy-done.7, f32[8,64]{1,0:T(8,128)S(1)} %copy-done.28), kind=kOutput, calls=%fused_computation.2 | convolution fusion | flops 1821966336 | bytes 6686720 | tf_op jit(solution)/shard_map/bld,tbhle->dthe/dot_general | solution.py:76
  137.0 4.3 %copy.163 = bf16[768,2304]{1,0:T(8,128)(2,1)S(1)} copy(bf16[768,2304]{0,1:T(8,128)(2,1)} %bitcast.210) | data formatting | bytes 7077888 | tf_op jit(solution)/shard_map/reshape | solution.py:78
  141.3 1.9 pad_maximum_fusion.1
  143.6 7.5 %all_to_all.42 = bf16[2,4,2,48,3072]{4,3,2,1,0:T(8,128)(2,1)S(1)} all-to-all(bf16[2,4,2,48,3072]{4,3,2,1,0:T(8,128)(2,1)S(1)} %copy.165), channel_id=1, replica_groups={{0,1},{2,3},{4,5},{6,7},{8,9},{10,11},{12,13},{14,15},{16,17},{18,19},{..., dimensions={0} | all-to-all | bytes 9437184 | tf_op jit(solution)/shard_map/all_to_all | solution.py:86
  152.4 35.7 %all_to_all.43 = bf16[2,4,48,3072]{3,2,1,0:T(8,128)(2,1)S(1)} all-to-all(bf16[2,4,48,3072]{3,2,1,0:T(8,128)(2,1)S(1)} %copy.166), channel_id=1, replica_groups={{0,2},{1,3},{4,6},{5,7},{8,10},{9,11},{12,14},{13,15},{16,18},{17,19},{..., dimensions={0} | all-to-all | bytes 4718592 | tf_op jit(solution)/shard_map/all_to_all | solution.py:86
  188.0 1.5 fusion.51
  189.5 4.6 %all-to-all-start.4 = ((bf16[4,48,3072]{2,1,0:T(8,128)(2,1)}), bf16[4,48,3072]{2,1,0:T(8,128)(2,1)S(1)}, u32[]{:S(2)}, u32[]{:S(2)}) async-start(bf16[4,48,3072]{2,1,0:T(8,128)(2,1)} %fusion.51), calls=%async_computation.4 | async-start | bytes 2359296 | tf_op jit(solution)/shard_map/all_to_all | solution.py:86
  194.1 6.6 %fusion.27 = (f32[8,64]{1,0:T(8,128)S(1)}, f32[8,64,768,1,1]{2,1,3,0,4:T(8,128)S(1)}) fusion(bf16[8,64,768]{2,1,0:T(8,128)(2,1)S(1)} %copy-done.8, bf16[768,3,12,64,1]{0,3,2,4,1:T(8,128)(2,1)} %bitcast.207, bf16[1,8,12,64,64]{4,3,2,1,0:T(8,128)(2,1)} %copy-done.29, bf16[1,8,12,64,64]{4,3,2,1,0:T(8,128)(2,1)} %copy-done.31, ...), kind=kOutput, calls=%fused_computation.59 | convolution fusion | flops 1815477760 | bytes 8259584 | tf_op jit(solution)/shard_map/tbhle,dthe->bld/dot_general | solution.py:65
  202.1 20.6 %all-to-all-done.4 = bf16[4,48,3072]{2,1,0:T(8,128)(2,1)S(1)} async-done(((bf16[4,48,3072]{2,1,0:T(8,128)(2,1)}), bf16[4,48,3072]{2,1,0:T(8,128)(2,1)S(1)}, u32[]{:S(2)}, u32[]{:S(2)}) %all-to-all-start.4) | async-done | bytes 1179680 | tf_op jit(solution)/shard_map/all_to_all | solution.py:86
  223.6 1.8 convert_element_type.220
  (94 shorter events, 16.0 us)
Async XLA Ops:
  9.5 1.1 copy-start.5
  9.5 2.2 slice-start
  10.9 0.6 copy-start.25
  11.8 3.6 %copy-start.27 = (f32[8,64]{1,0:T(8,128)}, f32[8,64]{1,0:T(8,128)S(1)}, u32[]{:S(2)}) copy-start(f32[8,64]{1,0:T(8,128)S(1)} %fusion.72) | copy-start | bytes 6148
  21.2 5.6 %copy-start.2 = (bf16[3,8,12,64,64]{4,3,2,0,1:T(8,128)(2,1)}, bf16[3,8,12,64,64]{4,3,2,0,1:T(8,128)(2,1)S(1)}, u32[]{:S(2)}) copy-start(bf16[3,8,12,64,64]{4,3,2,0,1:T(8,128)(2,1)S(1)} %convert_bitcast_fusion) | copy-start | bytes 7077892
  26.8 1.6 copy-start
  26.8 1.7 copy-start.23
  26.8 1.7 copy-start.6
  26.8 2.9 %copy-start.15 = (bf16[768,768]{1,0:T(8,128)(2,1)S(1)}, bf16[768,768]{1,0:T(8,128)(2,1)}, u32[]{:S(2)}) copy-start(bf16[768,768]{1,0:T(8,128)(2,1)} %slice.68) | copy-start | bytes 3538948
  28.5 2.1 copy-start.11
  31.9 26.2 %all-to-all-start = ((bf16[8,64,768]{2,0,1:T(8,128)(2,1)}), bf16[8,64,768]{2,0,1:T(8,128)(2,1)}, u32[]{:S(2)}, u32[]{:S(2)}) async-start(bf16[8,64,768]{2,0,1:T(8,128)(2,1)} %copy.145), calls=%async_computation | async-start | bytes 1572864 | tf_op jit(solution)/shard_map/all_to_all | solution.py:113
  41.8 2.0 slice-start.1
  47.5 16.8 %copy-start.3 = (bf16[768,2304]{0,1:T(8,128)(2,1)S(1)}, bf16[768,2304]{0,1:T(8,128)(2,1)}, u32[]{:S(2)}) copy-start(bf16[768,2304]{0,1:T(8,128)(2,1)} %copy.150) | copy-start | bytes 10616836
  67.9 8.0 %copy-start.17 = (bf16[3,4,12,128,64]{3,4,2,0,1:T(8,128)(2,1)}, bf16[3,4,12,128,64]{3,4,2,0,1:T(8,128)(2,1)S(1)}, u32[]{:S(2)}) copy-start(bf16[3,4,12,128,64]{3,4,2,0,1:T(8,128)(2,1)S(1)} %convert_bitcast_fusion.1) | copy-start | bytes 7077892
  68.5 3.1 %copy-start.21 = (bf16[4,12,128,64]{2,3,0,1:T(8,128)(2,1)S(1)}, bf16[4,12,128,64]{2,3,0,1:T(8,128)(2,1)}, u32[]{:S(2)}) copy-start(bf16[4,12,128,64]{2,3,0,1:T(8,128)(2,1)} %fusion.48) | copy-start | bytes 2359300
  79.2 2.9 %copy-start.18 = (bf16[1,4,12,128,64]{3,4,2,1,0:T(8,128)(2,1)S(1)}, bf16[1,4,12,128,64]{3,4,2,1,0:T(8,128)(2,1)}, u32[]{:S(2)}) copy-start(bf16[1,4,12,128,64]{3,4,2,1,0:T(8,128)(2,1)} %fusion.50) | copy-start | bytes 2359300
  79.2 2.9 %copy-start.19 = (bf16[1,4,12,128,64]{3,4,2,1,0:T(8,128)(2,1)S(1)}, bf16[1,4,12,128,64]{3,4,2,1,0:T(8,128)(2,1)}, u32[]{:S(2)}) copy-start(bf16[1,4,12,128,64]{3,4,2,1,0:T(8,128)(2,1)} %fusion.49) | copy-start | bytes 2359300
  82.1 3.7 %copy-start.4 = (bf16[1,4,12,128,64]{3,4,2,1,0:T(8,128)(2,1)}, bf16[1,4,12,128,64]{3,4,2,1,0:T(8,128)(2,1)S(1)}, u32[]{:S(2)}) copy-start(bf16[1,4,12,128,64]{3,4,2,1,0:T(8,128)(2,1)S(1)} %fusion.47) | copy-start | bytes 2359300
  82.1 3.6 %copy-start.20 = (bf16[128,4,768]{2,1,0:T(4,128)(2,1)S(1)}, bf16[128,4,768]{2,1,0:T(4,128)(2,1)}, u32[]{:S(2)}) copy-start(bf16[128,4,768]{2,1,0:T(4,128)(2,1)} %param.5) | copy-start | bytes 2359300
  87.3 7.1 %copy-start.24 = (f32[8,12,64]{2,1,0:T(8,128)S(1)}, f32[8,12,64]{2,1,0:T(8,128)}, u32[]{:S(2)}) copy-start(f32[8,12,64]{2,1,0:T(8,128)} %copy-done.23) | copy-start | bytes 73732
  88.9 24.9 %all-to-all-start.1 = ((bf16[128,4,768]{2,1,0:T(4,128)(2,1)}), bf16[128,4,768]{2,1,0:T(4,128)(2,1)S(1)}, u32[]{:S(2)}, u32[]{:S(2)}) async-start(bf16[128,4,768]{2,1,0:T(4,128)(2,1)} %copy.158), calls=%async_computation.1 | async-start | bytes 1572864 | tf_op jit(solution)/shard_map/all_to_all | solution.py:120
  94.3 129.3 %reduce-scatter.2.cloned.1.call-start = ((), (), s32[]{:S(2)}) async-start(), calls=%async_computation.6 | async-start | bytes 5013504 | tf_op jit(solution)/shard_map/reduce_scatter | solution.py:117
  101.0 2.0 copy-start.12
  106.6 4.2 %copy-start.14 = (bf16[12,64,768]{2,1,0:T(8,128)(2,1)S(1)}, bf16[12,64,768]{2,1,0:T(8,128)(2,1)}, u32[]{:S(2)}) copy-start(bf16[12,64,768]{2,1,0:T(8,128)(2,1)} %bitcast_convert_fusion.2) | copy-start | bytes 3538948
  113.7 1.5 copy-start.16
  115.3 2.5 %copy-start.9 = (bf16[8,64,768]{2,1,0:T(8,128)(2,1)S(1)}, bf16[8,64,768]{2,1,0:T(8,128)(2,1)}, u32[]{:S(2)}) copy-start(bf16[8,64,768]{2,1,0:T(8,128)(2,1)} %all_to_all.33) | copy-start | bytes 2359300
  115.3 2.5 %copy-start.22 = (bf16[768,8,64]{0,2,1:T(8,128)(2,1)S(1)}, bf16[768,8,64]{0,2,1:T(8,128)(2,1)}, u32[]{:S(2)}) copy-start(bf16[768,8,64]{0,2,1:T(8,128)(2,1)} %dot_general.96) | copy-start | bytes 2359300
  117.8 4.4 %copy-start.1 = (f32[8,12,64,64]{2,3,1,0:T(8,128)S(1)}, f32[8,12,64,64]{2,3,1,0:T(8,128)}, u32[]{:S(2)}) copy-start(f32[8,12,64,64]{2,3,1,0:T(8,128)} %copy-done) | copy-start | bytes 4718596
  122.2 2.2 copy-start.13
  124.5 8.5 %copy-start.29 = (bf16[1,8,12,64,64]{4,3,2,1,0:T(8,128)(2,1)}, bf16[1,8,12,64,64]{4,3,2,1,0:T(8,128)(2,1)S(1)}, u32[]{:S(2)}) copy-start(bf16[1,8,12,64,64]{4,3,2,1,0:T(8,128)(2,1)S(1)} %fusion.38) | copy-start | bytes 2359300
  129.9 3.1 %copy-start.31 = (bf16[1,8,12,64,64]{4,3,2,1,0:T(8,128)(2,1)}, bf16[1,8,12,64,64]{4,3,2,1,0:T(8,128)(2,1)S(1)}, u32[]{:S(2)}) copy-start(bf16[1,8,12,64,64]{4,3,2,1,0:T(8,128)(2,1)S(1)} %fusion.37) | copy-start | bytes 2359300
  129.9 3.1 %copy-start.7 = (bf16[8,64,768]{2,1,0:T(8,128)(2,1)S(1)}, bf16[8,64,768]{2,1,0:T(8,128)(2,1)}, u32[]{:S(2)}) copy-start(bf16[8,64,768]{2,1,0:T(8,128)(2,1)} %param.4) | copy-start | bytes 2359300
  129.9 3.1 %copy-start.28 = (f32[8,64]{1,0:T(8,128)S(1)}, f32[8,64]{1,0:T(8,128)}, u32[]{:S(2)}) copy-start(f32[8,64]{1,0:T(8,128)} %copy-done.27) | copy-start | bytes 6148
  133.0 4.0 %copy-start.30 = (bf16[1,8,12,64,64]{4,3,2,1,0:T(8,128)(2,1)}, bf16[1,8,12,64,64]{4,3,2,1,0:T(8,128)(2,1)S(1)}, u32[]{:S(2)}) copy-start(bf16[1,8,12,64,64]{4,3,2,1,0:T(8,128)(2,1)S(1)} %fusion.36) | copy-start | bytes 2359300
  188.0 6.1 %copy-start.8 = (bf16[8,64,768]{2,1,0:T(8,128)(2,1)S(1)}, bf16[8,64,768]{2,1,0:T(8,128)(2,1)}, u32[]{:S(2)}) copy-start(bf16[8,64,768]{2,1,0:T(8,128)(2,1)} %param.4) | copy-start | bytes 2359300
  189.5 33.1 %all-to-all-start.4 = ((bf16[4,48,3072]{2,1,0:T(8,128)(2,1)}), bf16[4,48,3072]{2,1,0:T(8,128)(2,1)S(1)}, u32[]{:S(2)}, u32[]{:S(2)}) async-start(bf16[4,48,3072]{2,1,0:T(8,128)(2,1)} %fusion.51), calls=%async_computation.4 | async-start | bytes 2359296 | tf_op jit(solution)/shard_map/all_to_all | solution.py:86
  194.1 6.6 %copy-start.26 = (f32[8,64]{1,0:T(8,128)S(1)}, f32[8,64]{1,0:T(8,128)}, u32[]{:S(2)}) copy-start(f32[8,64]{1,0:T(8,128)} %copy-done.25) | copy-start | bytes 6148
  194.1 6.6 %copy-start.10 = (bf16[8,64,768]{2,1,0:T(8,128)(2,1)S(1)}, bf16[8,64,768]{2,1,0:T(8,128)(2,1)}, u32[]{:S(2)}) copy-start(bf16[8,64,768]{2,1,0:T(8,128)(2,1)} %all_to_all.33) | copy-start | bytes 2359300
Sparse Core Ops, SparseCore 0:
  113.9 81.0 reduce-scatter.1

commit v7 on v6

--- a/solution.py
+++ b/solution.py
@@ -101,9 +101,13 @@
     sent = lax.optimization_barrier(term.astype(jnp.bfloat16))
     blocks = sent.reshape((count // 4, 2, 2, block) + rest)
     couples = [[low, low + 1] for low in range(0, count, 2)]
-    first = swap_sum(jnp.moveaxis(blocks, 2, 0), axis_name, couples).astype(jnp.bfloat16)
-    neighbours = [[low, low + 2] for low in range(count) if not (low >> 1) & 1]
-    second = swap_sum(jnp.moveaxis(first, 1, 0), axis_name, neighbours).astype(jnp.bfloat16)
+    first = swap_sum(jnp.moveaxis(blocks, 2, 0), axis_name, couples)
+    index = lax.axis_index(axis_name)
+    mine = (index >> 1) & 1
+    keep = lax.dynamic_index_in_dim(first, mine, axis=1, keepdims=False)
+    send = lax.dynamic_index_in_dim(first, 1 - mine, axis=1, keepdims=False)
+    received = lax.ppermute(send.astype(jnp.bfloat16), axis_name, perm=[(i, i ^ 2) for i in range(count)])
+    second = (keep + received.astype(jnp.float32)).astype(jnp.bfloat16)
     others = [[high * 4 + low for high in range(count // 4)] for low in range(4)]
     return swap_sum(second, axis_name, others)
 

time: 234 us -> 234 us (level)
  blocking collectives: 43.2 us -> 7.52 us
  waiting for transfers between devices: 27.9 us -> 61.5 us
  matrix products: 61.9 us -> 58.7 us
    all_to_all x2 -> x1, blocking collectives: 43.2 us -> 7.52 us  [swap_sum(): lax.all_to_all(parts, axis_name, split_axis=0, concat_axis=0, axis_index_...]
    ppermute x0 -> x1, waiting for transfers between devices: none -> 34.1 us  [staged_scatter(): lax.ppermute(send.astype(jnp.bfloat16), axis_name, perm=[(i, i ^ 2) for i...]
    unnamed x64 -> x66, local copies, waits for them, and re-layouts: 3.95 us -> 7.71 us
    dot_general x2, matrix products: 8.2 us -> 11.1 us  [weight_term(): jnp.einsum(cell_form + ',tbhle->dthe', normed, grad_projected, preferred_...]
    dot_general x5, matrix products: 11.1 us -> 8.53 us  [attend_heads(): jnp.einsum('bhlm,bhme->bhle', weights, values_part, preferred_element_typ...]
  transfers between devices with their start and end apart: 4 -> 5, of which waited for: 2 -> 3; matrix products, arithmetic and copies ran while one was open for 30% -> 29% of each run, Pallas kernels for 0% -> 0%
where the time goes in v7:
time: 234 us; the launch traced here: 233 us
  waiting for transfers between devices  61.5 us (26%)
  matrix products  58.7 us (25%)
  local copies, waits for them, and re-layouts  43.1 us (18%)
  other arithmetic  28 us (12%)
  starting transfers between devices  19.7 us (8%)
  between operations  14.5 us (6%)
  blocking collectives  7.52 us (3%)
    ppermute x1, waiting for transfers between devices, staged_scatter(): lax.ppermute(send.astype(jnp.bfloat16), axis_name, perm=[(i, i ^ 2) for i...  34.1 us
    all_to_all x1, waiting for transfers between devices, swap_sum(): lax.all_to_all(parts, axis_name, split_axis=0, concat_axis=0, axis_index_...  20.1 us
    dot_general x2, matrix products, weight_term(): jnp.einsum(cell_form + ',tbhle->dthe', normed, grad_projected, preferred_...  11.1 us
    dot_general x2, matrix products, backward(): jnp.einsum('tbhle,dthe->' + cell_form, grad_projected, projection, prefer...  10.2 us
    slice x6, local copies, waits for them, and re-layouts, split_weight(): weight[:, :3 * model_width].reshape(model_width, 3, HEADS, head_size)  9.55 us
    dot_general x2, matrix products, forward(): jnp.einsum(cell_form + ',dthe->tbhle', normed, projection, preferred_elem...  9.46 us
    dot_general x6, matrix products, attend_heads(): jnp.einsum('bhle,bhme->bhlm', queries, keys_part, preferred_element_type=...  9.43 us
    dot_general x5, matrix products, attend_heads(): jnp.einsum('bhlm,bhme->bhle', weights, values_part, preferred_element_typ...  8.53 us
  transfers between devices with their start and end apart: 5, of which 3 were waited for; matrix products, arithmetic and copies ran while one was open for 29% of the time, Pallas kernels for 0%

profile of v7, /device:TPU:0, one launch (start us, length us, event | category | flops | bytes accessed | tf_op | source)
XLA Modules:
  0.0 233.1 jit_solution(4853492042943011425)
XLA Ops:
  7.2 2.4 %slice.62 = bf16[768,768]{1,0:T(8,128)(2,1)} slice(bf16[768,3072]{1,0:T(8,128)(2,1)} %param.6), slice={[0:768], [2304:3072]} | slice | bytes 2359296 | tf_op jit(solution)/shard_map/slice | solution.py:34
  11.8 3.6 %copy.140 = bf16[768,2304]{0,1:T(8,128)(2,1)} copy(bf16[768,2304]{1,0:T(8,128)(2,1)S(1)} %slice-done) | data formatting | bytes 7077888 | tf_op jit(solution)/shard_map/slice | solution.py:33
  15.4 5.8 %convert_bitcast_fusion = bf16[3,8,12,64,64]{4,3,2,0,1:T(8,128)(2,1)S(1)} fusion(bf16[768,3,12,64,1]{0,3,2,1,4:T(8,128)(2,1)} %bitcast.208, bf16[8,64,768]{2,1,0:T(8,128)(2,1)} %param.4, f32[8,64]{1,0:T(8,128)S(1)} %fusion.72), kind=kOutput, calls=%fused_computation.8 | convolution fusion | flops 1814298624 | bytes 6686720 | tf_op jit(solution)/shard_map/bld,dthe->tbhle/dot_general | solution.py:43
  22.2 4.7 %fusion.84 = (f32[8,12,64]{2,1,0:T(8,128)S(1)}, f32[8,12,64,64]{2,3,1,0:T(8,128)S(1)}) fusion(f32[8,12,64,64]{2,3,1,0:T(8,128)S(1)} %fusion.44), kind=kOutput, calls=%fused_computation.129 | output fusion | flops 1572927 | bytes 3170304 | tf_op jit(solution)/shard_map/sub | solution.py:21
  31.9 7.4 %all-to-all-start = ((bf16[8,64,768]{2,0,1:T(8,128)(2,1)}), bf16[8,64,768]{2,0,1:T(8,128)(2,1)}, u32[]{:S(2)}, u32[]{:S(2)}) async-start(bf16[8,64,768]{2,0,1:T(8,128)(2,1)} %copy.142), calls=%async_computation | async-start | bytes 1572864 | tf_op jit(solution)/shard_map/all_to_all | solution.py:117
  39.4 2.4 %slice.57 = bf16[768,768]{1,0:T(8,128)(2,1)} slice(bf16[768,3072]{1,0:T(8,128)(2,1)} %param.7), slice={[0:768], [2304:3072]} | slice | bytes 2359296 | tf_op jit(solution)/shard_map/slice | solution.py:34
  41.8 2.0 slice-done.1
  43.8 3.7 %copy.147 = bf16[768,2304]{0,1:T(8,128)(2,1)} copy(bf16[768,2304]{1,0:T(8,128)(2,1)S(1)} %slice-done.1) | data formatting | bytes 7077888 | tf_op jit(solution)/shard_map/slice | solution.py:33
  47.5 3.4 %fusion.48 = bf16[4,12,128,64]{2,3,0,1:T(8,128)(2,1)} fusion(bf16[12,64,768,1]{2,1,3,0:T(8,128)(2,1)} %bitcast.219, bf16[128,4,768]{2,1,0:T(4,128)(2,1)} %param.5), kind=kOutput, calls=%fused_computation.90 | convolution fusion | flops 604372992 | bytes 2752512 | tf_op jit(solution)/shard_map/lbf,hef->bhle/dot_general | solution.py:60
  50.9 7.3 %all-to-all-done = bf16[8,64,768]{2,0,1:T(8,128)(2,1)} async-done(((bf16[8,64,768]{2,0,1:T(8,128)(2,1)}), bf16[8,64,768]{2,0,1:T(8,128)(2,1)}, u32[]{:S(2)}, u32[]{:S(2)}) %all-to-all-start) | async-done | bytes 786464 | tf_op jit(solution)/shard_map/all_to_all | solution.py:117
  58.1 2.0 multiply_reduce_fusion.2
  60.1 1.4 copy.144
  61.5 1.3 multiply_add_fusion
  62.9 1.4 copy.145
  64.3 3.6 %convert_bitcast_fusion.1 = bf16[3,4,12,128,64]{3,4,2,0,1:T(8,128)(2,1)S(1)} fusion(bf16[768,3,12,64,1]{0,3,2,1,4:T(8,128)(2,1)S(1)} %bitcast.210, f32[16,8,4]{1,2,0:T(4,128)} %copy.145, bf16[8,64,768]{2,0,1:T(8,128)(2,1)} %all-to-all-done), kind=kOutput, calls=%fused_computation.44 | convolution fusion | flops 1814298624 | bytes 6686720 | tf_op jit(solution)/shard_map/lbd,dthe->tbhle/dot_general | solution.py:43
  68.6 3.0 %fusion.85 = (f32[4,12,128]{2,1,0:T(8,128)S(1)}, f32[4,12,128,128]{2,3,1,0:T(8,128)S(1)}) fusion(f32[4,12,128,128]{2,3,1,0:T(8,128)S(1)} %fusion.65), kind=kOutput, calls=%fused_computation.130 | output fusion | flops 3145855 | bytes 6316032 | tf_op jit(solution)/shard_map/jvp()/sub | solution.py:21
  71.7 2.2 fusion.6
  73.9 2.1 fusion.50
  76.0 1.7 fusion.49
  79.2 2.9 %fusion.47 = bf16[1,4,12,128,64]{3,4,2,1,0:T(8,128)(2,1)S(1)} fusion(bf16[4,12,128,128]{2,3,1,0:T(8,128)(2,1)} %get-tuple-element.4, bf16[4,12,128,64]{2,3,0,1:T(8,128)(2,1)} %fusion.48), kind=kOutput, calls=%fused_computation.89 | convolution fusion | flops 101056512 | bytes 3145728 | tf_op jit(solution)/shard_map/transpose(jvp(bhlm,bhme->bhle))/dot_general | solution.py:22
  82.1 3.6 %fusion.32 = (f32[128,4]{0,1:T(4,128)S(1)}, f32[4,128,768,1,1]{2,1,3,0,4:T(8,128)S(1)}) fusion(bf16[768,3,12,64,1]{0,3,2,4,1:T(8,128)(2,1)S(1)} %bitcast.211, bf16[1,4,12,128,64]{3,4,2,1,0:T(8,128)(2,1)S(1)} %fusion.47, bf16[1,4,12,128,64]{3,4,2,1,0:T(8,128)(2,1)S(1)} %copy-done.18, bf16[1,4,12,128,64]{3,4,2,1,0:T(8,128)(2,1)S(1)} %copy-done.19, ...), kind=kOutput, calls=%fused_computation.71 | convolution fusion | flops 1815477760 | bytes 8259584 | tf_op jit(solution)/shard_map/tbhle,dthe->lbd/dot_general | solution.py:65
  85.8 1.5 fusion.21
  87.3 1.5 copy.155
  88.8 5.5 %all-to-all-start.1 = ((bf16[128,4,768]{2,1,0:T(4,128)(2,1)}), bf16[128,4,768]{2,1,0:T(4,128)(2,1)S(1)}, u32[]{:S(2)}, u32[]{:S(2)}) async-start(bf16[128,4,768]{2,1,0:T(4,128)(2,1)} %copy.155), calls=%async_computation.1 | async-start | bytes 1572864 | tf_op jit(solution)/shard_map/all_to_all | solution.py:124
  95.0 2.5 %copy.159 = bf16[12,64,8,64]{1,0,3,2:T(8,128)(2,1)S(1)} copy(bf16[12,64,8,64]{1,3,0,2:T(8,128)(2,1)} %bitcast.215) | data formatting | bytes 1572864 | tf_op jit(solution)/shard_map/convert_element_type | solution.py:23
  97.5 2.3 dot_general.96
  99.8 1.9 fusion.52
  101.7 2.0 copy.163
  103.6 3.6 %bitcast_convert_fusion.2 = bf16[12,64,768]{2,1,0:T(8,128)(2,1)} fusion(bf16[4,12,128,128]{2,3,1,0:T(8,128)(2,1)S(1)} %copy-done.13, bf16[128,4,768]{2,1,0:T(4,128)(2,1)} %param.5, bf16[3,4,12,128,64]{3,4,2,0,1:T(8,128)(2,1)} %copy-done.17), kind=kOutput, calls=%fused_computation.39 | convolution fusion | flops 705626112 | bytes 4325376 | tf_op jit(solution)/shard_map/bhle,lbf->hef/dot_general | solution.py:79
  107.3 4.2 %bitcast_convert_fusion.1 = bf16[768,2304]{1,0:T(8,128)(2,1)S(1)} fusion(bf16[2304,4,128]{2,0,1:T(8,128)(2,1)} %bitcast.214, f32[128,4]{0,1:T(4,128)S(1)} %get-tuple-element.7, bf16[8,64,768]{2,0,1:T(8,128)(2,1)} %all-to-all-done), kind=kOutput, calls=%fused_computation.3 | convolution fusion | flops 1814888448 | bytes 6686720 | tf_op jit(solution)/shard_map/lbd,tbhle->dthe/dot_general | solution.py:76
  111.5 2.8 %pad_maximum_fusion.2 = bf16[768,3072]{1,0:T(8,128)(2,1)} fusion(bf16[768,768]{1,0:T(8,128)(2,1)S(1)} %bitcast.216, bf16[768,2304]{1,0:T(8,128)(2,1)S(1)} %bitcast_convert_fusion.1), kind=kLoop, calls=%fused_computation.6 | loop fusion | flops 9437184 | bytes 9437184 | tf_op jit(solution)/shard_map/concatenate | solution.py:82
  116.2 1.4 convolution_convert_fusion
  118.1 1.7 fusion.38
  120.8 2.0 fusion.37
  122.8 2.1 fusion.36
  125.7 1.5 copy.161
  127.2 6.8 %bitcast_convert_fusion = bf16[768,3,12,64]{0,3,2,1:T(8,128)(2,1)} fusion(bf16[1,8,12,64,64]{4,3,2,1,0:T(8,128)(2,1)} %fusion.38, bf16[1,8,12,64,64]{4,3,2,1,0:T(8,128)(2,1)} %fusion.37, bf16[1,8,12,64,64]{4,3,2,1,0:T(8,128)(2,1)} %fusion.36, bf16[8,64,768]{2,1,0:T(8,128)(2,1)S(1)} %copy-done.8, f32[8,64]{1,0:T(8,128)S(1)} %copy-done.30), kind=kOutput, calls=%fused_computation.2 | convolution fusion | flops 1821966336 | bytes 6686720 | tf_op jit(solution)/shard_map/bld,tbhle->dthe/dot_general | solution.py:76
  134.0 4.4 %copy.160 = bf16[768,2304]{1,0:T(8,128)(2,1)S(1)} copy(bf16[768,2304]{0,1:T(8,128)(2,1)} %bitcast.212) | data formatting | bytes 7077888 | tf_op jit(solution)/shard_map/reshape | solution.py:78
  138.4 1.9 pad_maximum_fusion.1
  140.7 7.5 %all_to_all.37 = bf16[2,4,2,48,3072]{4,3,2,1,0:T(8,128)(2,1)S(1)} all-to-all(bf16[2,4,2,48,3072]{4,3,2,1,0:T(8,128)(2,1)S(1)} %copy.162), channel_id=1, replica_groups={{0,1},{2,3},{4,5},{6,7},{8,9},{10,11},{12,13},{14,15},{16,17},{18,19},{..., dimensions={0} | all-to-all | bytes 9437184 | tf_op jit(solution)/shard_map/all_to_all | solution.py:86
  149.2 2.1 copy-done
  151.4 2.0 collective-permute-start
  153.4 34.1 %collective-permute-done = bf16[4,48,3072]{2,1,0:T(8,128)(2,1)S(1)} collective-permute-done((bf16[4,48,3072]{2,1,0:T(8,128)(2,1)S(1)}, bf16[4,48,3072]{2,1,0:T(8,128)(2,1)S(1)}, u32[]{:S(2)}, u32[]{:S(2)}) %collective-permute-start) | collective-permute-done | bytes 1179680 | tf_op jit(solution)/shard_map/ppermute | solution.py:109
  187.6 3.0 %fusion.18 = bf16[4,48,3072]{2,1,0:T(8,128)(2,1)} fusion(bf16[4,48,3072]{2,1,0:T(8,128)(2,1)S(1)} %collective-permute-done, f32[1,4,2,48,3072]{4,3,2,1,0:T(8,128)} %copy-done, s32[]{:T(128)S(6)} %select_n.7), kind=kLoop, calls=%fused_computation.41 | loop fusion | flops 1769472 | bytes 4718596 | tf_op jit(solution)/shard_map/convert_element_type | solution.py:110
  190.6 4.8 %all-to-all-start.3 = ((bf16[4,48,3072]{2,1,0:T(8,128)(2,1)}), bf16[4,48,3072]{2,1,0:T(8,128)(2,1)S(1)}, u32[]{:S(2)}, u32[]{:S(2)}) async-start(bf16[4,48,3072]{2,1,0:T(8,128)(2,1)} %fusion.18), calls=%async_computation.3 | async-start | bytes 2359296 | tf_op jit(solution)/shard_map/all_to_all | solution.py:86
  195.4 6.6 %fusion.27 = (f32[8,64]{1,0:T(8,128)S(1)}, f32[8,64,768,1,1]{2,1,3,0,4:T(8,128)S(1)}) fusion(bf16[8,64,768]{2,1,0:T(8,128)(2,1)S(1)} %copy-done.9, bf16[768,3,12,64,1]{0,3,2,4,1:T(8,128)(2,1)} %bitcast.209, bf16[1,8,12,64,64]{4,3,2,1,0:T(8,128)(2,1)} %fusion.38, bf16[1,8,12,64,64]{4,3,2,1,0:T(8,128)(2,1)} %fusion.37, bf16[1,8,12,64,64]{4,3,2,1,0:T(8,128)(2,1)} %fusion.36), kind=kOutput, calls=%fused_computation.60 | convolution fusion | flops 1815477760 | bytes 8259584 | tf_op jit(solution)/shard_map/tbhle,dthe->bld/dot_general | solution.py:65
  203.3 20.1 %all-to-all-done.3 = bf16[4,48,3072]{2,1,0:T(8,128)(2,1)S(1)} async-done(((bf16[4,48,3072]{2,1,0:T(8,128)(2,1)}), bf16[4,48,3072]{2,1,0:T(8,128)(2,1)S(1)}, u32[]{:S(2)}, u32[]{:S(2)}) %all-to-all-start.3) | async-done | bytes 1179680 | tf_op jit(solution)/shard_map/all_to_all | solution.py:86
  224.4 1.8 convert_element_type.211
  (98 shorter events, 19.0 us)
Async XLA Ops:
  9.5 1.1 copy-start.6
  9.5 2.2 slice-start
  10.9 0.6 copy-start.27
  11.8 3.6 %copy-start.29 = (f32[8,64]{1,0:T(8,128)}, f32[8,64]{1,0:T(8,128)S(1)}, u32[]{:S(2)}) copy-start(f32[8,64]{1,0:T(8,128)S(1)} %fusion.72) | copy-start | bytes 6148
  21.2 5.6 %copy-start.3 = (bf16[3,8,12,64,64]{4,3,2,0,1:T(8,128)(2,1)}, bf16[3,8,12,64,64]{4,3,2,0,1:T(8,128)(2,1)S(1)}, u32[]{:S(2)}) copy-start(bf16[3,8,12,64,64]{4,3,2,0,1:T(8,128)(2,1)S(1)} %convert_bitcast_fusion) | copy-start | bytes 7077892
  26.8 1.6 copy-start.1
  26.8 1.7 copy-start.23
  26.9 1.7 copy-start.7
  26.9 2.9 %copy-start.15 = (bf16[768,768]{1,0:T(8,128)(2,1)S(1)}, bf16[768,768]{1,0:T(8,128)(2,1)}, u32[]{:S(2)}) copy-start(bf16[768,768]{1,0:T(8,128)(2,1)} %slice.62) | copy-start | bytes 3538948
  28.5 2.1 copy-start.12
  31.9 26.2 %all-to-all-start = ((bf16[8,64,768]{2,0,1:T(8,128)(2,1)}), bf16[8,64,768]{2,0,1:T(8,128)(2,1)}, u32[]{:S(2)}, u32[]{:S(2)}) async-start(bf16[8,64,768]{2,0,1:T(8,128)(2,1)} %copy.142), calls=%async_computation | async-start | bytes 1572864 | tf_op jit(solution)/shard_map/all_to_all | solution.py:117
  41.8 2.0 slice-start.1
  47.5 16.8 %copy-start.4 = (bf16[768,2304]{0,1:T(8,128)(2,1)S(1)}, bf16[768,2304]{0,1:T(8,128)(2,1)}, u32[]{:S(2)}) copy-start(bf16[768,2304]{0,1:T(8,128)(2,1)} %copy.147) | copy-start | bytes 10616836
  67.9 8.0 %copy-start.17 = (bf16[3,4,12,128,64]{3,4,2,0,1:T(8,128)(2,1)}, bf16[3,4,12,128,64]{3,4,2,0,1:T(8,128)(2,1)S(1)}, u32[]{:S(2)}) copy-start(bf16[3,4,12,128,64]{3,4,2,0,1:T(8,128)(2,1)S(1)} %convert_bitcast_fusion.1) | copy-start | bytes 7077892
  68.6 3.1 %copy-start.22 = (bf16[4,12,128,64]{2,3,0,1:T(8,128)(2,1)S(1)}, bf16[4,12,128,64]{2,3,0,1:T(8,128)(2,1)}, u32[]{:S(2)}) copy-start(bf16[4,12,128,64]{2,3,0,1:T(8,128)(2,1)} %fusion.48) | copy-start | bytes 2359300
  79.2 2.9 %copy-start.18 = (bf16[1,4,12,128,64]{3,4,2,1,0:T(8,128)(2,1)S(1)}, bf16[1,4,12,128,64]{3,4,2,1,0:T(8,128)(2,1)}, u32[]{:S(2)}) copy-start(bf16[1,4,12,128,64]{3,4,2,1,0:T(8,128)(2,1)} %fusion.50) | copy-start | bytes 2359300
  79.2 2.9 %copy-start.19 = (bf16[1,4,12,128,64]{3,4,2,1,0:T(8,128)(2,1)S(1)}, bf16[1,4,12,128,64]{3,4,2,1,0:T(8,128)(2,1)}, u32[]{:S(2)}) copy-start(bf16[1,4,12,128,64]{3,4,2,1,0:T(8,128)(2,1)} %fusion.49) | copy-start | bytes 2359300
  82.1 3.7 %copy-start.5 = (bf16[1,4,12,128,64]{3,4,2,1,0:T(8,128)(2,1)}, bf16[1,4,12,128,64]{3,4,2,1,0:T(8,128)(2,1)S(1)}, u32[]{:S(2)}) copy-start(bf16[1,4,12,128,64]{3,4,2,1,0:T(8,128)(2,1)S(1)} %fusion.47) | copy-start | bytes 2359300
  82.1 3.6 %copy-start.20 = (bf16[128,4,768]{2,1,0:T(4,128)(2,1)S(1)}, bf16[128,4,768]{2,1,0:T(4,128)(2,1)}, u32[]{:S(2)}) copy-start(bf16[128,4,768]{2,1,0:T(4,128)(2,1)} %param.5) | copy-start | bytes 2359300
  87.3 7.0 %copy-start.24 = (f32[8,12,64]{2,1,0:T(8,128)S(1)}, f32[8,12,64]{2,1,0:T(8,128)}, u32[]{:S(2)}) copy-start(f32[8,12,64]{2,1,0:T(8,128)} %copy-done.23) | copy-start | bytes 73732
  88.8 25.5 %all-to-all-start.1 = ((bf16[128,4,768]{2,1,0:T(4,128)(2,1)}), bf16[128,4,768]{2,1,0:T(4,128)(2,1)S(1)}, u32[]{:S(2)}, u32[]{:S(2)}) async-start(bf16[128,4,768]{2,1,0:T(4,128)(2,1)} %copy.155), calls=%async_computation.1 | async-start | bytes 1572864 | tf_op jit(solution)/shard_map/all_to_all | solution.py:124
  94.3 130.1 %reduce-scatter.2.cloned.1.call-start = ((), (), s32[]{:S(2)}) async-start(), calls=%async_computation.5 | async-start | bytes 5013504 | tf_op jit(solution)/shard_map/reduce_scatter | solution.py:121
  101.7 2.0 copy-start.13
  107.3 4.2 %copy-start.14 = (bf16[12,64,768]{2,1,0:T(8,128)(2,1)S(1)}, bf16[12,64,768]{2,1,0:T(8,128)(2,1)}, u32[]{:S(2)}) copy-start(bf16[12,64,768]{2,1,0:T(8,128)(2,1)} %bitcast_convert_fusion.2) | copy-start | bytes 3538948
  114.6 1.6 copy-start.16
  114.8 10.1 %copy-start.10 = (bf16[8,64,768]{2,1,0:T(8,128)(2,1)}, bf16[8,64,768]{2,1,0:T(8,128)(2,1)S(1)}, u32[]{:S(2)}) copy-start(bf16[8,64,768]{2,1,0:T(8,128)(2,1)S(1)} %all_to_all.30) | copy-start | bytes 2359300
  116.2 1.9 copy-start.2
  116.2 1.9 copy-start.25
  116.2 3.6 %slice-start.2 = ((s8[4718592]{0:T(1024)(128)(4,1)}), s8[4194304]{0:T(1024)(128)(4,1)S(1)}, s32[]{:S(2)}) async-start(s8[4718592]{0:T(1024)(128)(4,1)} %bitcast.206), calls=%async_computation.8 | async-start | bytes 8388608
  118.1 1.7 slice-start.3
  118.1 1.7 copy-start.26
  122.8 2.1 copy-start.21
  124.9 2.3 copy-start.8
  124.9 2.3 copy-start.30
  149.1 2.1 copy-start
  151.4 36.1 %collective-permute-start = (bf16[4,48,3072]{2,1,0:T(8,128)(2,1)S(1)}, bf16[4,48,3072]{2,1,0:T(8,128)(2,1)S(1)}, u32[]{:S(2)}, u32[]{:S(2)}) collective-permute-start(bf16[4,48,3072]{2,1,0:T(8,128)(2,1)S(1)} %fusion.51), channel_id=1, source_target_pairs={{0,2},{1,3},{2,0},{3,1},{4,6},{5,7},{6,4},{7,5},{8,10},{9,11},{10,... | collective-permute-start | bytes 3538952 | tf_op jit(solution)/shard_map/ppermute | solution.py:109
  190.6 4.8 %copy-start.9 = (bf16[8,64,768]{2,1,0:T(8,128)(2,1)S(1)}, bf16[8,64,768]{2,1,0:T(8,128)(2,1)}, u32[]{:S(2)}) copy-start(bf16[8,64,768]{2,1,0:T(8,128)(2,1)} %param.4) | copy-start | bytes 2359300
  190.6 32.9 %all-to-all-start.3 = ((bf16[4,48,3072]{2,1,0:T(8,128)(2,1)}), bf16[4,48,3072]{2,1,0:T(8,128)(2,1)S(1)}, u32[]{:S(2)}, u32[]{:S(2)}) async-start(bf16[4,48,3072]{2,1,0:T(8,128)(2,1)} %fusion.18), calls=%async_computation.3 | async-start | bytes 2359296 | tf_op jit(solution)/shard_map/all_to_all | solution.py:86
  195.3 6.6 %copy-start.28 = (f32[8,64]{1,0:T(8,128)S(1)}, f32[8,64]{1,0:T(8,128)}, u32[]{:S(2)}) copy-start(f32[8,64]{1,0:T(8,128)} %copy-done.27) | copy-start | bytes 6148
  195.4 6.6 %copy-start.11 = (bf16[8,64,768]{2,1,0:T(8,128)(2,1)S(1)}, bf16[8,64,768]{2,1,0:T(8,128)(2,1)}, u32[]{:S(2)}) copy-start(bf16[8,64,768]{2,1,0:T(8,128)(2,1)} %copy-done.10) | copy-start | bytes 2359300
Sparse Core Ops, SparseCore 0:
  114.5 83.7 reduce-scatter.1

commit v8 on v6

--- a/solution.py
+++ b/solution.py
@@ -79,7 +79,7 @@
     second = jnp.einsum(
         "bhle," + out_form + "->hef", attended, upstream, preferred_element_type=jnp.float32
     ).reshape(model_width, model_width)
-    return jnp.concatenate([first, second], axis=1)
+    return [first, second]
 
 
 def swap_sum(parts, axis_name, groups):
@@ -113,14 +113,17 @@
     mid_columns = lax.all_to_all(row_saved[4], "cell", split_axis=1, concat_axis=0, tiled=True)
     col_saved = forward(mid_columns, col_weight, 0, False)
     grad_mid_columns, grad_col_proj = backward(col_saved, col_weight, cotangent, 0)
-    col_term = weight_term(col_saved[1], grad_col_proj, col_saved[3], cotangent, 0)
-    col_grad = lax.psum_scatter(
-        col_term.astype(jnp.bfloat16), "cell", scatter_dimension=0, tiled=True
-    ).astype(jnp.float32)
+    col_pieces = weight_term(col_saved[1], grad_col_proj, col_saved[3], cotangent, 0)
     grad_mid = lax.all_to_all(grad_mid_columns, "cell", split_axis=0, concat_axis=1, tiled=True)
     grad_cells, grad_row_proj = backward(row_saved, row_weight, grad_mid, 1)
-    row_term = weight_term(row_saved[1], grad_row_proj, row_saved[3], grad_mid, 1)
-    row_grad = staged_scatter(row_term, "cell")
+    row_pieces = weight_term(row_saved[1], grad_row_proj, row_saved[3], grad_mid, 1)
+    early = jnp.concatenate(col_pieces + [row_pieces[1]], axis=1)
+    early_grad = lax.psum_scatter(
+        early.astype(jnp.bfloat16), "cell", scatter_dimension=0, tiled=True
+    ).astype(jnp.float32)
+    col_width = col_pieces[0].shape[1] + col_pieces[1].shape[1]
+    col_grad = early_grad[:, :col_width]
+    row_grad = jnp.concatenate([staged_scatter(row_pieces[0], "cell"), early_grad[:, col_width:]], axis=1)
     return (grad_cells, row_grad, col_grad)
 
 

time: 234 us -> 243 us (1.038)
  waiting for transfers between devices: 27.9 us -> 41.1 us
  matrix products: 61.9 us -> 53.7 us
  blocking collectives: 43.2 us -> 46.8 us
  other arithmetic: 25.9 us -> 22.4 us
  local copies, waits for them, and re-layouts: 41.2 us -> 44.3 us
    all_to_all x1, waiting for transfers between devices: 20.6 us -> 27.9 us  [swap_sum(): lax.all_to_all(parts, axis_name, split_axis=0, concat_axis=0, axis_index_...]
    optimization_barrier x0 -> x1, local copies, waits for them, and re-layouts: none -> 4.49 us  [staged_scatter(): sent = lax.optimization_barrier(term.astype(jnp.bfloat16))]
    unnamed x64 -> x68, local copies, waits for them, and re-layouts: 3.95 us -> 8.33 us
    reshape x1 -> x0, local copies, waits for them, and re-layouts: 4.31 us -> none  [weight_term(): first = jnp.einsum(cell_form + ',tbhle->dthe', normed, grad_projected, pr...]
    all_to_all x1, waiting for transfers between devices: 0.01 us -> 3.66 us  [body(): lax.all_to_all(grad_mid_columns, 'cell', split_axis=0, concat_axis=1, til...]
    all_to_all x2, blocking collectives: 43.2 us -> 46.8 us  [swap_sum(): lax.all_to_all(parts, axis_name, split_axis=0, concat_axis=0, axis_index_...]
    dot_general x6, matrix products: 10.7 us -> 7.13 us  [attend_heads(): jnp.einsum('bhle,bhme->bhlm', queries, keys_part, preferred_element_type=...]
    slice x0 -> x2, local copies, waits for them, and re-layouts: none -> 2.71 us  [the longest x1 1.81 us: body(): col_grad = early_grad[:, :col_width]]
  transfers between devices with their start and end apart: 4 -> 4, of which waited for: 2 -> 4; matrix products, arithmetic and copies ran while one was open for 30% -> 21% of each run, Pallas kernels for 0% -> 0%
where the time goes in v8:
time: 243 us; the launch traced here: 241 us
  matrix products  53.7 us (22%)
  blocking collectives  46.8 us (19%)
  local copies, waits for them, and re-layouts  44.3 us (18%)
  waiting for transfers between devices  41.1 us (17%)
  other arithmetic  22.4 us (9%)
  starting transfers between devices  18.1 us (7%)
  between operations  14.6 us (6%)
    all_to_all x2, blocking collectives, swap_sum(): lax.all_to_all(parts, axis_name, split_axis=0, concat_axis=0, axis_index_...  46.8 us
    all_to_all x1, waiting for transfers between devices, swap_sum(): lax.all_to_all(parts, axis_name, split_axis=0, concat_axis=0, axis_index_...  27.9 us
    dot_general x2, matrix products, backward(): jnp.einsum('tbhle,dthe->' + cell_form, grad_projected, projection, prefer...  9.59 us
    dot_general x2, matrix products, forward(): jnp.einsum(cell_form + ',dthe->tbhle', normed, projection, preferred_elem...  9.47 us
    slice x6, local copies, waits for them, and re-layouts, split_weight(): weight[:, :3 * model_width].reshape(model_width, 3, HEADS, head_size)  9.42 us
    dot_general x2, matrix products, weight_term(): jnp.einsum(cell_form + ',tbhle->dthe', normed, grad_projected, preferred_...  9.12 us
    dot_general x5, matrix products, attend_heads(): jnp.einsum('bhlm,bhme->bhle', weights, values_part, preferred_element_typ...  8.96 us
    unnamed x68, local copies, waits for them, and re-layouts  8.33 us
  transfers between devices with their start and end apart: 4, of which 4 were waited for; matrix products, arithmetic and copies ran while one was open for 21% of the time, Pallas kernels for 0%

profile of v8, /device:TPU:0, one launch (start us, length us, event | category | flops | bytes accessed | tf_op | source)
XLA Modules:
  0.0 241.0 jit_solution(18223384629519892125)
XLA Ops:
  7.2 2.4 slice.74
  11.8 3.5 %copy.144 = bf16[768,2304]{0,1:T(8,128)(2,1)} copy(bf16[768,2304]{1,0:T(8,128)(2,1)S(1)} %slice-done) | data formatting | bytes 7077888 | tf_op jit(solution)/shard_map/slice | solution.py:33
  15.3 5.8 %convert_bitcast_fusion = bf16[3,8,12,64,64]{4,3,2,0,1:T(8,128)(2,1)S(1)} fusion(bf16[768,3,12,64,1]{0,3,2,1,4:T(8,128)(2,1)} %bitcast.208, bf16[8,64,768]{2,1,0:T(8,128)(2,1)} %param.4, f32[8,64]{1,0:T(8,128)S(1)} %fusion.72), kind=kOutput, calls=%fused_computation.6 | convolution fusion | flops 1814298624 | bytes 6686720 | tf_op jit(solution)/shard_map/bld,dthe->tbhle/dot_general | solution.py:43
  22.1 4.7 %fusion.84 = (f32[8,12,64]{2,1,0:T(8,128)S(1)}, f32[8,12,64,64]{2,3,1,0:T(8,128)S(1)}) fusion(f32[8,12,64,64]{2,3,1,0:T(8,128)S(1)} %fusion.44), kind=kOutput, calls=%fused_computation.128 | output fusion | flops 1572927 | bytes 3170304 | tf_op jit(solution)/shard_map/sub | solution.py:21
  28.5 1.2 copy-done.15
  30.6 1.3 copy.146
  31.9 7.4 %all-to-all-start = ((bf16[8,64,768]{2,0,1:T(8,128)(2,1)}), bf16[8,64,768]{2,0,1:T(8,128)(2,1)}, u32[]{:S(2)}, u32[]{:S(2)}) async-start(bf16[8,64,768]{2,0,1:T(8,128)(2,1)} %copy.146), calls=%async_computation | async-start | bytes 1572864 | tf_op jit(solution)/shard_map/all_to_all | solution.py:113
  39.3 2.4 slice.69
  41.7 2.0 slice-done.1
  43.7 3.6 %copy.151 = bf16[768,2304]{0,1:T(8,128)(2,1)} copy(bf16[768,2304]{1,0:T(8,128)(2,1)S(1)} %slice-done.1) | data formatting | bytes 7077888 | tf_op jit(solution)/shard_map/slice | solution.py:33
  47.3 3.4 %fusion.48 = bf16[4,12,128,64]{2,3,0,1:T(8,128)(2,1)} fusion(bf16[12,64,768,1]{2,1,3,0:T(8,128)(2,1)} %bitcast.218, bf16[128,4,768]{2,1,0:T(4,128)(2,1)} %param.5), kind=kOutput, calls=%fused_computation.88 | convolution fusion | flops 604372992 | bytes 2752512 | tf_op jit(solution)/shard_map/lbf,hef->bhle/dot_general | solution.py:60
  50.7 7.4 %all-to-all-done = bf16[8,64,768]{2,0,1:T(8,128)(2,1)} async-done(((bf16[8,64,768]{2,0,1:T(8,128)(2,1)}), bf16[8,64,768]{2,0,1:T(8,128)(2,1)}, u32[]{:S(2)}, u32[]{:S(2)}) %all-to-all-start) | async-done | bytes 786464 | tf_op jit(solution)/shard_map/all_to_all | solution.py:113
  58.1 2.0 multiply_reduce_fusion.2
  60.1 1.4 copy.148
  61.5 1.3 multiply_add_fusion
  62.8 1.4 copy.149
  64.2 3.6 %convert_bitcast_fusion.1 = bf16[3,4,12,128,64]{3,4,2,0,1:T(8,128)(2,1)S(1)} fusion(bf16[768,3,12,64,1]{0,3,2,1,4:T(8,128)(2,1)S(1)} %bitcast.210, f32[16,8,4]{1,2,0:T(4,128)} %copy.149, bf16[8,64,768]{2,0,1:T(8,128)(2,1)} %all-to-all-done), kind=kOutput, calls=%fused_computation.40 | convolution fusion | flops 1814298624 | bytes 6686720 | tf_op jit(solution)/shard_map/lbd,dthe->tbhle/dot_general | solution.py:43
  68.5 3.0 %fusion.85 = (f32[4,12,128]{2,1,0:T(8,128)S(1)}, f32[4,12,128,128]{2,3,1,0:T(8,128)S(1)}) fusion(f32[4,12,128,128]{2,3,1,0:T(8,128)S(1)} %fusion.65), kind=kOutput, calls=%fused_computation.129 | output fusion | flops 3145855 | bytes 6316032 | tf_op jit(solution)/shard_map/jvp()/sub | solution.py:21
  71.6 2.2 fusion.6
  73.9 2.1 fusion.50
  75.9 1.7 fusion.49
  79.2 2.9 %fusion.47 = bf16[1,4,12,128,64]{3,4,2,1,0:T(8,128)(2,1)S(1)} fusion(bf16[4,12,128,128]{2,3,1,0:T(8,128)(2,1)} %get-tuple-element.4, bf16[4,12,128,64]{2,3,0,1:T(8,128)(2,1)} %fusion.48), kind=kOutput, calls=%fused_computation.87 | convolution fusion | flops 101056512 | bytes 3145728 | tf_op jit(solution)/shard_map/transpose(jvp(bhlm,bhme->bhle))/dot_general | solution.py:22
  82.1 3.6 %fusion.32 = (f32[128,4]{0,1:T(4,128)S(1)}, f32[4,128,768,1,1]{2,1,3,0,4:T(8,128)S(1)}) fusion(bf16[768,3,12,64,1]{0,3,2,4,1:T(8,128)(2,1)S(1)} %bitcast.211, bf16[1,4,12,128,64]{3,4,2,1,0:T(8,128)(2,1)S(1)} %fusion.47, bf16[1,4,12,128,64]{3,4,2,1,0:T(8,128)(2,1)S(1)} %copy-done.18, bf16[1,4,12,128,64]{3,4,2,1,0:T(8,128)(2,1)S(1)} %copy-done.19, ...), kind=kOutput, calls=%fused_computation.69 | convolution fusion | flops 1815477760 | bytes 8259584 | tf_op jit(solution)/shard_map/tbhle,dthe->lbd/dot_general | solution.py:65
  85.8 1.5 fusion.21
  87.3 1.5 copy.159
  88.8 5.5 %all-to-all-start.1 = ((bf16[128,4,768]{2,1,0:T(4,128)(2,1)}), bf16[128,4,768]{2,1,0:T(4,128)(2,1)}, u32[]{:S(2)}, u32[]{:S(2)}) async-start(bf16[128,4,768]{2,1,0:T(4,128)(2,1)} %copy.159), calls=%async_computation.1 | async-start | bytes 1572864 | tf_op jit(solution)/shard_map/all_to_all | solution.py:117
  94.4 2.5 %copy.171 = bf16[12,64,8,64]{1,0,3,2:T(8,128)(2,1)S(1)} copy(bf16[12,64,8,64]{1,3,0,2:T(8,128)(2,1)} %bitcast.214) | data formatting | bytes 1572864 | tf_op jit(solution)/shard_map/convert_element_type | solution.py:23
  96.9 2.2 dot_general.101
  99.2 1.6 fusion.51
  101.3 3.1 %bitcast_convert_fusion.3 = bf16[12,64,768]{2,1,0:T(8,128)(2,1)S(1)} fusion(bf16[4,12,128,128]{2,3,1,0:T(8,128)(2,1)} %get-tuple-element.4, bf16[128,4,768]{2,1,0:T(4,128)(2,1)} %param.5, bf16[3,4,12,128,64]{3,4,2,0,1:T(8,128)(2,1)} %copy-done.17), kind=kOutput, calls=%fused_computation.39 | convolution fusion | flops 705626112 | bytes 4325376 | tf_op jit(solution)/shard_map/bhle,lbf->hef/dot_general | solution.py:79
  104.3 5.1 %bitcast_convert_fusion.1 = bf16[768,2304]{1,0:T(8,128)(2,1)} fusion(bf16[2304,4,128]{2,0,1:T(8,128)(2,1)S(1)} %bitcast.213, f32[128,4]{0,1:T(4,128)S(1)} %get-tuple-element.7, bf16[8,64,768]{2,0,1:T(8,128)(2,1)} %all-to-all-done), kind=kOutput, calls=%fused_computation.3 | convolution fusion | flops 1814888448 | bytes 6686720 | tf_op jit(solution)/shard_map/lbd,tbhle->dthe/dot_general | solution.py:76
  109.5 3.7 %all-to-all-done.1 = bf16[128,4,768]{2,1,0:T(4,128)(2,1)} async-done(((bf16[128,4,768]{2,1,0:T(4,128)(2,1)}), bf16[128,4,768]{2,1,0:T(4,128)(2,1)}, u32[]{:S(2)}, u32[]{:S(2)}) %all-to-all-start.1) | async-done | bytes 786464 | tf_op jit(solution)/shard_map/all_to_all | solution.py:117
  113.1 1.4 copy.232
  115.6 1.4 copy-done.5
  117.0 2.8 %pad_maximum_fusion = bf16[768,3840]{1,0:T(8,128)(2,1)} fusion(bf16[768,768]{1,0:T(8,128)(2,1)S(1)} %bitcast_convert_fusion.2, bf16[768,768]{1,0:T(8,128)(2,1)S(1)} %bitcast.215, bf16[768,2304]{1,0:T(8,128)(2,1)S(1)} %copy-done.5), kind=kLoop, calls=%fused_computation.4 | loop fusion | flops 17694720 | bytes 11796480 | tf_op jit(solution)/shard_map/concatenate | solution.py:120
  121.2 1.4 convolution_convert_fusion
  123.1 2.5 %fusion.11 = (f32[8,12,64]{2,1,0:T(8,128)S(1)}, bf16[8,12,64,64]{2,3,1,0:T(8,128)(2,1)S(1)}) fusion(f32[8,12,64,64]{2,3,1,0:T(8,128)S(1)} %copy-done.1, f32[8,12,64]{2,1,0:T(8,128)S(1)} %multiply_divide_fusion, bf16[3,8,12,64,64]{4,3,2,0,1:T(8,128)(2,1)} %copy-done.2, bf16[8,64,12,64]{3,1,2,0:T(8,128)(2,1)S(1)} %convolution_convert_fusion), kind=kOutput, calls=%fused_computation.21 | convolution fusion | flops 52291584 | bytes 4767744 | tf_op jit(solution)/shard_map/transpose(jvp(bhlm,bhme->bhle))/dot_general | solution.py:22
  129.4 4.0 %bitcast_convert_fusion = bf16[768,3,12,64]{0,3,2,1:T(8,128)(2,1)} fusion(bf16[1,8,12,64,64]{4,3,2,1,0:T(8,128)(2,1)S(1)} %fusion.38, bf16[1,8,12,64,64]{4,3,2,1,0:T(8,128)(2,1)S(1)} %fusion.37, bf16[1,8,12,64,64]{4,3,2,1,0:T(8,128)(2,1)S(1)} %fusion.36, bf16[8,64,768]{2,1,0:T(8,128)(2,1)S(1)} %copy-done.10, f32[8,64]{1,0:T(8,128)S(1)} %copy-done.28), kind=kOutput, calls=%fused_computation.2 | convolution fusion | flops 1821966336 | bytes 6686720 | tf_op jit(solution)/shard_map/bld,tbhle->dthe/dot_general | solution.py:76
  133.5 4.5 %copy.163 = bf16[768,2304]{1,0:T(8,128)(2,1)S(1)} copy(bf16[768,2304]{0,1:T(8,128)(2,1)} %bitcast.212) | data formatting | bytes 7077888 | tf_op jit(solution)/shard_map/optimization_barrier | solution.py:101
  138.2 6.6 %all_to_all.42 = bf16[2,4,2,48,2304]{4,3,2,1,0:T(8,128)(2,1)S(1)} all-to-all(bf16[2,4,2,48,2304]{4,3,2,1,0:T(8,128)(2,1)S(1)} %copy.164), channel_id=1, replica_groups={{0,1},{2,3},{4,5},{6,7},{8,9},{10,11},{12,13},{14,15},{16,17},{18,19},{..., dimensions={0} | all-to-all | bytes 7077888 | tf_op jit(solution)/shard_map/all_to_all | solution.py:86
  145.3 40.2 %all_to_all.43 = bf16[2,4,48,2304]{3,2,1,0:T(8,128)(2,1)S(1)} all-to-all(bf16[2,4,48,2304]{3,2,1,0:T(8,128)(2,1)S(1)} %copy.165), channel_id=1, replica_groups={{0,2},{1,3},{4,6},{5,7},{8,10},{9,11},{12,14},{13,15},{16,18},{17,19},{..., dimensions={0} | all-to-all | bytes 3538944 | tf_op jit(solution)/shard_map/all_to_all | solution.py:86
  186.7 5.1 %all-to-all-start.4 = ((bf16[4,48,2304]{2,1,0:T(8,128)(2,1)}), bf16[4,48,2304]{2,1,0:T(8,128)(2,1)}, u32[]{:S(2)}, u32[]{:S(2)}) async-start(bf16[4,48,2304]{2,1,0:T(8,128)(2,1)} %fusion.53), calls=%async_computation.4 | async-start | bytes 1769472 | tf_op jit(solution)/shard_map/all_to_all | solution.py:86
  191.8 6.0 %fusion.27 = (f32[8,64]{1,0:T(8,128)S(1)}, f32[8,64,768,1,1]{2,1,3,0,4:T(8,128)S(1)}) fusion(bf16[8,64,768]{2,1,0:T(8,128)(2,1)} %param.4, bf16[768,3,12,64,1]{0,3,2,4,1:T(8,128)(2,1)S(1)} %bitcast.209, bf16[1,8,12,64,64]{4,3,2,1,0:T(8,128)(2,1)} %copy-done.29, bf16[1,8,12,64,64]{4,3,2,1,0:T(8,128)(2,1)} %copy-done.31, ...), kind=kOutput, calls=%fused_computation.58 | convolution fusion | flops 1815477760 | bytes 8259584 | tf_op jit(solution)/shard_map/tbhle,dthe->bld/dot_general | solution.py:65
  197.9 1.3 fusion.23
  199.2 27.9 %all-to-all-done.4 = bf16[4,48,2304]{2,1,0:T(8,128)(2,1)} async-done(((bf16[4,48,2304]{2,1,0:T(8,128)(2,1)}), bf16[4,48,2304]{2,1,0:T(8,128)(2,1)}, u32[]{:S(2)}, u32[]{:S(2)}) %all-to-all-start.4) | async-done | bytes 884768 | tf_op jit(solution)/shard_map/all_to_all | solution.py:86
  227.1 1.4 add_bitcast_fusion
  228.4 2.2 reduce-scatter.2.cloned.1.call-done
  232.3 1.8 slice.104
  (99 shorter events, 18.8 us)
Async XLA Ops:
  9.5 1.1 copy-start.8
  9.5 2.2 slice-start
  10.9 0.6 copy-start.25
  11.8 3.5 %copy-start.27 = (f32[8,64]{1,0:T(8,128)}, f32[8,64]{1,0:T(8,128)S(1)}, u32[]{:S(2)}) copy-start(f32[8,64]{1,0:T(8,128)S(1)} %fusion.72) | copy-start | bytes 6148
  21.2 5.6 %copy-start.2 = (bf16[3,8,12,64,64]{4,3,2,0,1:T(8,128)(2,1)}, bf16[3,8,12,64,64]{4,3,2,0,1:T(8,128)(2,1)S(1)}, u32[]{:S(2)}) copy-start(bf16[3,8,12,64,64]{4,3,2,0,1:T(8,128)(2,1)S(1)} %convert_bitcast_fusion) | copy-start | bytes 7077892
  26.8 1.7 copy-start
  26.8 1.7 copy-start.23
  26.8 1.7 copy-start.9
  26.8 2.9 %copy-start.15 = (bf16[768,768]{1,0:T(8,128)(2,1)S(1)}, bf16[768,768]{1,0:T(8,128)(2,1)}, u32[]{:S(2)}) copy-start(bf16[768,768]{1,0:T(8,128)(2,1)} %slice.74) | copy-start | bytes 3538948
  28.5 2.1 copy-start.14
  31.9 26.2 %all-to-all-start = ((bf16[8,64,768]{2,0,1:T(8,128)(2,1)}), bf16[8,64,768]{2,0,1:T(8,128)(2,1)}, u32[]{:S(2)}, u32[]{:S(2)}) async-start(bf16[8,64,768]{2,0,1:T(8,128)(2,1)} %copy.146), calls=%async_computation | async-start | bytes 1572864 | tf_op jit(solution)/shard_map/all_to_all | solution.py:113
  41.7 2.0 slice-start.1
  47.3 16.9 %copy-start.4 = (bf16[768,2304]{0,1:T(8,128)(2,1)S(1)}, bf16[768,2304]{0,1:T(8,128)(2,1)}, u32[]{:S(2)}) copy-start(bf16[768,2304]{0,1:T(8,128)(2,1)} %copy.151) | copy-start | bytes 10616836
  67.9 8.0 %copy-start.17 = (bf16[3,4,12,128,64]{3,4,2,0,1:T(8,128)(2,1)}, bf16[3,4,12,128,64]{3,4,2,0,1:T(8,128)(2,1)S(1)}, u32[]{:S(2)}) copy-start(bf16[3,4,12,128,64]{3,4,2,0,1:T(8,128)(2,1)S(1)} %convert_bitcast_fusion.1) | copy-start | bytes 7077892
  68.5 3.1 %copy-start.21 = (bf16[4,12,128,64]{2,3,0,1:T(8,128)(2,1)S(1)}, bf16[4,12,128,64]{2,3,0,1:T(8,128)(2,1)}, u32[]{:S(2)}) copy-start(bf16[4,12,128,64]{2,3,0,1:T(8,128)(2,1)} %fusion.48) | copy-start | bytes 2359300
  79.2 2.9 %copy-start.18 = (bf16[1,4,12,128,64]{3,4,2,1,0:T(8,128)(2,1)S(1)}, bf16[1,4,12,128,64]{3,4,2,1,0:T(8,128)(2,1)}, u32[]{:S(2)}) copy-start(bf16[1,4,12,128,64]{3,4,2,1,0:T(8,128)(2,1)} %fusion.50) | copy-start | bytes 2359300
  79.2 2.9 %copy-start.19 = (bf16[1,4,12,128,64]{3,4,2,1,0:T(8,128)(2,1)S(1)}, bf16[1,4,12,128,64]{3,4,2,1,0:T(8,128)(2,1)}, u32[]{:S(2)}) copy-start(bf16[1,4,12,128,64]{3,4,2,1,0:T(8,128)(2,1)} %fusion.49) | copy-start | bytes 2359300
  82.1 3.7 %copy-start.6 = (bf16[1,4,12,128,64]{3,4,2,1,0:T(8,128)(2,1)}, bf16[1,4,12,128,64]{3,4,2,1,0:T(8,128)(2,1)S(1)}, u32[]{:S(2)}) copy-start(bf16[1,4,12,128,64]{3,4,2,1,0:T(8,128)(2,1)S(1)} %fusion.47) | copy-start | bytes 2359300
  82.1 3.6 %copy-start.20 = (bf16[128,4,768]{2,1,0:T(4,128)(2,1)S(1)}, bf16[128,4,768]{2,1,0:T(4,128)(2,1)}, u32[]{:S(2)}) copy-start(bf16[128,4,768]{2,1,0:T(4,128)(2,1)} %param.5) | copy-start | bytes 2359300
  88.8 24.3 %all-to-all-start.1 = ((bf16[128,4,768]{2,1,0:T(4,128)(2,1)}), bf16[128,4,768]{2,1,0:T(4,128)(2,1)}, u32[]{:S(2)}, u32[]{:S(2)}) async-start(bf16[128,4,768]{2,1,0:T(4,128)(2,1)} %copy.159), calls=%async_computation.1 | async-start | bytes 1572864 | tf_op jit(solution)/shard_map/all_to_all | solution.py:117
  94.3 136.2 %reduce-scatter.2.cloned.1.call-start = ((), (), s32[]{:S(2)}) async-start(), calls=%async_computation.6 | async-start | bytes 6266880 | tf_op jit(solution)/shard_map/reduce_scatter | solution.py:121
  96.9 2.3 copy-start.7
  109.5 5.3 %copy-start.22 = (bf16[768,8,64]{0,2,1:T(8,128)(2,1)S(1)}, bf16[768,8,64]{0,2,1:T(8,128)(2,1)}, u32[]{:S(2)}) copy-start(bf16[768,8,64]{0,2,1:T(8,128)(2,1)} %dot_general.101) | copy-start | bytes 2359300
  114.7 0.9 copy-start.12
  114.7 2.3 copy-start.5
  119.9 0.8 copy-start.24
  119.9 1.3 copy-start.16
  121.2 1.9 copy-start.1
  123.1 3.2 %slice-start.2 = ((s8[4718592]{0:T(1024)(128)(4,1)}), s8[4194304]{0:T(1024)(128)(4,1)S(1)}, s32[]{:S(2)}) async-start(s8[4718592]{0:T(1024)(128)(4,1)} %bitcast.206), calls=%async_computation.9 | async-start | bytes 8388608
  125.6 1.1 slice-start.3
  126.2 2.4 copy-start.29
  127.6 1.2 copy-start.30
  127.7 1.8 copy-start.10
  127.7 1.8 copy-start.28
  129.4 4.0 %copy-start.31 = (bf16[1,8,12,64,64]{4,3,2,1,0:T(8,128)(2,1)}, bf16[1,8,12,64,64]{4,3,2,1,0:T(8,128)(2,1)S(1)}, u32[]{:S(2)}) copy-start(bf16[1,8,12,64,64]{4,3,2,1,0:T(8,128)(2,1)S(1)} %fusion.37) | copy-start | bytes 2359300
  185.6 6.2 %copy-start.3 = (bf16[768,2304]{0,1:T(8,128)(2,1)S(1)}, bf16[768,2304]{0,1:T(8,128)(2,1)}, u32[]{:S(2)}) copy-start(bf16[768,2304]{0,1:T(8,128)(2,1)} %copy.144) | copy-start | bytes 10616836
  186.7 40.3 %all-to-all-start.4 = ((bf16[4,48,2304]{2,1,0:T(8,128)(2,1)}), bf16[4,48,2304]{2,1,0:T(8,128)(2,1)}, u32[]{:S(2)}, u32[]{:S(2)}) async-start(bf16[4,48,2304]{2,1,0:T(8,128)(2,1)} %fusion.53), calls=%async_computation.4 | async-start | bytes 1769472 | tf_op jit(solution)/shard_map/all_to_all | solution.py:86
  191.8 6.0 %copy-start.26 = (f32[8,64]{1,0:T(8,128)S(1)}, f32[8,64]{1,0:T(8,128)}, u32[]{:S(2)}) copy-start(f32[8,64]{1,0:T(8,128)} %copy-done.25) | copy-start | bytes 6148
  191.8 6.0 %copy-start.11 = (bf16[8,64,768]{2,1,0:T(8,128)(2,1)S(1)}, bf16[8,64,768]{2,1,0:T(8,128)(2,1)}, u32[]{:S(2)}) copy-start(bf16[8,64,768]{2,1,0:T(8,128)(2,1)} %param.4) | copy-start | bytes 2359300
  191.8 6.0 %copy-start.13 = (bf16[8,64,768]{2,1,0:T(8,128)(2,1)S(1)}, bf16[8,64,768]{2,1,0:T(8,128)(2,1)}, u32[]{:S(2)}) copy-start(bf16[8,64,768]{2,1,0:T(8,128)(2,1)} %copy-done.12) | copy-start | bytes 2359300
Sparse Core Ops, SparseCore 0:
  120.0 110.5 reduce-scatter.1

commit v9 on v6

--- a/solution.py
+++ b/solution.py
@@ -79,7 +79,7 @@
     second = jnp.einsum(
         "bhle," + out_form + "->hef", attended, upstream, preferred_element_type=jnp.float32
     ).reshape(model_width, model_width)
-    return jnp.concatenate([first, second], axis=1)
+    return [first, second]
 
 
 def swap_sum(parts, axis_name, groups):
@@ -113,14 +113,16 @@
     mid_columns = lax.all_to_all(row_saved[4], "cell", split_axis=1, concat_axis=0, tiled=True)
     col_saved = forward(mid_columns, col_weight, 0, False)
     grad_mid_columns, grad_col_proj = backward(col_saved, col_weight, cotangent, 0)
-    col_term = weight_term(col_saved[1], grad_col_proj, col_saved[3], cotangent, 0)
+    col_term = jnp.concatenate(weight_term(col_saved[1], grad_col_proj, col_saved[3], cotangent, 0), axis=1)
     col_grad = lax.psum_scatter(
         col_term.astype(jnp.bfloat16), "cell", scatter_dimension=0, tiled=True
     ).astype(jnp.float32)
     grad_mid = lax.all_to_all(grad_mid_columns, "cell", split_axis=0, concat_axis=1, tiled=True)
     grad_cells, grad_row_proj = backward(row_saved, row_weight, grad_mid, 1)
-    row_term = weight_term(row_saved[1], grad_row_proj, row_saved[3], grad_mid, 1)
-    row_grad = staged_scatter(row_term, "cell")
+    row_pieces = weight_term(row_saved[1], grad_row_proj, row_saved[3], grad_mid, 1)
+    early_grad = staged_scatter(row_pieces[1], "cell")
+    early_grad, late_piece = lax.optimization_barrier((early_grad, row_pieces[0]))
+    row_grad = jnp.concatenate([staged_scatter(late_piece, "cell"), early_grad], axis=1)
     return (grad_cells, row_grad, col_grad)
 
 

time: 234 us -> 247 us (1.056)
  waiting for transfers between devices: 27.9 us -> 37.8 us
  starting transfers between devices: 17.5 us -> 26.6 us
  blocking collectives: 43.2 us -> 35.9 us
    all_to_all x1 -> x3, waiting for transfers between devices: 20.6 us -> 30.5 us  [swap_sum(): lax.all_to_all(parts, axis_name, split_axis=0, concat_axis=0, axis_index_...]
    all_to_all x1 -> x3, starting transfers between devices: 4.6 us -> 13.4 us  [swap_sum(): lax.all_to_all(parts, axis_name, split_axis=0, concat_axis=0, axis_index_...]
    all_to_all x2 -> x3, blocking collectives: 43.2 us -> 35.9 us  [swap_sum(): lax.all_to_all(parts, axis_name, split_axis=0, concat_axis=0, axis_index_...]
    optimization_barrier x0 -> x1, local copies, waits for them, and re-layouts: none -> 4.32 us  [body(): lax.optimization_barrier((early_grad, row_pieces[0]))]
    reshape x1, local copies, waits for them, and re-layouts: 4.31 us -> 0.08 us  [staged_scatter(): blocks = sent.reshape((count // 4, 2, 2, block) + rest)]
    dot_general x2, matrix products: 8.2 us -> 11 us  [weight_term(): jnp.einsum(cell_form + ',tbhle->dthe', normed, grad_projected, preferred_...]
    another operation x1 -> x0, local copies, waits for them, and re-layouts: 2.52 us -> none
  transfers between devices with their start and end apart: 4 -> 6, of which waited for: 2 -> 4; matrix products, arithmetic and copies ran while one was open for 30% -> 29% of each run, Pallas kernels for 0% -> 0%
where the time goes in v9:
time: 247 us; the launch traced here: 245 us
  matrix products  63.3 us (26%)
  local copies, waits for them, and re-layouts  39.2 us (16%)
  waiting for transfers between devices  37.8 us (15%)
  blocking collectives  35.9 us (15%)
  other arithmetic  28 us (11%)
  starting transfers between devices  26.6 us (11%)
  between operations  14.6 us (6%)
    all_to_all x3, blocking collectives, swap_sum(): lax.all_to_all(parts, axis_name, split_axis=0, concat_axis=0, axis_index_...  35.9 us
    all_to_all x3, waiting for transfers between devices, swap_sum(): lax.all_to_all(parts, axis_name, split_axis=0, concat_axis=0, axis_index_...  30.5 us
    all_to_all x3, starting transfers between devices, swap_sum(): lax.all_to_all(parts, axis_name, split_axis=0, concat_axis=0, axis_index_...  13.4 us
    dot_general x5, matrix products, attend_heads(): jnp.einsum('bhlm,bhme->bhle', weights, values_part, preferred_element_typ...  12 us
    dot_general x2, matrix products, weight_term(): jnp.einsum(cell_form + ',tbhle->dthe', normed, grad_projected, preferred_...  11 us
    dot_general x2, matrix products, backward(): jnp.einsum('tbhle,dthe->' + cell_form, grad_projected, projection, prefer...  9.55 us
    slice x6, local copies, waits for them, and re-layouts, split_weight(): weight[:, :3 * model_width].reshape(model_width, 3, HEADS, head_size)  9.52 us
    dot_general x6, matrix products, attend_heads(): jnp.einsum('bhle,bhme->bhlm', queries, keys_part, preferred_element_type=...  9.51 us
  transfers between devices with their start and end apart: 6, of which 4 were waited for; matrix products, arithmetic and copies ran while one was open for 29% of the time, Pallas kernels for 0%

profile of v9, /device:TPU:0, one launch (start us, length us, event | category | flops | bytes accessed | tf_op | source)
XLA Modules:
  0.0 245.3 jit_solution(16574952234752271845)
XLA Ops:
  7.2 2.4 slice.92
  11.8 3.6 %copy.144 = bf16[768,2304]{0,1:T(8,128)(2,1)} copy(bf16[768,2304]{1,0:T(8,128)(2,1)S(1)} %slice-done) | data formatting | bytes 7077888 | tf_op jit(solution)/shard_map/slice | solution.py:33
  15.4 5.8 %convert_bitcast_fusion = bf16[3,8,12,64,64]{4,3,2,0,1:T(8,128)(2,1)S(1)} fusion(bf16[768,3,12,64,1]{0,3,2,1,4:T(8,128)(2,1)} %bitcast.221, bf16[8,64,768]{2,1,0:T(8,128)(2,1)} %param.4, f32[8,64]{1,0:T(8,128)S(1)} %fusion.75), kind=kOutput, calls=%fused_computation.5 | convolution fusion | flops 1814298624 | bytes 6686720 | tf_op jit(solution)/shard_map/bld,dthe->tbhle/dot_general | solution.py:43
  22.2 4.7 %fusion.87 = (f32[8,12,64]{2,1,0:T(8,128)S(1)}, f32[8,12,64,64]{2,3,1,0:T(8,128)S(1)}) fusion(f32[8,12,64,64]{2,3,1,0:T(8,128)S(1)} %fusion.45), kind=kOutput, calls=%fused_computation.134 | output fusion | flops 1572927 | bytes 3170304 | tf_op jit(solution)/shard_map/sub | solution.py:21
  31.9 7.4 %all-to-all-start = ((bf16[8,64,768]{2,0,1:T(8,128)(2,1)}), bf16[8,64,768]{2,0,1:T(8,128)(2,1)}, u32[]{:S(2)}, u32[]{:S(2)}) async-start(bf16[8,64,768]{2,0,1:T(8,128)(2,1)} %copy.146), calls=%async_computation | async-start | bytes 1572864 | tf_op jit(solution)/shard_map/all_to_all | solution.py:113
  39.4 2.5 %slice.87 = bf16[768,768]{1,0:T(8,128)(2,1)} slice(bf16[768,3072]{1,0:T(8,128)(2,1)} %param.7), slice={[0:768], [2304:3072]} | slice | bytes 2359296 | tf_op jit(solution)/shard_map/slice | solution.py:34
  41.8 2.0 slice-done.1
  43.8 3.6 %copy.151 = bf16[768,2304]{0,1:T(8,128)(2,1)} copy(bf16[768,2304]{1,0:T(8,128)(2,1)S(1)} %slice-done.1) | data formatting | bytes 7077888 | tf_op jit(solution)/shard_map/slice | solution.py:33
  47.5 3.4 %fusion.49 = bf16[4,12,128,64]{2,3,0,1:T(8,128)(2,1)} fusion(bf16[12,64,768,1]{2,1,3,0:T(8,128)(2,1)} %bitcast.232, bf16[128,4,768]{2,1,0:T(4,128)(2,1)} %param.5), kind=kOutput, calls=%fused_computation.88 | convolution fusion | flops 604372992 | bytes 2752512 | tf_op jit(solution)/shard_map/lbf,hef->bhle/dot_general | solution.py:60
  50.9 7.3 %all-to-all-done = bf16[8,64,768]{2,0,1:T(8,128)(2,1)} async-done(((bf16[8,64,768]{2,0,1:T(8,128)(2,1)}), bf16[8,64,768]{2,0,1:T(8,128)(2,1)}, u32[]{:S(2)}, u32[]{:S(2)}) %all-to-all-start) | async-done | bytes 786464 | tf_op jit(solution)/shard_map/all_to_all | solution.py:113
  58.1 2.0 multiply_reduce_fusion.2
  60.1 1.4 copy.148
  64.3 3.6 %convert_bitcast_fusion.1 = bf16[3,4,12,128,64]{3,4,2,0,1:T(8,128)(2,1)S(1)} fusion(bf16[768,3,12,64,1]{0,3,2,1,4:T(8,128)(2,1)S(1)} %bitcast.223, f32[16,8,4]{1,2,0:T(4,128)} %copy.149, bf16[8,64,768]{2,0,1:T(8,128)(2,1)} %all-to-all-done), kind=kOutput, calls=%fused_computation.39 | convolution fusion | flops 1814298624 | bytes 6686720 | tf_op jit(solution)/shard_map/lbd,dthe->tbhle/dot_general | solution.py:43
  68.6 3.0 %fusion.88 = (f32[4,12,128]{2,1,0:T(8,128)S(1)}, f32[4,12,128,128]{2,3,1,0:T(8,128)S(1)}) fusion(f32[4,12,128,128]{2,3,1,0:T(8,128)S(1)} %fusion.66), kind=kOutput, calls=%fused_computation.135 | output fusion | flops 3145855 | bytes 6316032 | tf_op jit(solution)/shard_map/jvp()/sub | solution.py:21
  71.7 2.2 fusion.6
  73.9 2.1 fusion.51
  76.0 1.7 fusion.50
  79.2 2.9 %fusion.48 = bf16[1,4,12,128,64]{3,4,2,1,0:T(8,128)(2,1)S(1)} fusion(bf16[4,12,128,128]{2,3,1,0:T(8,128)(2,1)} %get-tuple-element.8, bf16[4,12,128,64]{2,3,0,1:T(8,128)(2,1)} %fusion.49), kind=kOutput, calls=%fused_computation.87 | convolution fusion | flops 101056512 | bytes 3145728 | tf_op jit(solution)/shard_map/transpose(jvp(bhlm,bhme->bhle))/dot_general | solution.py:22
  82.1 3.6 %fusion.33 = (f32[128,4]{0,1:T(4,128)S(1)}, f32[4,128,768,1,1]{2,1,3,0,4:T(8,128)S(1)}) fusion(bf16[768,3,12,64,1]{0,3,2,4,1:T(8,128)(2,1)S(1)} %bitcast.224, bf16[1,4,12,128,64]{3,4,2,1,0:T(8,128)(2,1)S(1)} %fusion.48, bf16[1,4,12,128,64]{3,4,2,1,0:T(8,128)(2,1)S(1)} %copy-done.17, bf16[1,4,12,128,64]{3,4,2,1,0:T(8,128)(2,1)S(1)} %copy-done.18, ...), kind=kOutput, calls=%fused_computation.69 | convolution fusion | flops 1815477760 | bytes 8259584 | tf_op jit(solution)/shard_map/tbhle,dthe->lbd/dot_general | solution.py:65
  85.8 1.5 fusion.22
  87.3 1.5 copy.159
  88.8 5.5 %all-to-all-start.1 = ((bf16[128,4,768]{2,1,0:T(4,128)(2,1)}), bf16[128,4,768]{2,1,0:T(4,128)(2,1)S(1)}, u32[]{:S(2)}, u32[]{:S(2)}) async-start(bf16[128,4,768]{2,1,0:T(4,128)(2,1)} %copy.159), calls=%async_computation.1 | async-start | bytes 1572864 | tf_op jit(solution)/shard_map/all_to_all | solution.py:120
  94.6 2.5 %copy.162 = bf16[12,64,8,64]{1,0,3,2:T(8,128)(2,1)S(1)} copy(bf16[12,64,8,64]{1,3,0,2:T(8,128)(2,1)} %bitcast.228) | data formatting | bytes 1572864 | tf_op jit(solution)/shard_map/convert_element_type | solution.py:23
  97.1 2.0 dot_general.95
  99.2 1.9 fusion.52
  101.0 2.0 copy.168
  103.0 3.6 %bitcast_convert_fusion.1 = bf16[12,64,768]{2,1,0:T(8,128)(2,1)} fusion(bf16[4,12,128,128]{2,3,1,0:T(8,128)(2,1)S(1)} %copy-done.12, bf16[128,4,768]{2,1,0:T(4,128)(2,1)} %param.5, bf16[3,4,12,128,64]{3,4,2,0,1:T(8,128)(2,1)} %copy-done.16), kind=kOutput, calls=%fused_computation.37 | convolution fusion | flops 705626112 | bytes 4325376 | tf_op jit(solution)/shard_map/bhle,lbf->hef/dot_general | solution.py:79
  106.6 4.2 %bitcast_convert_fusion = bf16[768,2304]{1,0:T(8,128)(2,1)S(1)} fusion(bf16[2304,4,128]{2,0,1:T(8,128)(2,1)} %bitcast.227, f32[128,4]{0,1:T(4,128)S(1)} %get-tuple-element.11, bf16[8,64,768]{2,0,1:T(8,128)(2,1)} %all-to-all-done), kind=kOutput, calls=%fused_computation.2 | convolution fusion | flops 1814888448 | bytes 6686720 | tf_op jit(solution)/shard_map/lbd,tbhle->dthe/dot_general | solution.py:76
  110.9 2.9 %pad_maximum_fusion.1 = bf16[768,3072]{1,0:T(8,128)(2,1)} fusion(bf16[768,768]{1,0:T(8,128)(2,1)S(1)} %bitcast.229, bf16[768,2304]{1,0:T(8,128)(2,1)S(1)} %bitcast_convert_fusion), kind=kLoop, calls=%fused_computation.4 | loop fusion | flops 9437184 | bytes 9437184 | tf_op jit(solution)/shard_map/concatenate | solution.py:116
  116.2 3.1 %convolution_convert_fusion = bf16[8,64,12,64]{3,1,2,0:T(8,128)(2,1)S(1)} fusion(bf16[12,64,768,1]{2,1,0,3:T(8,128)(2,1)} %bitcast.230, bf16[8,64,768,1]{2,1,0,3:T(8,128)(2,1)} %reshape.161), kind=kOutput, calls=%fused_computation.44 | convolution fusion | flops 604372992 | bytes 2752512 | tf_op jit(solution)/shard_map/blf,hef->bhle/dot_general | solution.py:60
  119.3 3.1 %fusion.11 = (f32[8,12,64]{2,1,0:T(8,128)S(1)}, bf16[8,12,64,64]{2,3,1,0:T(8,128)(2,1)S(1)}) fusion(f32[8,12,64,64]{2,3,1,0:T(8,128)S(1)} %copy-done.1, f32[8,12,64]{2,1,0:T(8,128)S(1)} %multiply_divide_fusion, bf16[3,8,12,64,64]{4,3,2,0,1:T(8,128)(2,1)} %copy-done.2, bf16[8,64,12,64]{3,1,2,0:T(8,128)(2,1)S(1)} %convolution_convert_fusion), kind=kOutput, calls=%fused_computation.20 | convolution fusion | flops 52291584 | bytes 4767744 | tf_op jit(solution)/shard_map/transpose(jvp(bhlm,bhme->bhle))/dot_general | solution.py:22
  122.4 2.0 fusion.38
  124.4 2.2 fusion.37
  127.5 4.9 %all_to_all.57 = bf16[2,4,2,48,768]{4,3,1,2,0:T(8,128)(2,1)S(1)} all-to-all(bf16[2,4,2,48,768]{4,3,1,2,0:T(8,128)(2,1)S(1)} %bitcast.218), channel_id=1, replica_groups={{0,1},{2,3},{4,5},{6,7},{8,9},{10,11},{12,13},{14,15},{16,17},{18,19},{..., dimensions={0} | all-to-all | bytes 2359296 | tf_op jit(solution)/shard_map/all_to_all | solution.py:86
  133.3 4.5 %all-to-all-start.3 = ((bf16[2,4,48,768]{3,2,1,0:T(8,128)(2,1)}), bf16[2,4,48,768]{3,2,1,0:T(8,128)(2,1)}, u32[]{:S(2)}, u32[]{:S(2)}) async-start(bf16[2,4,48,768]{3,2,1,0:T(8,128)(2,1)} %fusion.73), calls=%async_computation.3 | async-start | bytes 1179648 | tf_op jit(solution)/shard_map/all_to_all | solution.py:86
  137.9 3.1 %fusion.39 = bf16[1,8,12,64,64]{4,3,2,1,0:T(8,128)(2,1)} fusion(bf16[8,64,12,64]{3,1,2,0:T(8,128)(2,1)} %copy-done.13, f32[8,12,64,64]{2,3,1,0:T(8,128)S(1)} %copy-done.1, f32[8,12,64]{2,1,0:T(8,128)S(1)} %copy-done.24), kind=kOutput, calls=%fused_computation.80 | convolution fusion | flops 51511296 | bytes 3170304 | tf_op jit(solution)/shard_map/transpose(jvp(bhlm,bhme->bhle))/dot_general | solution.py:22
  141.0 6.8 %all-to-all-done.3 = bf16[2,4,48,768]{3,2,1,0:T(8,128)(2,1)} async-done(((bf16[2,4,48,768]{3,2,1,0:T(8,128)(2,1)}), bf16[2,4,48,768]{3,2,1,0:T(8,128)(2,1)}, u32[]{:S(2)}, u32[]{:S(2)}) %all-to-all-start.3) | async-done | bytes 589856 | tf_op jit(solution)/shard_map/all_to_all | solution.py:86
  147.9 1.8 fusion.74
  149.7 4.6 %all-to-all-start.4 = ((bf16[4,48,768]{2,1,0:T(8,128)(2,1)}), bf16[4,48,768]{2,1,0:T(8,128)(2,1)S(1)}, u32[]{:S(2)}, u32[]{:S(2)}) async-start(bf16[4,48,768]{2,1,0:T(8,128)(2,1)} %fusion.74), calls=%async_computation.4 | async-start | bytes 589824 | tf_op jit(solution)/shard_map/all_to_all | solution.py:86
  154.3 6.8 %fusion.18 = bf16[768,3,12,64,1]{0,3,2,4,1:T(8,128)(2,1)} fusion(bf16[1,8,12,64,64]{4,3,2,1,0:T(8,128)(2,1)} %fusion.39, bf16[1,8,12,64,64]{4,3,2,1,0:T(8,128)(2,1)} %fusion.38, bf16[1,8,12,64,64]{4,3,2,1,0:T(8,128)(2,1)} %fusion.37, bf16[8,64,768]{2,1,0:T(8,128)(2,1)} %param.4, f32[8,64]{1,0:T(8,128)S(1)} %copy-done.28), kind=kOutput, calls=%fused_computation.40 | convolution fusion | flops 1820196864 | bytes 6686720 | tf_op jit(solution)/shard_map/bld,tbhle->dthe/dot_general | solution.py:76
  161.1 9.0 %all-to-all-done.4 = bf16[4,48,768]{2,1,0:T(8,128)(2,1)S(1)} async-done(((bf16[4,48,768]{2,1,0:T(8,128)(2,1)}), bf16[4,48,768]{2,1,0:T(8,128)(2,1)S(1)}, u32[]{:S(2)}, u32[]{:S(2)}) %all-to-all-start.4) | async-done | bytes 294944 | tf_op jit(solution)/shard_map/all_to_all | solution.py:86
  170.8 4.3 %copy.165 = bf16[768,2304]{1,0:T(8,128)(2,1)S(1)} copy(bf16[768,2304]{0,1:T(8,128)(2,1)} %bitcast.225) | data formatting | bytes 7077888 | tf_op jit(solution)/shard_map/optimization_barrier | solution.py:124
  175.4 6.6 %all_to_all.58 = bf16[2,4,2,48,2304]{4,3,2,1,0:T(8,128)(2,1)S(1)} all-to-all(bf16[2,4,2,48,2304]{4,3,2,1,0:T(8,128)(2,1)S(1)} %copy.166), channel_id=1, replica_groups={{0,1},{2,3},{4,5},{6,7},{8,9},{10,11},{12,13},{14,15},{16,17},{18,19},{..., dimensions={0} | all-to-all | bytes 7077888 | tf_op jit(solution)/shard_map/all_to_all | solution.py:86
  182.5 24.4 %all_to_all.59 = bf16[2,4,48,2304]{3,2,1,0:T(8,128)(2,1)S(1)} all-to-all(bf16[2,4,48,2304]{3,2,1,0:T(8,128)(2,1)S(1)} %copy.167), channel_id=1, replica_groups={{0,2},{1,3},{4,6},{5,7},{8,10},{9,11},{12,14},{13,15},{16,18},{17,19},{..., dimensions={0} | all-to-all | bytes 3538944 | tf_op jit(solution)/shard_map/all_to_all | solution.py:86
  208.1 4.3 %all-to-all-start.7 = ((bf16[4,48,2304]{2,1,0:T(8,128)(2,1)}), bf16[4,48,2304]{2,1,0:T(8,128)(2,1)}, u32[]{:S(2)}, u32[]{:S(2)}) async-start(bf16[4,48,2304]{2,1,0:T(8,128)(2,1)} %fusion.54), calls=%async_computation.7 | async-start | bytes 1769472 | tf_op jit(solution)/shard_map/all_to_all | solution.py:86
  212.5 5.9 %fusion.28 = (f32[8,64]{1,0:T(8,128)S(1)}, f32[8,64,768,1,1]{2,1,3,0,4:T(8,128)S(1)}) fusion(bf16[8,64,768]{2,1,0:T(8,128)(2,1)} %param.4, bf16[768,3,12,64,1]{0,3,2,4,1:T(8,128)(2,1)S(1)} %bitcast.222, bf16[1,8,12,64,64]{4,3,2,1,0:T(8,128)(2,1)} %fusion.39, bf16[1,8,12,64,64]{4,3,2,1,0:T(8,128)(2,1)} %fusion.38, bf16[1,8,12,64,64]{4,3,2,1,0:T(8,128)(2,1)} %fusion.37), kind=kOutput, calls=%fused_computation.58 | convolution fusion | flops 1815477760 | bytes 8259584 | tf_op jit(solution)/shard_map/tbhle,dthe->bld/dot_general | solution.py:65
  219.8 14.7 %all-to-all-done.7 = bf16[4,48,2304]{2,1,0:T(8,128)(2,1)} async-done(((bf16[4,48,2304]{2,1,0:T(8,128)(2,1)}), bf16[4,48,2304]{2,1,0:T(8,128)(2,1)}, u32[]{:S(2)}, u32[]{:S(2)}) %all-to-all-start.7) | async-done | bytes 884768 | tf_op jit(solution)/shard_map/all_to_all | solution.py:86
  236.7 1.8 convert_element_type.283
  (101 shorter events, 24.0 us)
Async XLA Ops:
  9.5 1.1 copy-start.6
  9.5 2.2 slice-start
  10.9 0.6 copy-start.25
  11.8 3.6 %copy-start.27 = (f32[8,64]{1,0:T(8,128)}, f32[8,64]{1,0:T(8,128)S(1)}, u32[]{:S(2)}) copy-start(f32[8,64]{1,0:T(8,128)S(1)} %fusion.75) | copy-start | bytes 6148
  21.2 5.6 %copy-start.2 = (bf16[3,8,12,64,64]{4,3,2,0,1:T(8,128)(2,1)}, bf16[3,8,12,64,64]{4,3,2,0,1:T(8,128)(2,1)S(1)}, u32[]{:S(2)}) copy-start(bf16[3,8,12,64,64]{4,3,2,0,1:T(8,128)(2,1)S(1)} %convert_bitcast_fusion) | copy-start | bytes 7077892
  26.8 1.6 copy-start
  26.8 1.7 copy-start.23
  26.9 1.7 copy-start.7
  26.9 2.9 %copy-start.15 = (bf16[768,768]{1,0:T(8,128)(2,1)S(1)}, bf16[768,768]{1,0:T(8,128)(2,1)}, u32[]{:S(2)}) copy-start(bf16[768,768]{1,0:T(8,128)(2,1)} %slice.92) | copy-start | bytes 3538948
  28.5 2.1 copy-start.11
  31.9 26.2 %all-to-all-start = ((bf16[8,64,768]{2,0,1:T(8,128)(2,1)}), bf16[8,64,768]{2,0,1:T(8,128)(2,1)}, u32[]{:S(2)}, u32[]{:S(2)}) async-start(bf16[8,64,768]{2,0,1:T(8,128)(2,1)} %copy.146), calls=%async_computation | async-start | bytes 1572864 | tf_op jit(solution)/shard_map/all_to_all | solution.py:113
  41.8 2.0 slice-start.1
  47.5 16.8 %copy-start.4 = (bf16[768,2304]{0,1:T(8,128)(2,1)S(1)}, bf16[768,2304]{0,1:T(8,128)(2,1)}, u32[]{:S(2)}) copy-start(bf16[768,2304]{0,1:T(8,128)(2,1)} %copy.151) | copy-start | bytes 10616836
  67.9 8.0 %copy-start.16 = (bf16[3,4,12,128,64]{3,4,2,0,1:T(8,128)(2,1)}, bf16[3,4,12,128,64]{3,4,2,0,1:T(8,128)(2,1)S(1)}, u32[]{:S(2)}) copy-start(bf16[3,4,12,128,64]{3,4,2,0,1:T(8,128)(2,1)S(1)} %convert_bitcast_fusion.1) | copy-start | bytes 7077892
  68.6 3.1 %copy-start.21 = (bf16[4,12,128,64]{2,3,0,1:T(8,128)(2,1)S(1)}, bf16[4,12,128,64]{2,3,0,1:T(8,128)(2,1)}, u32[]{:S(2)}) copy-start(bf16[4,12,128,64]{2,3,0,1:T(8,128)(2,1)} %fusion.49) | copy-start | bytes 2359300
  79.2 2.9 %copy-start.17 = (bf16[1,4,12,128,64]{3,4,2,1,0:T(8,128)(2,1)S(1)}, bf16[1,4,12,128,64]{3,4,2,1,0:T(8,128)(2,1)}, u32[]{:S(2)}) copy-start(bf16[1,4,12,128,64]{3,4,2,1,0:T(8,128)(2,1)} %fusion.51) | copy-start | bytes 2359300
  79.2 2.9 %copy-start.18 = (bf16[1,4,12,128,64]{3,4,2,1,0:T(8,128)(2,1)S(1)}, bf16[1,4,12,128,64]{3,4,2,1,0:T(8,128)(2,1)}, u32[]{:S(2)}) copy-start(bf16[1,4,12,128,64]{3,4,2,1,0:T(8,128)(2,1)} %fusion.50) | copy-start | bytes 2359300
  82.1 3.7 %copy-start.5 = (bf16[1,4,12,128,64]{3,4,2,1,0:T(8,128)(2,1)}, bf16[1,4,12,128,64]{3,4,2,1,0:T(8,128)(2,1)S(1)}, u32[]{:S(2)}) copy-start(bf16[1,4,12,128,64]{3,4,2,1,0:T(8,128)(2,1)S(1)} %fusion.48) | copy-start | bytes 2359300
  82.1 3.6 %copy-start.19 = (bf16[128,4,768]{2,1,0:T(4,128)(2,1)S(1)}, bf16[128,4,768]{2,1,0:T(4,128)(2,1)}, u32[]{:S(2)}) copy-start(bf16[128,4,768]{2,1,0:T(4,128)(2,1)} %param.5) | copy-start | bytes 2359300
  87.3 7.3 %copy-start.24 = (f32[8,12,64]{2,1,0:T(8,128)S(1)}, f32[8,12,64]{2,1,0:T(8,128)}, u32[]{:S(2)}) copy-start(f32[8,12,64]{2,1,0:T(8,128)} %copy-done.23) | copy-start | bytes 73732
  88.8 24.9 %all-to-all-start.1 = ((bf16[128,4,768]{2,1,0:T(4,128)(2,1)}), bf16[128,4,768]{2,1,0:T(4,128)(2,1)S(1)}, u32[]{:S(2)}, u32[]{:S(2)}) async-start(bf16[128,4,768]{2,1,0:T(4,128)(2,1)} %copy.159), calls=%async_computation.1 | async-start | bytes 1572864 | tf_op jit(solution)/shard_map/all_to_all | solution.py:120
  94.3 142.4 %reduce-scatter.2.cloned.1.call-start = ((), (), s32[]{:S(2)}) async-start(), calls=%async_computation.9 | async-start | bytes 5013504 | tf_op jit(solution)/shard_map/reduce_scatter | solution.py:117
  101.0 2.0 copy-start.12
  106.6 4.2 %copy-start.14 = (bf16[12,64,768]{2,1,0:T(8,128)(2,1)S(1)}, bf16[12,64,768]{2,1,0:T(8,128)(2,1)}, u32[]{:S(2)}) copy-start(bf16[12,64,768]{2,1,0:T(8,128)(2,1)} %bitcast_convert_fusion.1) | copy-start | bytes 3538948
  116.2 3.1 %copy-start.1 = (f32[8,12,64,64]{2,3,1,0:T(8,128)S(1)}, f32[8,12,64,64]{2,3,1,0:T(8,128)}, u32[]{:S(2)}) copy-start(f32[8,12,64,64]{2,3,1,0:T(8,128)} %copy-done) | copy-start | bytes 4718596
  116.2 6.2 %slice-start.2 = ((s8[4718592]{0:T(1024)(128)(4,1)}), s8[4194304]{0:T(1024)(128)(4,1)S(1)}, s32[]{:S(2)}) async-start(s8[4718592]{0:T(1024)(128)(4,1)} %bitcast.219), calls=%async_computation.12 | async-start | bytes 8388608
  119.3 3.1 %copy-start.13 = (bf16[8,64,12,64]{3,1,2,0:T(8,128)(2,1)}, bf16[8,64,12,64]{3,1,2,0:T(8,128)(2,1)S(1)}, u32[]{:S(2)}) copy-start(bf16[8,64,12,64]{3,1,2,0:T(8,128)(2,1)S(1)} %convolution_convert_fusion) | copy-start | bytes 2359300
  119.3 3.1 %slice-start.3 = ((s8[4718592]{0:T(1024)(128)(4,1)}), s8[524288]{0:T(1024)(128)(4,1)S(1)}, s32[]{:S(2)}) async-start(s8[4718592]{0:T(1024)(128)(4,1)} %bitcast.219), calls=%async_computation.13 | async-start | bytes 1048576
  124.4 2.2 copy-start.9
  124.4 2.2 copy-start.20
  133.3 14.5 %all-to-all-start.3 = ((bf16[2,4,48,768]{3,2,1,0:T(8,128)(2,1)}), bf16[2,4,48,768]{3,2,1,0:T(8,128)(2,1)}, u32[]{:S(2)}, u32[]{:S(2)}) async-start(bf16[2,4,48,768]{3,2,1,0:T(8,128)(2,1)} %fusion.73), calls=%async_computation.3 | async-start | bytes 1179648 | tf_op jit(solution)/shard_map/all_to_all | solution.py:86
  137.9 16.4 %copy-start.28 = (f32[8,64]{1,0:T(8,128)S(1)}, f32[8,64]{1,0:T(8,128)}, u32[]{:S(2)}) copy-start(f32[8,64]{1,0:T(8,128)} %copy-done.27) | copy-start | bytes 6148
  149.7 20.4 %all-to-all-start.4 = ((bf16[4,48,768]{2,1,0:T(8,128)(2,1)}), bf16[4,48,768]{2,1,0:T(8,128)(2,1)S(1)}, u32[]{:S(2)}, u32[]{:S(2)}) async-start(bf16[4,48,768]{2,1,0:T(8,128)(2,1)} %fusion.74), calls=%async_computation.4 | async-start | bytes 589824 | tf_op jit(solution)/shard_map/all_to_all | solution.py:86
  206.9 5.5 %copy-start.3 = (bf16[768,2304]{0,1:T(8,128)(2,1)S(1)}, bf16[768,2304]{0,1:T(8,128)(2,1)}, u32[]{:S(2)}) copy-start(bf16[768,2304]{0,1:T(8,128)(2,1)} %copy.144) | copy-start | bytes 10616836
  208.1 26.4 %all-to-all-start.7 = ((bf16[4,48,2304]{2,1,0:T(8,128)(2,1)}), bf16[4,48,2304]{2,1,0:T(8,128)(2,1)}, u32[]{:S(2)}, u32[]{:S(2)}) async-start(bf16[4,48,2304]{2,1,0:T(8,128)(2,1)} %fusion.54), calls=%async_computation.7 | async-start | bytes 1769472 | tf_op jit(solution)/shard_map/all_to_all | solution.py:86
  212.4 6.0 %copy-start.26 = (f32[8,64]{1,0:T(8,128)S(1)}, f32[8,64]{1,0:T(8,128)}, u32[]{:S(2)}) copy-start(f32[8,64]{1,0:T(8,128)} %copy-done.25) | copy-start | bytes 6148
  212.4 6.0 %copy-start.8 = (bf16[8,64,768]{2,1,0:T(8,128)(2,1)S(1)}, bf16[8,64,768]{2,1,0:T(8,128)(2,1)}, u32[]{:S(2)}) copy-start(bf16[8,64,768]{2,1,0:T(8,128)(2,1)} %param.4) | copy-start | bytes 2359300
  212.4 6.0 %copy-start.10 = (bf16[8,64,768]{2,1,0:T(8,128)(2,1)S(1)}, bf16[8,64,768]{2,1,0:T(8,128)(2,1)}, u32[]{:S(2)}) copy-start(bf16[8,64,768]{2,1,0:T(8,128)(2,1)} %all_to_all.42) | copy-start | bytes 2359300
  218.4 17.4 %copy-start.22 = (f32[48,768]{1,0:T(8,128)S(1)}, f32[48,768]{1,0:T(8,128)}, u32[]{:S(2)}) copy-start(f32[48,768]{1,0:T(8,128)} %add_bitcast_fusion.1) | copy-start | bytes 442372
Sparse Core Ops, SparseCore 0:
  113.9 79.8 reduce-scatter.1
